TPU v7x, 32 devices: a whole 2x2x4 slice. The times are simulated.
32 devices in a mesh: groups: 2 (over x), dp: 16 (over z, y, core).
Axes of the slice: x: 2, y: 2, z: 4, core: 2. Of those that a mesh axis runs over, the one named last changes fastest.
Arguments:
- frames: bfloat16 [128, 256, 1536], P(('groups', 'dp')), parts along dimension 0, may hold values from -6 to 6
- cotangent: bfloat16 [128, 256, 1536], P(('groups', 'dp')), parts along dimension 0, may hold values from -6 to 6
- gain: float32 [1536], replicated, may hold values from 0.25 to 1.75
- down_weight: bfloat16 [320, 1536, 256], P('groups', 'dp'), parts along dimension 0, may hold values from -0.15625 to 0.15625
- up_weight: bfloat16 [320, 1536, 256], P('groups', 'dp'), parts along dimension 0, may hold values from -0.375 to 0.375
- slot_lang: int32 [32, 2], P('groups'), parts along dimension 0, may hold values from 0 to 159
- utt_slot: int32 [128], P('groups'), parts along dimension 0, may hold values from 0 to 1
- lengths: int32 [128], P('groups'), parts along dimension 0, may hold values from 64 to 256
Outputs:
- frame_grads: bfloat16 [128, 256, 1536], P(('groups', 'dp')), parts along dimension 0
- down_grads: bfloat16 [320, 1536, 256], P('groups', 'dp'), parts along dimension 0
- up_grads: bfloat16 [320, 1536, 256], P('groups', 'dp'), parts along dimension 0
There are 2 independent parts, one for each index of `groups`. A program takes and returns all parts, laid end to end along the dimension named above; an argument that names none is the same for every part. Nothing has to cross between parts.
All inputs are finite; a program needn't handle non-finite values.
Results may differ from a plain program's by a relative error of at most 0.0061.
Values may be sent and summed in bfloat16 or wider, within the bound.
No kernel may reach another device: no remote copies, remote signals or barrier semaphores. Data moves between devices by JAX's collectives and lax.ppermute only.
A program may use at most 128 MiB of HBM per device.

v0:
```python
import jax
import jax.numpy as jnp
from jax import lax
from jax.sharding import PartitionSpec as P


def local_pass(frames, cotangent, gain, w_down, w_up, live_mask):
    values = frames.astype(jnp.float32)
    centre_mean = jnp.mean(values, axis=2, keepdims=True)
    mean_removed = values - centre_mean
    variance = jnp.mean(mean_removed * mean_removed, axis=2, keepdims=True)
    reciprocal_deviation = lax.rsqrt(variance + 1e-06)
    standardized_input = mean_removed * reciprocal_deviation
    layer_normed = (standardized_input * gain).astype(jnp.bfloat16)
    pre_act = jnp.einsum("ufd,udr->ufr", layer_normed, w_down, preferred_element_type=jnp.float32)
    sigmoid_pre = jax.nn.sigmoid(pre_act)
    hidden = (pre_act * sigmoid_pre).astype(jnp.bfloat16)
    masked_up = jnp.where(live_mask, cotangent, jnp.zeros_like(cotangent))
    grad_up = jnp.einsum("ufd,ufr->udr", masked_up, hidden, preferred_element_type=jnp.float32)
    d_hidden = jnp.einsum("ufd,udr->ufr", masked_up, w_up, preferred_element_type=jnp.float32)
    d_pre = (d_hidden * sigmoid_pre * (1.0 + pre_act * (1.0 - sigmoid_pre))).astype(jnp.bfloat16)
    grad_down = jnp.einsum("ufd,ufr->udr", layer_normed, d_pre, preferred_element_type=jnp.float32)
    d_normed = jnp.einsum("ufr,udr->ufd", d_pre, w_down, preferred_element_type=jnp.float32)
    scaled_rows = d_normed * gain
    inner_gradient = (
        scaled_rows
        - jnp.mean(scaled_rows, axis=2, keepdims=True)
        - standardized_input * jnp.mean(scaled_rows * standardized_input, axis=2, keepdims=True)
    ) * reciprocal_deviation
    d_frames = (cotangent.astype(jnp.float32) + inner_gradient).astype(jnp.bfloat16)
    return (d_frames, grad_down, grad_up)


def on_device(frames, cotangent, gain, down_weight, up_weight, slot_lang, utt_slot, lengths):
    devices = lax.axis_size("dp")
    self_index = lax.axis_index("dp")
    per_device = frames.shape[0]
    lang_count, row_count, bottleneck = down_weight.shape
    owners = jnp.arange(utt_slot.shape[0], dtype=jnp.int32) // per_device
    utt_lang = slot_lang[owners, utt_slot]
    own_lengths = lax.dynamic_slice_in_dim(lengths, self_index * per_device, per_device)
    live_mask = (jnp.arange(frames.shape[1], dtype=jnp.int32)[None, :] < own_lengths[:, None])[
        :, :, None
    ]
    send_down = jnp.take(down_weight, utt_lang, axis=0).reshape(
        devices, per_device, row_count, bottleneck
    )
    send_up = jnp.take(up_weight, utt_lang, axis=0).reshape(
        devices, per_device, row_count, bottleneck
    )
    got_down, got_up = (
        lax.all_to_all(send_down, "dp", split_axis=0, concat_axis=2, tiled=True),
        lax.all_to_all(send_up, "dp", split_axis=0, concat_axis=2, tiled=True),
    )
    d_frames, grad_down, grad_up = local_pass(
        frames, cotangent, gain, got_down[0], got_up[0], live_mask
    )
    back_down, back_up = (
        lax.all_to_all(grad_down[None], "dp", split_axis=2, concat_axis=0, tiled=True),
        lax.all_to_all(grad_up[None], "dp", split_axis=2, concat_axis=0, tiled=True),
    )
    members = utt_lang.shape[0]
    lang_ids = jnp.arange(lang_count, dtype=jnp.int32)
    lang_table = (lang_ids[:, None] == utt_lang[None, :]).astype(jnp.float32)
    sum_down = jnp.dot(
        lang_table,
        back_down.reshape(members, row_count * bottleneck),
        precision=lax.Precision.HIGHEST,
    )
    sum_up = jnp.dot(
        lang_table,
        back_up.reshape(members, row_count * bottleneck),
        precision=lax.Precision.HIGHEST,
    )
    counts = jnp.sum(jnp.where(utt_lang[None, :] == lang_ids[:, None], lengths[None, :], 0), axis=1)
    scaling = lax.rsqrt(jnp.maximum(counts, 1).astype(jnp.float32))[:, None]
    down_grads = (
        (sum_down * scaling).reshape(lang_count, row_count, bottleneck).astype(jnp.bfloat16)
    )
    up_grads = (sum_up * scaling).reshape(lang_count, row_count, bottleneck).astype(jnp.bfloat16)
    return (d_frames, down_grads, up_grads)


def solution(mesh):
    placed = (
        P(("groups", "dp"), None, None),
        P(("groups", "dp"), None, None),
        P(),
        P("groups", "dp", None),
        P("groups", "dp", None),
        P("groups", None),
        P("groups"),
        P("groups"),
    )
    return jax.shard_map(
        on_device,
        mesh=mesh,
        in_specs=placed,
        out_specs=(
            P(("groups", "dp"), None, None),
            P("groups", "dp", None),
            P("groups", "dp", None),
        ),
        check_vma=False,
    )
```

profile of v0, /device:TPU:15, one launch (start us, length us, event | category | flops | bytes accessed | tf_op | source)
XLA Modules:
  0.0 478.6 jit_solution(11438838528285541702)
XLA Ops:
  2.2 4.0 gather_fusion.2
  6.2 5.6 %gather_fusion.1 = bf16[64,96,256]{2,1,0:T(8,128)(2,1)} fusion(bf16[160,96,256]{2,1,0:T(8,128)(2,1)} %param.14, s32[1024]{0:T(1024)S(1)} %pad_clamp_fusion), kind=kCustom, calls=%fused_computation.clone | custom fusion | bytes 6291712 | tf_op jit(solution)/shard_map/jit(_take)/gather | solution.py:48
  11.9 4.2 broadcast_select_fusion
  16.1 76.5 %all_to_all.60 = bf16[16,4,96,256]{3,2,1,0:T(8,128)(2,1)} all-to-all(bf16[16,4,96,256]{3,2,1,0:T(8,128)(2,1)S(1)} %bitcast.51), channel_id=1, replica_groups=mesh['groups'=2,'dp'=16] {'dp'}, dimensions={0} | all-to-all | bytes 6291456 | tf_op jit(solution)/shard_map/all_to_all | solution.py:52
  92.5 5.2 %all-to-all-start = ((bf16[16,4,96,256]{3,2,1,0:T(8,128)(2,1)}), bf16[16,4,96,256]{3,2,1,0:T(8,128)(2,1)}, u32[]{:S(2)}, u32[]{:S(2)}) async-start(bf16[16,4,96,256]{3,2,1,0:T(8,128)(2,1)} %bitcast.50), calls=%async_computation | async-start | bytes 6291456 | tf_op jit(solution)/shard_map/all_to_all | solution.py:53
  103.5 1.8 convolution_bitcast_fusion
  105.3 11.8 %copy.35 = f32[1,4,1536,256]{3,1,0,2:T(4,128)} copy(f32[1,4,1536,256]{3,2,1,0:T(8,128)S(1)} %convolution_bitcast_fusion) | data formatting | bytes 12582912 | tf_op jit(solution)/shard_map/broadcast_in_dim | solution.py:60
  117.1 50.6 %all-to-all-done = bf16[16,4,96,256]{3,2,1,0:T(8,128)(2,1)} async-done(((bf16[16,4,96,256]{3,2,1,0:T(8,128)(2,1)}), bf16[16,4,96,256]{3,2,1,0:T(8,128)(2,1)}, u32[]{:S(2)}, u32[]{:S(2)}) %all-to-all-start) | async-done | bytes 3145760 | tf_op jit(solution)/shard_map/all_to_all | solution.py:53
  167.7 5.2 %all-to-all-start.3 = ((f32[1,4,1536,256]{3,1,0,2:T(4,128)}), f32[1,4,1536,256]{3,1,0,2:T(4,128)}, u32[]{:S(2)}, u32[]{:S(2)}) async-start(f32[1,4,1536,256]{3,1,0,2:T(4,128)} %copy.35), calls=%async_computation.3 | async-start | bytes 12582912 | tf_op jit(solution)/shard_map/all_to_all | solution.py:60
  173.0 2.3 copy.29
  179.9 11.8 %copy.32 = f32[1,4,1536,256]{3,1,0,2:T(4,128)} copy(f32[1,4,1536,256]{3,2,1,0:T(8,128)S(1)} %convolution_bitcast_fusion.1) | data formatting | bytes 12582912 | tf_op jit(solution)/shard_map/broadcast_in_dim | solution.py:59
  191.7 118.5 %all-to-all-done.3 = f32[1,4,1536,256]{3,1,0,2:T(4,128)} async-done(((f32[1,4,1536,256]{3,1,0,2:T(4,128)}), f32[1,4,1536,256]{3,1,0,2:T(4,128)}, u32[]{:S(2)}, u32[]{:S(2)}) %all-to-all-start.3) | async-done | bytes 6291488 | tf_op jit(solution)/shard_map/all_to_all | solution.py:60
  310.2 5.2 %all-to-all-start.2 = ((f32[1,4,1536,256]{3,1,0,2:T(4,128)}), f32[1,4,1536,256]{3,1,0,2:T(4,128)}, u32[]{:S(2)}, u32[]{:S(2)}) async-start(f32[1,4,1536,256]{3,1,0,2:T(4,128)} %copy.32), calls=%async_computation.2 | async-start | bytes 12582912 | tf_op jit(solution)/shard_map/all_to_all | solution.py:59
  315.6 4.3 multiply_reduce_fusion
  319.9 3.9 fusion.12
  323.8 3.9 copy.36
  327.7 3.6 copy.41
  331.3 9.4 %fusion.1 = bf16[160,24576]{1,0:T(8,128)(2,1)} fusion(f32[64,24576]{1,0:T(8,128)S(1)} %bitcast.47, f32[160]{0:T(256)S(1)} %convert_rsqrt_fusion, s32[64]{0:T(128)S(1)} %gather_fusion), kind=kOutput, calls=%fused_computation.6 | convolution fusion | flops 3027773440 | bytes 14156672 | tf_op jit(solution)/shard_map/dot_general | solution.py:70
  340.6 8.9 %copy.42 = bf16[20,8,96,256]{3,2,1,0:T(8,128)(2,1)} copy(bf16[20,8,96,256]{3,1,2,0:T(8,128)(2,1)} %bitcast.44) | data formatting | bytes 15728640
  349.5 103.2 %all-to-all-done.2 = f32[1,4,1536,256]{3,1,0,2:T(4,128)} async-done(((f32[1,4,1536,256]{3,1,0,2:T(4,128)}), f32[1,4,1536,256]{3,1,0,2:T(4,128)}, u32[]{:S(2)}, u32[]{:S(2)}) %all-to-all-start.2) | async-done | bytes 6291488 | tf_op jit(solution)/shard_map/all_to_all | solution.py:59
  452.8 3.9 copy.33
  456.6 3.6 copy.39
  460.2 9.1 %fusion = bf16[160,24576]{1,0:T(8,128)(2,1)} fusion(f32[64,24576]{1,0:T(8,128)S(1)} %bitcast.45, f32[160]{0:T(256)S(1)} %convert_rsqrt_fusion, s32[64]{0:T(128)S(1)} %gather_fusion), kind=kOutput, calls=%fused_computation.5 | convolution fusion | flops 3027773440 | bytes 14156672 | tf_op jit(solution)/shard_map/dot_general | solution.py:65
  469.3 8.9 %copy.40 = bf16[20,8,96,256]{3,2,1,0:T(8,128)(2,1)} copy(bf16[20,8,96,256]{3,1,2,0:T(8,128)(2,1)} %bitcast.43) | data formatting | bytes 15728640
  (44 shorter events, 12.0 us)
Async XLA Ops:
  0.6 0.7 copy-start
  16.1 81.7 %copy-start.10 = (s32[64]{0:T(128)S(1)}, s32[64]{0:T(128)}, u32[]{:S(2)}) copy-start(s32[64]{0:T(128)} %param.17) | copy-start | bytes 772
  16.1 81.9 %copy-start.2 = (bf16[4,256,1536]{2,1,0:T(8,128)(2,1)S(1)}, bf16[4,256,1536]{2,1,0:T(8,128)(2,1)}, u32[]{:S(2)}) copy-start(bf16[4,256,1536]{2,1,0:T(8,128)(2,1)} %param.10) | copy-start | bytes 9437188
  92.5 75.2 %all-to-all-start = ((bf16[16,4,96,256]{3,2,1,0:T(8,128)(2,1)}), bf16[16,4,96,256]{3,2,1,0:T(8,128)(2,1)}, u32[]{:S(2)}, u32[]{:S(2)}) async-start(bf16[16,4,96,256]{3,2,1,0:T(8,128)(2,1)} %bitcast.50), calls=%async_computation | async-start | bytes 6291456 | tf_op jit(solution)/shard_map/all_to_all | solution.py:53
  97.8 1.9 copy-start.3
  97.9 3.7 copy-start.9
  99.9 1.7 copy-start.4
  101.6 1.9 copy-start.5
  103.5 1.8 copy-start.11
  167.7 142.5 %all-to-all-start.3 = ((f32[1,4,1536,256]{3,1,0,2:T(4,128)}), f32[1,4,1536,256]{3,1,0,2:T(4,128)}, u32[]{:S(2)}, u32[]{:S(2)}) async-start(f32[1,4,1536,256]{3,1,0,2:T(4,128)} %copy.35), calls=%async_computation.3 | async-start | bytes 12582912 | tf_op jit(solution)/shard_map/all_to_all | solution.py:60
  173.0 2.8 copy-start.6
  173.0 3.1 copy-start.12
  177.3 0.8 copy-start.8
  310.2 142.5 %all-to-all-start.2 = ((f32[1,4,1536,256]{3,1,0,2:T(4,128)}), f32[1,4,1536,256]{3,1,0,2:T(4,128)}, u32[]{:S(2)}, u32[]{:S(2)}) async-start(f32[1,4,1536,256]{3,1,0,2:T(4,128)} %copy.32), calls=%async_computation.2 | async-start | bytes 12582912 | tf_op jit(solution)/shard_map/all_to_all | solution.py:59
  315.6 4.3 copy-start.7
  469.3 8.9 %copy-start.1 = (s32[16,2]{0,1:T(2,128)S(1)}, s32[16,2]{0,1:T(2,128)}, u32[]{:S(2)}) copy-start(s32[16,2]{0,1:T(2,128)} %param.15) | copy-start | bytes 388
where the time goes:
time: 486 us; the launch traced here: 479 us
  waiting for transfers between devices  272 us (56%)
  blocking collectives  76.5 us (16%)
  local copies, waits for them, and re-layouts  73.7 us (15%)
  matrix products  28.7 us (6%)
  starting transfers between devices  15.7 us (3%)
  other arithmetic  10.4 us (2%)
    all_to_all x1, waiting for transfers between devices, on_device(): lax.all_to_all(grad_up[None], 'dp', split_axis=2, concat_axis=0, tiled=True)  119 us
    all_to_all x1, waiting for transfers between devices, on_device(): lax.all_to_all(grad_down[None], 'dp', split_axis=2, concat_axis=0, tiled=...  103 us
    all_to_all x1, blocking collectives, on_device(): lax.all_to_all(send_down, 'dp', split_axis=0, concat_axis=2, tiled=True)  76.5 us
    all_to_all x1, waiting for transfers between devices, on_device(): lax.all_to_all(send_up, 'dp', split_axis=0, concat_axis=2, tiled=True)  50.6 us
    unnamed x30, local copies, waits for them, and re-layouts  29.1 us
    broadcast_in_dim x1, local copies, waits for them, and re-layouts, on_device(): grad_down[None]  11.8 us
    broadcast_in_dim x1, local copies, waits for them, and re-layouts, on_device(): grad_up[None]  11.8 us
  transfers between devices with their start and end apart: 3, of which 3 were waited for; matrix products, arithmetic and copies ran while one was open for 14% of the time, Pallas kernels for 0%

commit v1 on v0

--- a/solution.py
+++ b/solution.py
@@ -4,7 +4,7 @@
 from jax.sharding import PartitionSpec as P
 
 
-def local_pass(frames, cotangent, gain, w_down, w_up, live_mask):
+def local_pass(frames, cotangent, gain, w_down, w_up, live_mask, slot_select):
     values = frames.astype(jnp.float32)
     centre_mean = jnp.mean(values, axis=2, keepdims=True)
     mean_removed = values - centre_mean
@@ -16,10 +16,12 @@
     sigmoid_pre = jax.nn.sigmoid(pre_act)
     hidden = (pre_act * sigmoid_pre).astype(jnp.bfloat16)
     masked_up = jnp.where(live_mask, cotangent, jnp.zeros_like(cotangent))
-    grad_up = jnp.einsum("ufd,ufr->udr", masked_up, hidden, preferred_element_type=jnp.float32)
+    hidden_slots = hidden[None] * slot_select[:, :, None, None]
+    grad_up = jnp.einsum("ufd,sufr->sdr", masked_up, hidden_slots, preferred_element_type=jnp.float32)
     d_hidden = jnp.einsum("ufd,udr->ufr", masked_up, w_up, preferred_element_type=jnp.float32)
     d_pre = (d_hidden * sigmoid_pre * (1.0 + pre_act * (1.0 - sigmoid_pre))).astype(jnp.bfloat16)
-    grad_down = jnp.einsum("ufd,ufr->udr", layer_normed, d_pre, preferred_element_type=jnp.float32)
+    d_pre_slots = d_pre[None] * slot_select[:, :, None, None]
+    grad_down = jnp.einsum("ufd,sufr->sdr", layer_normed, d_pre_slots, preferred_element_type=jnp.float32)
     d_normed = jnp.einsum("ufr,udr->ufd", d_pre, w_down, preferred_element_type=jnp.float32)
     scaled_rows = d_normed * gain
     inner_gradient = (
@@ -35,33 +37,37 @@
     devices = lax.axis_size("dp")
     self_index = lax.axis_index("dp")
     per_device = frames.shape[0]
+    slots = slot_lang.shape[1]
     lang_count, row_count, bottleneck = down_weight.shape
     owners = jnp.arange(utt_slot.shape[0], dtype=jnp.int32) // per_device
     utt_lang = slot_lang[owners, utt_slot]
     own_lengths = lax.dynamic_slice_in_dim(lengths, self_index * per_device, per_device)
+    own_slot = lax.dynamic_slice_in_dim(utt_slot, self_index * per_device, per_device)
     live_mask = (jnp.arange(frames.shape[1], dtype=jnp.int32)[None, :] < own_lengths[:, None])[
         :, :, None
     ]
-    send_down = jnp.take(down_weight, utt_lang, axis=0).reshape(
-        devices, per_device, row_count, bottleneck
+    list_langs = slot_lang.reshape(-1)
+    send_down = jnp.take(down_weight, list_langs, axis=0).reshape(
+        devices, slots, row_count, bottleneck
     )
-    send_up = jnp.take(up_weight, utt_lang, axis=0).reshape(
-        devices, per_device, row_count, bottleneck
+    send_up = jnp.take(up_weight, list_langs, axis=0).reshape(
+        devices, slots, row_count, bottleneck
     )
-    got_down, got_up = (
-        lax.all_to_all(send_down, "dp", split_axis=0, concat_axis=2, tiled=True),
-        lax.all_to_all(send_up, "dp", split_axis=0, concat_axis=2, tiled=True),
+    got_down = lax.all_to_all(send_down, "dp", split_axis=0, concat_axis=2, tiled=True)[0]
+    got_up = lax.all_to_all(send_up, "dp", split_axis=0, concat_axis=2, tiled=True)[0]
+    w_down = jnp.take(got_down, own_slot, axis=0)
+    w_up = jnp.take(got_up, own_slot, axis=0)
+    slot_select = (jnp.arange(slots, dtype=jnp.int32)[:, None] == own_slot[None, :]).astype(
+        jnp.bfloat16
     )
     d_frames, grad_down, grad_up = local_pass(
-        frames, cotangent, gain, got_down[0], got_up[0], live_mask
+        frames, cotangent, gain, w_down, w_up, live_mask, slot_select
     )
-    back_down, back_up = (
-        lax.all_to_all(grad_down[None], "dp", split_axis=2, concat_axis=0, tiled=True),
-        lax.all_to_all(grad_up[None], "dp", split_axis=2, concat_axis=0, tiled=True),
-    )
-    members = utt_lang.shape[0]
+    back_down = lax.all_to_all(grad_down[None], "dp", split_axis=2, concat_axis=0, tiled=True)
+    back_up = lax.all_to_all(grad_up[None], "dp", split_axis=2, concat_axis=0, tiled=True)
+    members = devices * slots
     lang_ids = jnp.arange(lang_count, dtype=jnp.int32)
-    lang_table = (lang_ids[:, None] == utt_lang[None, :]).astype(jnp.float32)
+    lang_table = (lang_ids[:, None] == list_langs[None, :]).astype(jnp.float32)
     sum_down = jnp.dot(
         lang_table,
         back_down.reshape(members, row_count * bottleneck),

time: 486 us -> 278 us (0.57); the launches traced: 479 us -> 277 us
  waiting for transfers between devices: 272 us -> 147 us
  blocking collectives: 76.5 us -> 0 us
  local copies, waits for them, and re-layouts: 73.7 us -> 59.5 us
  matrix products: 28.7 us -> 40.5 us
  starting transfers between devices: 15.7 us -> 21.5 us
    all_to_all x1 -> x0, blocking collectives: 76.5 us -> none  [on_device(): lax.all_to_all(send_down, 'dp', split_axis=0, concat_axis=2, tiled=True)]
    all_to_all x1, waiting for transfers between devices: 119 us -> 45.9 us  [on_device(): lax.all_to_all(grad_up[None], 'dp', split_axis=2, concat_axis=0, tiled=True)]
    all_to_all x1, waiting for transfers between devices: 103 us -> 54.5 us  [on_device(): lax.all_to_all(grad_down[None], 'dp', split_axis=2, concat_axis=0, tiled=...]
    unnamed x30 -> x17, local copies, waits for them, and re-layouts: 29.1 us -> 17.2 us
    dot_general x2, matrix products: 3.6 us -> 10.3 us  [the longest x1 5.6 us: local_pass(): jnp.einsum('ufd,sufr->sdr', masked_up, hidden_slots, preferred_element_ty...]
    all_to_all x1 -> x2, starting transfers between devices: 5.2 us -> 11.7 us  [the longest x1 6.82 us: on_device(): lax.all_to_all(send_down, 'dp', split_axis=0, concat_axis=2, tiled=True)[0]]
    broadcast_in_dim x1, local copies, waits for them, and re-layouts: 11.8 us -> 5.73 us  [on_device(): grad_down[None]]
    broadcast_in_dim x1, local copies, waits for them, and re-layouts: 11.8 us -> 5.76 us  [on_device(): grad_up[None]]
  transfers between devices with their start and end apart: 3 -> 4, of which waited for: 3 -> 4; matrix products, arithmetic and copies ran while one was open for 14% -> 24% of each run, Pallas kernels for 0% -> 0%
where the time goes in v1:
time: 278 us; the launch traced here: 277 us
  waiting for transfers between devices  147 us (53%)
  local copies, waits for them, and re-layouts  59.5 us (21%)
  matrix products  40.5 us (15%)
  starting transfers between devices  21.5 us (8%)
  other arithmetic  7.74 us (3%)
    all_to_all x1, waiting for transfers between devices, on_device(): lax.all_to_all(grad_down[None], 'dp', split_axis=2, concat_axis=0, tiled=...  54.5 us
    all_to_all x1, waiting for transfers between devices, on_device(): lax.all_to_all(grad_up[None], 'dp', split_axis=2, concat_axis=0, tiled=True)  45.9 us
    all_to_all x1, waiting for transfers between devices, on_device(): lax.all_to_all(send_down, 'dp', split_axis=0, concat_axis=2, tiled=True)[0]  36.2 us
    unnamed x17, local copies, waits for them, and re-layouts  17.2 us
    all_to_all x1, waiting for transfers between devices, on_device(): lax.all_to_all(send_up, 'dp', split_axis=0, concat_axis=2, tiled=True)[0]  10.2 us
    dot_general x1, matrix products, on_device(): jnp.dot(lang_table, back_up.reshape(members, row_count * bottleneck), pre...  8.82 us
    dot_general x1, matrix products, on_device(): jnp.dot(lang_table, back_down.reshape(members, row_count * bottleneck), p...  7.16 us
    all_to_all x1, starting transfers between devices, on_device(): lax.all_to_all(send_down, 'dp', split_axis=0, concat_axis=2, tiled=True)[0]  6.82 us
  transfers between devices with their start and end apart: 4, of which 4 were waited for; matrix products, arithmetic and copies ran while one was open for 24% of the time, Pallas kernels for 0%

profile of v1, /device:TPU:15, one launch (start us, length us, event | category | flops | bytes accessed | tf_op | source)
XLA Modules:
  0.0 276.9 jit_solution(3445962492048153863)
XLA Ops:
  1.5 3.9 %gather_fusion.3 = bf16[32,96,256]{2,1,0:T(8,128)(2,1)S(1)} fusion(bf16[160,96,256]{2,1,0:T(8,128)(2,1)} %param.15, s32[1024]{0:T(1024)S(1)} %pad_clamp_fusion.1), kind=kCustom, calls=%fused_computation.2.clone | custom fusion | bytes 3145856 | tf_op jit(solution)/shard_map/jit(_take)/gather | solution.py:50
  5.4 3.9 %gather_fusion.1 = bf16[32,96,256]{2,1,0:T(8,128)(2,1)S(1)} fusion(bf16[160,96,256]{2,1,0:T(8,128)(2,1)} %param.16, s32[1024]{0:T(1024)S(1)} %pad_clamp_fusion.1), kind=kCustom, calls=%fused_computation.clone | custom fusion | bytes 3145856 | tf_op jit(solution)/shard_map/jit(_take)/gather | solution.py:53
  11.3 6.8 %all-to-all-start.1 = ((bf16[16,2,96,256]{3,2,1,0:T(8,128)(2,1)}), bf16[16,2,96,256]{3,2,1,0:T(8,128)(2,1)}, u32[]{:S(2)}, u32[]{:S(2)}) async-start(bf16[16,2,96,256]{3,2,1,0:T(8,128)(2,1)} %bitcast.70), calls=%async_computation.1 | async-start | bytes 3145728 | tf_op jit(solution)/shard_map/all_to_all | solution.py:56
  18.2 36.2 %all-to-all-done.1 = bf16[16,2,96,256]{3,2,1,0:T(8,128)(2,1)} async-done(((bf16[16,2,96,256]{3,2,1,0:T(8,128)(2,1)}), bf16[16,2,96,256]{3,2,1,0:T(8,128)(2,1)}, u32[]{:S(2)}, u32[]{:S(2)}) %all-to-all-start.1) | async-done | bytes 1572896 | tf_op jit(solution)/shard_map/all_to_all | solution.py:56
  54.4 4.9 %all-to-all-start = ((bf16[16,2,96,256]{3,2,1,0:T(8,128)(2,1)}), bf16[16,2,96,256]{3,2,1,0:T(8,128)(2,1)}, u32[]{:S(2)}, u32[]{:S(2)}) async-start(bf16[16,2,96,256]{3,2,1,0:T(8,128)(2,1)} %bitcast.69), calls=%async_computation | async-start | bytes 3145728 | tf_op jit(solution)/shard_map/all_to_all | solution.py:57
  63.7 3.8 %gather_fusion.4 = bf16[4,1536,256]{2,1,0:T(8,128)(2,1)} fusion(bf16[2,1536,256]{2,1,0:T(8,128)(2,1)} %bitcast.60, s32[1024]{0:T(1024)S(1)} %pad_clamp_fusion), kind=kCustom, calls=%fused_computation.3.clone | custom fusion | bytes 6291472 | tf_op jit(solution)/shard_map/jit(_take)/gather | solution.py:58
  67.5 4.5 %multiply_convert_fusion = (bf16[4,256,256]{2,1,0:T(8,128)(2,1)}, f32[4,256,256]{2,1,0:T(8,128)}) fusion(bf16[4,1536,256]{2,1,0:T(8,128)(2,1)} %gather_fusion.4, pred[4]{0:T(512)(128)(4,1)S(1)} %get-tuple-element.7, bf16[4,256,1536]{2,1,0:T(8,128)(2,1)S(1)} %copy-done.1, f32[1536]{0:T(1024)S(1)} %copy-done.3, f32[4,256]{1,0:T(4,128)S(1)} %add_rsqrt_fusion, ...), kind=kOutput, calls=%fused_computation.44 | convolution fusion | flops 816054272 | bytes 7878660 | tf_op jit(solution)/shard_map/ufd,udr->ufr/dot_general | solution.py:15
  74.0 5.6 %convolution_bitcast_fusion = f32[1,2,1536,256]{2,3,1,0:T(8,128)} fusion(bf16[4,256,1536]{2,1,0:T(8,128)(2,1)} %param.13, pred[4,256]{1,0:T(4,128)(4,1)S(1)} %iota_compare_fusion.4, bf16[4,256,256]{1,2,0:T(8,128)(2,1)} %copy.48, bf16[2,4]{1,0:T(2,128)(2,1)S(1)} %compare_convert_fusion), kind=kOutput, calls=%fused_computation.24 | convolution fusion | flops 1612709888 | bytes 6816784 | tf_op jit(solution)/shard_map/ufd,sufr->sdr/dot_general | solution.py:20
  79.6 5.8 %copy.49 = f32[1,2,1536,256]{3,1,0,2:T(2,128)} copy(f32[1,2,1536,256]{2,3,1,0:T(8,128)} %convolution_bitcast_fusion) | data formatting | bytes 6291456 | tf_op jit(solution)/shard_map/broadcast_in_dim | solution.py:67
  85.4 10.2 %all-to-all-done = bf16[16,2,96,256]{3,2,1,0:T(8,128)(2,1)} async-done(((bf16[16,2,96,256]{3,2,1,0:T(8,128)(2,1)}), bf16[16,2,96,256]{3,2,1,0:T(8,128)(2,1)}, u32[]{:S(2)}, u32[]{:S(2)}) %all-to-all-start) | async-done | bytes 1572896 | tf_op jit(solution)/shard_map/all_to_all | solution.py:57
  95.6 4.9 %all-to-all-start.3 = ((f32[1,2,1536,256]{3,1,0,2:T(2,128)}), f32[1,2,1536,256]{3,1,0,2:T(2,128)}, u32[]{:S(2)}, u32[]{:S(2)}) async-start(f32[1,2,1536,256]{3,1,0,2:T(2,128)} %copy.49), calls=%async_computation.3 | async-start | bytes 6291456 | tf_op jit(solution)/shard_map/all_to_all | solution.py:67
  103.2 3.8 %gather_fusion.2 = bf16[4,1536,256]{2,1,0:T(8,128)(2,1)} fusion(bf16[2,1536,256]{2,1,0:T(8,128)(2,1)} %bitcast.59, s32[1024]{0:T(1024)S(1)} %pad_clamp_fusion), kind=kCustom, calls=%fused_computation.1.clone | custom fusion | bytes 6291472 | tf_op jit(solution)/shard_map/jit(_take)/gather | solution.py:59
  107.0 5.2 %fusion.31 = bf16[4,256,256]{2,1,0:T(8,128)(2,1)} fusion(bf16[4,1536,256]{2,1,0:T(8,128)(2,1)} %gather_fusion.2, pred[4]{0:T(512)(128)(4,1)S(1)} %get-tuple-element.7, bf16[4,256,1536]{2,1,0:T(8,128)(2,1)} %param.13, pred[4,256]{1,0:T(4,128)(4,1)S(1)} %iota_compare_fusion.4, f32[4,256,256]{2,1,0:T(8,128)} %get-tuple-element.13), kind=kOutput, calls=%fused_computation.41 | convolution fusion | flops 810811392 | bytes 7865348 | tf_op jit(solution)/shard_map/ufd,udr->ufr/dot_general | solution.py:21
  114.2 4.7 %convolution_bitcast_fusion.1 = f32[1,2,1536,256]{2,3,1,0:T(8,128)} fusion(bf16[4,256,1536]{2,1,0:T(8,128)(2,1)S(1)} %copy-done.1, f32[1536]{0:T(1024)S(1)} %copy-done.3, f32[4,256]{1,0:T(4,128)S(1)} %add_rsqrt_fusion, f32[4,256]{1,0:T(4,128)S(1)} %broadcast_multiply_fusion.2, bf16[2,4]{1,0:T(2,128)(2,1)S(1)} %compare_convert_fusion, ...), kind=kOutput, calls=%fused_computation.25 | convolution fusion | flops 1619001344 | bytes 6830096 | tf_op jit(solution)/shard_map/ufd,sufr->sdr/dot_general | solution.py:24
  118.9 5.7 %copy.45 = f32[1,2,1536,256]{3,1,0,2:T(2,128)} copy(f32[1,2,1536,256]{2,3,1,0:T(8,128)} %convolution_bitcast_fusion.1) | data formatting | bytes 6291456 | tf_op jit(solution)/shard_map/broadcast_in_dim | solution.py:66
  124.6 45.9 %all-to-all-done.3 = f32[1,2,1536,256]{3,1,0,2:T(2,128)} async-done(((f32[1,2,1536,256]{3,1,0,2:T(2,128)}), f32[1,2,1536,256]{3,1,0,2:T(2,128)}, u32[]{:S(2)}, u32[]{:S(2)}) %all-to-all-start.3) | async-done | bytes 3145760 | tf_op jit(solution)/shard_map/all_to_all | solution.py:67
  170.5 4.9 %all-to-all-start.2 = ((f32[1,2,1536,256]{3,1,0,2:T(2,128)}), f32[1,2,1536,256]{3,1,0,2:T(2,128)}, u32[]{:S(2)}, u32[]{:S(2)}) async-start(f32[1,2,1536,256]{3,1,0,2:T(2,128)} %copy.45), calls=%async_computation.2 | async-start | bytes 6291456 | tf_op jit(solution)/shard_map/all_to_all | solution.py:66
  176.5 4.6 %multiply_reduce_fusion = (f32[4,256]{1,0:T(4,128)S(1)}, f32[4,256]{1,0:T(4,128)S(1)}, f32[4,256,1536]{2,1,0:T(8,128)S(1)}) fusion(f32[1536]{0:T(1024)S(1)} %copy-done.3, f32[4,256]{1,0:T(4,128)S(1)} %add_rsqrt_fusion, f32[4,256]{1,0:T(4,128)S(1)} %broadcast_multiply_fusion.2, bf16[4,256,1536]{2,1,0:T(8,128)(2,1)S(1)} %copy-done.1, ...), kind=kOutput, calls=%fused_computation.23 | convolution fusion | flops 817887232 | bytes 13129732 | tf_op jit(solution)/shard_map/ufr,udr->ufd/dot_general | solution.py:25
  181.1 3.9 %fusion.12 = bf16[4,256,1536]{2,1,0:T(8,128)(2,1)} fusion(bf16[4,256,1536]{2,1,0:T(8,128)(2,1)S(1)} %copy-done.1, bf16[4,256,1536]{2,1,0:T(8,128)(2,1)S(1)} %copy-done.2, f32[4,256,1536]{2,1,0:T(8,128)S(1)} %get-tuple-element.11, f32[4,256]{1,0:T(4,128)S(1)} %get-tuple-element.14, f32[4,256]{1,0:T(4,128)S(1)} %get-tuple-element.15, f32[1536]{0:T(1024)S(1)} %copy-done.3, ...), kind=kLoop, calls=%fused_computation.21 | loop fusion | flops 17301504 | bytes 15751168 | tf_op jit(solution)/shard_map/convert_element_type | solution.py:32
  191.0 54.5 %all-to-all-done.2 = f32[1,2,1536,256]{3,1,0,2:T(2,128)} async-done(((f32[1,2,1536,256]{3,1,0,2:T(2,128)}), f32[1,2,1536,256]{3,1,0,2:T(2,128)}, u32[]{:S(2)}, u32[]{:S(2)}) %all-to-all-start.2) | async-done | bytes 3145760 | tf_op jit(solution)/shard_map/all_to_all | solution.py:66
  249.7 7.2 %fusion = bf16[160,24576]{1,0:T(8,128)(2,1)S(1)} fusion(f32[32,24576]{1,0:T(8,128)S(1)} %bitcast.66, f32[160]{0:T(256)S(1)} %convert_rsqrt_fusion, s32[32]{0:T(128)S(1)} %reshape.153), kind=kOutput, calls=%fused_computation.7 | convolution fusion | flops 1517818880 | bytes 11010816 | tf_op jit(solution)/shard_map/dot_general | solution.py:71
  256.9 5.6 %copy.55 = bf16[20,8,96,256]{3,2,1,0:T(8,128)(2,1)} copy(bf16[20,8,96,256]{3,1,2,0:T(8,128)(2,1)S(1)} %bitcast.58) | data formatting | bytes 15728640
  262.5 8.8 %fusion.1 = bf16[160,24576]{1,0:T(8,128)(2,1)S(1)} fusion(f32[32,24576]{1,0:T(8,128)} %bitcast.65, f32[160]{0:T(256)S(1)} %convert_rsqrt_fusion, s32[32]{0:T(128)S(1)} %reshape.153), kind=kOutput, calls=%fused_computation.8 | convolution fusion | flops 1517818880 | bytes 11010816 | tf_op jit(solution)/shard_map/dot_general | solution.py:76
  271.3 5.6 %copy.57 = bf16[20,8,96,256]{3,2,1,0:T(8,128)(2,1)} copy(bf16[20,8,96,256]{3,1,2,0:T(8,128)(2,1)S(1)} %bitcast.57) | data formatting | bytes 15728640
  (43 shorter events, 25.3 us)
Async XLA Ops:
  11.3 6.8 %copy-start.4 = (s32[64]{0:T(128)S(1)}, s32[64]{0:T(128)}, u32[]{:S(2)}) copy-start(s32[64]{0:T(128)} %param.18) | copy-start | bytes 772
  11.3 48.0 %copy-start.5 = (s32[64]{0:T(128)S(1)}, s32[64]{0:T(128)}, u32[]{:S(2)}) copy-start(s32[64]{0:T(128)} %param.19) | copy-start | bytes 772
  11.3 48.2 %copy-start.1 = (bf16[4,256,1536]{2,1,0:T(8,128)(2,1)S(1)}, bf16[4,256,1536]{2,1,0:T(8,128)(2,1)}, u32[]{:S(2)}) copy-start(bf16[4,256,1536]{2,1,0:T(8,128)(2,1)} %param.12) | copy-start | bytes 9437188
  11.3 43.1 %all-to-all-start.1 = ((bf16[16,2,96,256]{3,2,1,0:T(8,128)(2,1)}), bf16[16,2,96,256]{3,2,1,0:T(8,128)(2,1)}, u32[]{:S(2)}, u32[]{:S(2)}) async-start(bf16[16,2,96,256]{3,2,1,0:T(8,128)(2,1)} %bitcast.70), calls=%async_computation.1 | async-start | bytes 3145728 | tf_op jit(solution)/shard_map/all_to_all | solution.py:56
  54.4 41.2 %all-to-all-start = ((bf16[16,2,96,256]{3,2,1,0:T(8,128)(2,1)}), bf16[16,2,96,256]{3,2,1,0:T(8,128)(2,1)}, u32[]{:S(2)}, u32[]{:S(2)}) async-start(bf16[16,2,96,256]{3,2,1,0:T(8,128)(2,1)} %bitcast.69), calls=%async_computation | async-start | bytes 3145728 | tf_op jit(solution)/shard_map/all_to_all | solution.py:57
  63.7 3.8 %copy-start.3 = (f32[1536]{0:T(1024)S(1)}, f32[1536]{0:T(1024)}, u32[]{:S(2)}) copy-start(f32[1536]{0:T(1024)} %param.14) | copy-start | bytes 18436
  95.6 74.9 %all-to-all-start.3 = ((f32[1,2,1536,256]{3,1,0,2:T(2,128)}), f32[1,2,1536,256]{3,1,0,2:T(2,128)}, u32[]{:S(2)}, u32[]{:S(2)}) async-start(f32[1,2,1536,256]{3,1,0,2:T(2,128)} %copy.49), calls=%async_computation.3 | async-start | bytes 6291456 | tf_op jit(solution)/shard_map/all_to_all | solution.py:67
  124.6 50.8 %copy-start = (s32[16,2]{0,1:T(2,128)S(1)}, s32[16,2]{0,1:T(2,128)}, u32[]{:S(2)}) copy-start(s32[16,2]{0,1:T(2,128)} %param.17) | copy-start | bytes 388
  170.5 74.9 %all-to-all-start.2 = ((f32[1,2,1536,256]{3,1,0,2:T(2,128)}), f32[1,2,1536,256]{3,1,0,2:T(2,128)}, u32[]{:S(2)}, u32[]{:S(2)}) async-start(f32[1,2,1536,256]{3,1,0,2:T(2,128)} %copy.45), calls=%async_computation.2 | async-start | bytes 6291456 | tf_op jit(solution)/shard_map/all_to_all | solution.py:66
  176.5 4.6 %copy-start.2 = (bf16[4,256,1536]{2,1,0:T(8,128)(2,1)S(1)}, bf16[4,256,1536]{2,1,0:T(8,128)(2,1)}, u32[]{:S(2)}) copy-start(bf16[4,256,1536]{2,1,0:T(8,128)(2,1)} %param.13) | copy-start | bytes 9437188

commit v2 on v1

--- a/solution.py
+++ b/solution.py
@@ -46,15 +46,20 @@
     live_mask = (jnp.arange(frames.shape[1], dtype=jnp.int32)[None, :] < own_lengths[:, None])[
         :, :, None
     ]
-    list_langs = slot_lang.reshape(-1)
-    send_down = jnp.take(down_weight, list_langs, axis=0).reshape(
-        devices, slots, row_count, bottleneck
+    lang_ids = jnp.arange(lang_count, dtype=jnp.int32)
+    counts = jnp.sum(jnp.where(utt_lang[None, :] == lang_ids[:, None], lengths[None, :], 0), axis=1)
+    scaling = lax.rsqrt(jnp.maximum(counts, 1).astype(jnp.float32))
+    member_langs = slot_lang.T.reshape(-1)
+    send_down = jnp.take(down_weight, member_langs, axis=0).reshape(
+        slots, devices, row_count, bottleneck
     )
-    send_up = jnp.take(up_weight, list_langs, axis=0).reshape(
-        devices, slots, row_count, bottleneck
+    send_up = jnp.take(up_weight, member_langs, axis=0).reshape(
+        slots, devices, row_count, bottleneck
     )
-    got_down = lax.all_to_all(send_down, "dp", split_axis=0, concat_axis=2, tiled=True)[0]
-    got_up = lax.all_to_all(send_up, "dp", split_axis=0, concat_axis=2, tiled=True)[0]
+    got_down = lax.all_to_all(send_down, "dp", split_axis=1, concat_axis=1, tiled=True)
+    got_up = lax.all_to_all(send_up, "dp", split_axis=1, concat_axis=1, tiled=True)
+    got_down = got_down.reshape(slots, devices * row_count, bottleneck)
+    got_up = got_up.reshape(slots, devices * row_count, bottleneck)
     w_down = jnp.take(got_down, own_slot, axis=0)
     w_up = jnp.take(got_up, own_slot, axis=0)
     slot_select = (jnp.arange(slots, dtype=jnp.int32)[:, None] == own_slot[None, :]).astype(
@@ -63,27 +68,24 @@
     d_frames, grad_down, grad_up = local_pass(
         frames, cotangent, gain, w_down, w_up, live_mask, slot_select
     )
-    back_down = lax.all_to_all(grad_down[None], "dp", split_axis=2, concat_axis=0, tiled=True)
-    back_up = lax.all_to_all(grad_up[None], "dp", split_axis=2, concat_axis=0, tiled=True)
-    members = devices * slots
-    lang_ids = jnp.arange(lang_count, dtype=jnp.int32)
-    lang_table = (lang_ids[:, None] == list_langs[None, :]).astype(jnp.float32)
-    sum_down = jnp.dot(
-        lang_table,
-        back_down.reshape(members, row_count * bottleneck),
-        precision=lax.Precision.HIGHEST,
-    )
-    sum_up = jnp.dot(
-        lang_table,
-        back_up.reshape(members, row_count * bottleneck),
-        precision=lax.Precision.HIGHEST,
-    )
-    counts = jnp.sum(jnp.where(utt_lang[None, :] == lang_ids[:, None], lengths[None, :], 0), axis=1)
-    scaling = lax.rsqrt(jnp.maximum(counts, 1).astype(jnp.float32))[:, None]
-    down_grads = (
-        (sum_down * scaling).reshape(lang_count, row_count, bottleneck).astype(jnp.bfloat16)
-    )
-    up_grads = (sum_up * scaling).reshape(lang_count, row_count, bottleneck).astype(jnp.bfloat16)
+    own_scale = jnp.take(scaling, lax.dynamic_index_in_dim(slot_lang, self_index, 0, False))
+    own_scale = own_scale[:, None, None]
+
+    def exchange_back(grad):
+        scaled = (grad * own_scale).astype(jnp.bfloat16)
+        scaled = scaled.reshape(slots, devices, row_count, bottleneck)
+        back = lax.all_to_all(scaled, "dp", split_axis=1, concat_axis=1, tiled=True)
+        return back.reshape(slots * devices, row_count, bottleneck)
+
+    back_down = exchange_back(grad_down)
+    back_up = exchange_back(grad_up)
+    lang_table = (lang_ids[:, None] == member_langs[None, :]).astype(jnp.bfloat16)
+    down_grads = jnp.einsum(
+        "lm,mkr->lkr", lang_table, back_down, preferred_element_type=jnp.float32
+    ).astype(jnp.bfloat16)
+    up_grads = jnp.einsum(
+        "lm,mkr->lkr", lang_table, back_up, preferred_element_type=jnp.float32
+    ).astype(jnp.bfloat16)
     return (d_frames, down_grads, up_grads)
 
 

time: 278 us -> 217 us (0.78)
  waiting for transfers between devices: 147 us -> 98.8 us
  matrix products: 40.5 us -> 25.1 us
  local copies, waits for them, and re-layouts: 59.5 us -> 62.5 us
    all_to_all x4, waiting for transfers between devices: 147 us -> 98.8 us  [the longest x2 39.2 us: exchange_back(): back = lax.all_to_all(scaled, 'dp', split_axis=1, concat_axis=1, tiled=True)]
    broadcast_in_dim x2 -> x0, local copies, waits for them, and re-layouts: 11.5 us -> none  [the longest x1 5.76 us: on_device(): grad_up[None]]
    dot_general x2, matrix products: 16 us -> 4.59 us  [the longest x1 2.3 us: on_device(): jnp.einsum('lm,mkr->lkr', lang_table, back_down, preferred_element_type=j...]
    reshape x1 -> x5, local copies, waits for them, and re-layouts: 0.09 us -> 10.2 us  [the longest x2 5.37 us: exchange_back(): scaled = scaled.reshape(slots, devices, row_count, bottleneck)]
    convert_element_type x0 -> x2, local copies, waits for them, and re-layouts: none -> 5.15 us  [exchange_back(): scaled = (grad * own_scale).astype(jnp.bfloat16)]
    dot_general x1, matrix products: 5.17 us -> 2.19 us  [local_pass(): jnp.einsum('ufd,udr->ufr', masked_up, w_up, preferred_element_type=jnp.fl...]
    unnamed x17 -> x18, local copies, waits for them, and re-layouts: 17.2 us -> 15.9 us
    gather x2 -> x3, local copies, waits for them, and re-layouts: 7.76 us -> 8.4 us  [the longest x1 3.88 us: on_device(): jnp.take(down_weight, member_langs, axis=0)]
  transfers between devices with their start and end apart: 4 -> 4, of which waited for: 4 -> 4; matrix products, arithmetic and copies ran while one was open for 24% -> 21% of each run, Pallas kernels for 0% -> 0%
where the time goes in v2:
time: 217 us; the launch traced here: 216 us
  waiting for transfers between devices  98.8 us (46%)
  local copies, waits for them, and re-layouts  62.5 us (29%)
  matrix products  25.1 us (12%)
  starting transfers between devices  21.3 us (10%)
  other arithmetic  7.25 us (3%)
    all_to_all x2, waiting for transfers between devices, exchange_back(): back = lax.all_to_all(scaled, 'dp', split_axis=1, concat_axis=1, tiled=True)  39.2 us
    all_to_all x1, waiting for transfers between devices, on_device(): lax.all_to_all(send_down, 'dp', split_axis=1, concat_axis=1, tiled=True)  33.4 us
    all_to_all x1, waiting for transfers between devices, on_device(): lax.all_to_all(send_up, 'dp', split_axis=1, concat_axis=1, tiled=True)  26.2 us
    unnamed x18, local copies, waits for them, and re-layouts  15.9 us
    all_to_all x2, starting transfers between devices, exchange_back(): back = lax.all_to_all(scaled, 'dp', split_axis=1, concat_axis=1, tiled=True)  9.82 us
    all_to_all x1, starting transfers between devices, on_device(): lax.all_to_all(send_down, 'dp', split_axis=1, concat_axis=1, tiled=True)  6.55 us
    reshape x2, local copies, waits for them, and re-layouts, exchange_back(): scaled = scaled.reshape(slots, devices, row_count, bottleneck)  5.37 us
    convert_element_type x2, local copies, waits for them, and re-layouts, exchange_back(): scaled = (grad * own_scale).astype(jnp.bfloat16)  5.15 us
  transfers between devices with their start and end apart: 4, of which 4 were waited for; matrix products, arithmetic and copies ran while one was open for 21% of the time, Pallas kernels for 0%

profile of v2, /device:TPU:15, one launch (start us, length us, event | category | flops | bytes accessed | tf_op | source)
XLA Modules:
  0.0 215.7 jit_solution(16785040773158458793)
XLA Ops:
  1.4 3.9 %gather_fusion.4 = bf16[32,96,256]{2,1,0:T(8,128)(2,1)S(1)} fusion(bf16[160,96,256]{2,1,0:T(8,128)(2,1)} %param.15, s32[1024]{0:T(1024)S(1)} %pad_clamp_fusion.2), kind=kCustom, calls=%fused_computation.2.clone | custom fusion | bytes 3145856 | tf_op jit(solution)/shard_map/jit(_take)/gather | solution.py:53
  5.3 3.9 %gather_fusion.2 = bf16[32,96,256]{2,1,0:T(8,128)(2,1)S(1)} fusion(bf16[160,96,256]{2,1,0:T(8,128)(2,1)} %param.16, s32[1024]{0:T(1024)S(1)} %pad_clamp_fusion.2), kind=kCustom, calls=%fused_computation.clone | custom fusion | bytes 3145856 | tf_op jit(solution)/shard_map/jit(_take)/gather | solution.py:56
  12.0 6.6 %all-to-all-start.1 = ((bf16[2,16,96,256]{3,2,0,1:T(8,128)(2,1)}), bf16[2,16,96,256]{3,2,0,1:T(8,128)(2,1)}, u32[]{:S(2)}, u32[]{:S(2)}) async-start(bf16[2,16,96,256]{3,2,0,1:T(8,128)(2,1)} %copy.51), calls=%async_computation.1 | async-start | bytes 3145728 | tf_op jit(solution)/shard_map/all_to_all | solution.py:59
  18.6 2.8 %copy.49 = bf16[2,16,96,256]{3,2,0,1:T(8,128)(2,1)} copy(bf16[2,16,96,256]{3,2,1,0:T(8,128)(2,1)} %bitcast.69) | data formatting | bytes 3145728 | tf_op jit(solution)/shard_map/reshape | solution.py:56
  21.4 33.4 %all-to-all-done.1 = bf16[2,16,96,256]{3,2,0,1:T(8,128)(2,1)} async-done(((bf16[2,16,96,256]{3,2,0,1:T(8,128)(2,1)}), bf16[2,16,96,256]{3,2,0,1:T(8,128)(2,1)}, u32[]{:S(2)}, u32[]{:S(2)}) %all-to-all-start.1) | async-done | bytes 1572896 | tf_op jit(solution)/shard_map/all_to_all | solution.py:59
  54.8 4.9 %all-to-all-start = ((bf16[2,16,96,256]{3,2,0,1:T(8,128)(2,1)}), bf16[2,16,96,256]{3,2,0,1:T(8,128)(2,1)}, u32[]{:S(2)}, u32[]{:S(2)}) async-start(bf16[2,16,96,256]{3,2,0,1:T(8,128)(2,1)} %copy.49), calls=%async_computation | async-start | bytes 3145728 | tf_op jit(solution)/shard_map/all_to_all | solution.py:60
  63.3 2.7 %copy.52 = bf16[2,16,96,256]{3,2,1,0:T(8,128)(2,1)} copy(bf16[2,16,96,256]{3,2,0,1:T(8,128)(2,1)} %all-to-all-done.1) | data formatting | bytes 3145728 | tf_op jit(solution)/shard_map/all_to_all | solution.py:59
  66.0 3.8 %gather_fusion.5 = bf16[4,1536,256]{2,1,0:T(8,128)(2,1)} fusion(bf16[2,1536,256]{2,1,0:T(8,128)(2,1)} %bitcast.64, s32[1024]{0:T(1024)S(1)} %pad_clamp_fusion.1), kind=kCustom, calls=%fused_computation.3.clone | custom fusion | bytes 6291472 | tf_op jit(solution)/shard_map/jit(_take)/gather | solution.py:63
  69.8 26.2 %all-to-all-done = bf16[2,16,96,256]{3,2,0,1:T(8,128)(2,1)} async-done(((bf16[2,16,96,256]{3,2,0,1:T(8,128)(2,1)}), bf16[2,16,96,256]{3,2,0,1:T(8,128)(2,1)}, u32[]{:S(2)}, u32[]{:S(2)}) %all-to-all-start) | async-done | bytes 1572896 | tf_op jit(solution)/shard_map/all_to_all | solution.py:60
  96.0 2.7 %copy.50 = bf16[2,16,96,256]{3,2,1,0:T(8,128)(2,1)} copy(bf16[2,16,96,256]{3,2,0,1:T(8,128)(2,1)} %all-to-all-done) | data formatting | bytes 3145728 | tf_op jit(solution)/shard_map/all_to_all | solution.py:60
  98.7 3.8 %gather_fusion.3 = bf16[4,1536,256]{2,1,0:T(8,128)(2,1)} fusion(bf16[2,1536,256]{2,1,0:T(8,128)(2,1)} %bitcast.63, s32[1024]{0:T(1024)S(1)} %pad_clamp_fusion.1), kind=kCustom, calls=%fused_computation.1.clone | custom fusion | bytes 6291472 | tf_op jit(solution)/shard_map/jit(_take)/gather | solution.py:64
  102.5 4.4 %multiply_convert_fusion = (bf16[4,256,256]{2,1,0:T(8,128)(2,1)}, f32[4,256,256]{2,1,0:T(8,128)S(1)}) fusion(bf16[4,1536,256]{2,1,0:T(8,128)(2,1)} %gather_fusion.5, pred[4]{0:T(512)(128)(4,1)S(1)} %get-tuple-element.22, bf16[4,256,1536]{2,1,0:T(8,128)(2,1)S(1)} %copy-done.1, f32[1536]{0:T(1024)S(1)} %copy-done.5, f32[4,256]{1,0:T(4,128)S(1)} %add_rsqrt_fusion, ...), kind=kOutput, calls=%fused_computation.49 | convolution fusion | flops 816054272 | bytes 7878660 | tf_op jit(solution)/shard_map/ufd,udr->ufr/dot_general | solution.py:15
  111.2 4.2 %fusion.28 = bf16[2,1536,256]{1,2,0:T(8,128)(2,1)} fusion(bf16[4,256,1536]{2,1,0:T(8,128)(2,1)S(1)} %copy-done.1, f32[1536]{0:T(1024)S(1)} %copy-done.5, f32[4,256]{1,0:T(4,128)S(1)} %add_rsqrt_fusion, f32[4,256]{1,0:T(4,128)S(1)} %broadcast_multiply_fusion.2, f32[2]{0:T(128)S(1)} %and_select_fusion.1, bf16[2,4]{1,0:T(2,128)(2,1)S(1)} %compare_convert_fusion, ...), kind=kOutput, calls=%fused_computation.37 | convolution fusion | flops 1620574208 | bytes 5257240 | tf_op jit(solution)/shard_map/ufd,sufr->sdr/dot_general | solution.py:24
  117.9 2.7 %copy.55 = bf16[2,16,96,256]{3,2,0,1:T(8,128)(2,1)} copy(bf16[2,16,96,256]{3,2,1,0:T(8,128)(2,1)} %bitcast.66) | data formatting | bytes 3145728 | tf_op jit(solution)/shard_map/reshape | solution.py:76
  120.6 4.9 %all-to-all-start.2 = ((bf16[2,16,96,256]{3,2,0,1:T(8,128)(2,1)}), bf16[2,16,96,256]{3,2,0,1:T(8,128)(2,1)}, u32[]{:S(2)}, u32[]{:S(2)}) async-start(bf16[2,16,96,256]{3,2,0,1:T(8,128)(2,1)} %copy.55), calls=%async_computation.2 | async-start | bytes 3145728 | tf_op jit(solution)/shard_map/all_to_all | solution.py:77
  127.6 5.1 %fusion.25 = bf16[2,1536,256]{1,2,0:T(8,128)(2,1)} fusion(bf16[4,256,1536]{2,1,0:T(8,128)(2,1)} %param.13, pred[4,256]{1,0:T(4,128)(4,1)S(1)} %iota_compare_fusion.2, f32[2]{0:T(128)S(1)} %and_select_fusion.1, bf16[4,256,256]{1,2,0:T(8,128)(2,1)} %copy.57, bf16[2,4]{1,0:T(2,128)(2,1)S(1)} %compare_convert_fusion), kind=kOutput, calls=%fused_computation.36 | convolution fusion | flops 1614282752 | bytes 5243928 | tf_op jit(solution)/shard_map/ufd,sufr->sdr/dot_general | solution.py:20
  135.2 2.7 %copy.59 = bf16[2,16,96,256]{3,2,0,1:T(8,128)(2,1)} copy(bf16[2,16,96,256]{3,2,1,0:T(8,128)(2,1)} %bitcast.67) | data formatting | bytes 3145728 | tf_op jit(solution)/shard_map/reshape | solution.py:76
  137.9 23.9 %all-to-all-done.2 = bf16[2,16,96,256]{3,2,0,1:T(8,128)(2,1)} async-done(((bf16[2,16,96,256]{3,2,0,1:T(8,128)(2,1)}), bf16[2,16,96,256]{3,2,0,1:T(8,128)(2,1)}, u32[]{:S(2)}, u32[]{:S(2)}) %all-to-all-start.2) | async-done | bytes 1572896 | tf_op jit(solution)/shard_map/all_to_all | solution.py:77
  161.8 4.9 %all-to-all-start.3 = ((bf16[2,16,96,256]{3,2,0,1:T(8,128)(2,1)}), bf16[2,16,96,256]{3,2,0,1:T(8,128)(2,1)}, u32[]{:S(2)}, u32[]{:S(2)}) async-start(bf16[2,16,96,256]{3,2,0,1:T(8,128)(2,1)} %copy.59), calls=%async_computation.3 | async-start | bytes 3145728 | tf_op jit(solution)/shard_map/all_to_all | solution.py:77
  166.7 4.6 %multiply_reduce_fusion = (f32[4,256]{1,0:T(4,128)S(1)}, f32[4,256]{1,0:T(4,128)S(1)}, f32[4,256,1536]{2,1,0:T(8,128)S(1)}) fusion(f32[1536]{0:T(1024)S(1)} %copy-done.5, f32[4,256]{1,0:T(4,128)S(1)} %add_rsqrt_fusion, f32[4,256]{1,0:T(4,128)S(1)} %broadcast_multiply_fusion.2, bf16[4,256,1536]{2,1,0:T(8,128)(2,1)S(1)} %copy-done.1, ...), kind=kOutput, calls=%fused_computation.22 | convolution fusion | flops 817887232 | bytes 13129732 | tf_op jit(solution)/shard_map/ufr,udr->ufd/dot_general | solution.py:25
  171.4 4.0 %fusion.10 = bf16[4,256,1536]{2,1,0:T(8,128)(2,1)} fusion(bf16[4,256,1536]{2,1,0:T(8,128)(2,1)S(1)} %copy-done.1, bf16[4,256,1536]{2,1,0:T(8,128)(2,1)S(1)} %copy-done.4, f32[4,256,1536]{2,1,0:T(8,128)S(1)} %get-tuple-element.26, f32[4,256]{1,0:T(4,128)S(1)} %get-tuple-element.29, f32[4,256]{1,0:T(4,128)S(1)} %get-tuple-element.30, f32[1536]{0:T(1024)S(1)} %copy-done.5, ...), kind=kLoop, calls=%fused_computation.20 | loop fusion | flops 17301504 | bytes 15751168 | tf_op jit(solution)/shard_map/convert_element_type | solution.py:32
  179.9 7.8 %copy.61 = bf16[160,96,256]{2,1,0:T(8,128)(2,1)} copy(bf16[160,96,256]{2,0,1:T(8,128)(2,1)S(1)} %convolution_convert_fusion.1) | data formatting | bytes 15728640
  187.7 15.3 %all-to-all-done.3 = bf16[2,16,96,256]{3,2,0,1:T(8,128)(2,1)} async-done(((bf16[2,16,96,256]{3,2,0,1:T(8,128)(2,1)}), bf16[2,16,96,256]{3,2,0,1:T(8,128)(2,1)}, u32[]{:S(2)}, u32[]{:S(2)}) %all-to-all-start.3) | async-done | bytes 1572896 | tf_op jit(solution)/shard_map/all_to_all | solution.py:77
  207.6 8.1 %copy.62 = bf16[160,96,256]{2,1,0:T(8,128)(2,1)} copy(bf16[160,96,256]{2,0,1:T(8,128)(2,1)S(1)} %convolution_convert_fusion) | data formatting | bytes 15728640
  (51 shorter events, 27.7 us)
Async XLA Ops:
  12.0 42.8 %all-to-all-start.1 = ((bf16[2,16,96,256]{3,2,0,1:T(8,128)(2,1)}), bf16[2,16,96,256]{3,2,0,1:T(8,128)(2,1)}, u32[]{:S(2)}, u32[]{:S(2)}) async-start(bf16[2,16,96,256]{3,2,0,1:T(8,128)(2,1)} %copy.51), calls=%async_computation.1 | async-start | bytes 3145728 | tf_op jit(solution)/shard_map/all_to_all | solution.py:59
  18.5 41.2 %copy-start.7 = (s32[64]{0:T(128)S(1)}, s32[64]{0:T(128)}, u32[]{:S(2)}) copy-start(s32[64]{0:T(128)} %param.18) | copy-start | bytes 772
  18.5 41.2 %copy-start = (s32[16,2]{0,1:T(2,128)S(1)}, s32[16,2]{0,1:T(2,128)}, u32[]{:S(2)}) copy-start(s32[16,2]{0,1:T(2,128)} %param.17) | copy-start | bytes 388
  18.5 42.3 %copy-start.6 = (s32[64]{0:T(128)S(1)}, s32[64]{0:T(128)}, u32[]{:S(2)}) copy-start(s32[64]{0:T(128)} %param.19) | copy-start | bytes 772
  18.5 43.3 %copy-start.1 = (bf16[4,256,1536]{2,1,0:T(8,128)(2,1)S(1)}, bf16[4,256,1536]{2,1,0:T(8,128)(2,1)}, u32[]{:S(2)}) copy-start(bf16[4,256,1536]{2,1,0:T(8,128)(2,1)} %param.12) | copy-start | bytes 9437188
  54.8 41.2 %all-to-all-start = ((bf16[2,16,96,256]{3,2,0,1:T(8,128)(2,1)}), bf16[2,16,96,256]{3,2,0,1:T(8,128)(2,1)}, u32[]{:S(2)}, u32[]{:S(2)}) async-start(bf16[2,16,96,256]{3,2,0,1:T(8,128)(2,1)} %copy.49), calls=%async_computation | async-start | bytes 3145728 | tf_op jit(solution)/shard_map/all_to_all | solution.py:60
  98.7 3.8 %copy-start.5 = (f32[1536]{0:T(1024)S(1)}, f32[1536]{0:T(1024)}, u32[]{:S(2)}) copy-start(f32[1536]{0:T(1024)} %param.14) | copy-start | bytes 18436
  102.5 4.4 %copy-start.2 = (bf16[4,1536,256]{2,1,0:T(8,128)(2,1)S(1)}, bf16[4,1536,256]{2,1,0:T(8,128)(2,1)}, u32[]{:S(2)}) copy-start(bf16[4,1536,256]{2,1,0:T(8,128)(2,1)} %gather_fusion.3) | copy-start | bytes 9437188
  102.5 4.4 %copy-start.3 = (bf16[4,256,1536]{2,1,0:T(8,128)(2,1)S(1)}, bf16[4,256,1536]{2,1,0:T(8,128)(2,1)}, u32[]{:S(2)}) copy-start(bf16[4,256,1536]{2,1,0:T(8,128)(2,1)} %param.13) | copy-start | bytes 9437188
  120.6 41.2 %all-to-all-start.2 = ((bf16[2,16,96,256]{3,2,0,1:T(8,128)(2,1)}), bf16[2,16,96,256]{3,2,0,1:T(8,128)(2,1)}, u32[]{:S(2)}, u32[]{:S(2)}) async-start(bf16[2,16,96,256]{3,2,0,1:T(8,128)(2,1)} %copy.55), calls=%async_computation.2 | async-start | bytes 3145728 | tf_op jit(solution)/shard_map/all_to_all | solution.py:77
  161.8 41.2 %all-to-all-start.3 = ((bf16[2,16,96,256]{3,2,0,1:T(8,128)(2,1)}), bf16[2,16,96,256]{3,2,0,1:T(8,128)(2,1)}, u32[]{:S(2)}, u32[]{:S(2)}) async-start(bf16[2,16,96,256]{3,2,0,1:T(8,128)(2,1)} %copy.59), calls=%async_computation.3 | async-start | bytes 3145728 | tf_op jit(solution)/shard_map/all_to_all | solution.py:77
  166.7 4.6 %copy-start.4 = (bf16[4,256,1536]{2,1,0:T(8,128)(2,1)S(1)}, bf16[4,256,1536]{2,1,0:T(8,128)(2,1)}, u32[]{:S(2)}) copy-start(bf16[4,256,1536]{2,1,0:T(8,128)(2,1)} %param.13) | copy-start | bytes 9437188

commit v3 on v2

--- a/solution.py
+++ b/solution.py
@@ -49,19 +49,22 @@
     lang_ids = jnp.arange(lang_count, dtype=jnp.int32)
     counts = jnp.sum(jnp.where(utt_lang[None, :] == lang_ids[:, None], lengths[None, :], 0), axis=1)
     scaling = lax.rsqrt(jnp.maximum(counts, 1).astype(jnp.float32))
-    member_langs = slot_lang.T.reshape(-1)
+    member_langs = slot_lang.reshape(-1)
     send_down = jnp.take(down_weight, member_langs, axis=0).reshape(
-        slots, devices, row_count, bottleneck
+        devices, slots, row_count, bottleneck
     )
     send_up = jnp.take(up_weight, member_langs, axis=0).reshape(
-        slots, devices, row_count, bottleneck
+        devices, slots, row_count, bottleneck
     )
-    got_down = lax.all_to_all(send_down, "dp", split_axis=1, concat_axis=1, tiled=True)
-    got_up = lax.all_to_all(send_up, "dp", split_axis=1, concat_axis=1, tiled=True)
-    got_down = got_down.reshape(slots, devices * row_count, bottleneck)
-    got_up = got_up.reshape(slots, devices * row_count, bottleneck)
-    w_down = jnp.take(got_down, own_slot, axis=0)
-    w_up = jnp.take(got_up, own_slot, axis=0)
+    sent = jnp.concatenate([send_down, send_up], axis=1)
+    got = lax.all_to_all(sent, "dp", split_axis=0, concat_axis=0, tiled=True)
+
+    def own_rows(offset):
+        rows = jnp.take(got, own_slot + offset, axis=1)
+        return rows.transpose(1, 0, 2, 3).reshape(per_device, devices * row_count, bottleneck)
+
+    w_down = own_rows(0)
+    w_up = own_rows(slots)
     slot_select = (jnp.arange(slots, dtype=jnp.int32)[:, None] == own_slot[None, :]).astype(
         jnp.bfloat16
     )
@@ -70,21 +73,22 @@
     )
     own_scale = jnp.take(scaling, lax.dynamic_index_in_dim(slot_lang, self_index, 0, False))
     own_scale = own_scale[:, None, None]
-
-    def exchange_back(grad):
-        scaled = (grad * own_scale).astype(jnp.bfloat16)
-        scaled = scaled.reshape(slots, devices, row_count, bottleneck)
-        back = lax.all_to_all(scaled, "dp", split_axis=1, concat_axis=1, tiled=True)
-        return back.reshape(slots * devices, row_count, bottleneck)
-
-    back_down = exchange_back(grad_down)
-    back_up = exchange_back(grad_up)
-    lang_table = (lang_ids[:, None] == member_langs[None, :]).astype(jnp.bfloat16)
+    grads = jnp.concatenate([grad_down * own_scale, grad_up * own_scale], axis=0)
+    grads = grads.astype(jnp.bfloat16).reshape(2 * slots, devices, row_count, bottleneck)
+    back = lax.all_to_all(
+        grads.transpose(1, 0, 2, 3), "dp", split_axis=0, concat_axis=0, tiled=True
+    ).reshape(devices * 2 * slots, row_count, bottleneck)
+    both_langs = jnp.concatenate([slot_lang, slot_lang], axis=1).reshape(-1)
+    is_down = (jnp.arange(2 * slots, dtype=jnp.int32) < slots)[None, :]
+    is_down = jnp.broadcast_to(is_down, (devices, 2 * slots)).reshape(-1)
+    matches = lang_ids[:, None] == both_langs[None, :]
+    down_table = (matches & is_down[None, :]).astype(jnp.bfloat16)
+    up_table = (matches & ~is_down[None, :]).astype(jnp.bfloat16)
     down_grads = jnp.einsum(
-        "lm,mkr->lkr", lang_table, back_down, preferred_element_type=jnp.float32
+        "lm,mkr->lkr", down_table, back, preferred_element_type=jnp.float32
     ).astype(jnp.bfloat16)
     up_grads = jnp.einsum(
-        "lm,mkr->lkr", lang_table, back_up, preferred_element_type=jnp.float32
+        "lm,mkr->lkr", up_table, back, preferred_element_type=jnp.float32
     ).astype(jnp.bfloat16)
     return (d_frames, down_grads, up_grads)
 

time: 217 us -> 231 us (1.065)
  waiting for transfers between devices: 98.8 us -> 126 us
  local copies, waits for them, and re-layouts: 62.5 us -> 46.7 us
  other arithmetic: 7.25 us -> 17.1 us
  starting transfers between devices: 21.3 us -> 11.6 us
  matrix products: 25.1 us -> 29 us
    all_to_all x4 -> x2, waiting for transfers between devices: 98.8 us -> 126 us  [the longest x1 64.1 us: on_device(): got = lax.all_to_all(sent, 'dp', split_axis=0, concat_axis=0, tiled=True)]
    reshape x5 -> x1, local copies, waits for them, and re-layouts: 10.2 us -> 0.09 us  [on_device(): member_langs = slot_lang.reshape(-1)]
    all_to_all x4 -> x0, local copies, waits for them, and re-layouts: 9.9 us -> none  [the longest x2 4.57 us: exchange_back(): back = lax.all_to_all(scaled, 'dp', split_axis=1, concat_axis=1, tiled=True)]
    all_to_all x4 -> x2, starting transfers between devices: 21.3 us -> 11.6 us  [the longest x1 6.69 us: on_device(): got = lax.all_to_all(sent, 'dp', split_axis=0, concat_axis=0, tiled=True)]
    dot_general x2, matrix products: 4.59 us -> 11.8 us  [the longest x1 7.53 us: on_device(): jnp.einsum('lm,mkr->lkr', up_table, back, preferred_element_type=jnp.floa...]
    mul x0 -> x2, local copies, waits for them, and re-layouts: none -> 5.3 us  [the longest x1 2.72 us: on_device(): grad_up * own_scale]
    convert_element_type x2 -> x0, local copies, waits for them, and re-layouts: 5.15 us -> none  [exchange_back(): scaled = (grad * own_scale).astype(jnp.bfloat16)]
    select_n x2 -> x3, other arithmetic: 0.01 us -> 4.81 us  [own_rows(): rows = jnp.take(got, own_slot + offset, axis=1)]
  transfers between devices with their start and end apart: 4 -> 2, of which waited for: 4 -> 2; matrix products, arithmetic and copies ran while one was open for 21% -> 6% of each run, Pallas kernels for 0% -> 0%
where the time goes in v3:
time: 231 us
  waiting for transfers between devices  126 us (55%)
  local copies, waits for them, and re-layouts  46.7 us (20%)
  matrix products  29 us (13%)
  other arithmetic  17.1 us (7%)
  starting transfers between devices  11.6 us (5%)
    all_to_all x1, waiting for transfers between devices, on_device(): got = lax.all_to_all(sent, 'dp', split_axis=0, concat_axis=0, tiled=True)  64.1 us
    all_to_all x1, waiting for transfers between devices, on_device(): lax.all_to_all(grads.transpose(1, 0, 2, 3), 'dp', split_axis=0, concat_ax...  61.4 us
    unnamed x25, local copies, waits for them, and re-layouts  20.6 us
    dot_general x1, matrix products, on_device(): jnp.einsum('lm,mkr->lkr', up_table, back, preferred_element_type=jnp.floa...  7.53 us
    all_to_all x1, starting transfers between devices, on_device(): got = lax.all_to_all(sent, 'dp', split_axis=0, concat_axis=0, tiled=True)  6.69 us
    all_to_all x1, starting transfers between devices, on_device(): lax.all_to_all(grads.transpose(1, 0, 2, 3), 'dp', split_axis=0, concat_ax...  4.91 us
    gather x2, local copies, waits for them, and re-layouts, own_rows(): rows = jnp.take(got, own_slot + offset, axis=1)  4.82 us
    select_n x3, other arithmetic, own_rows(): rows = jnp.take(got, own_slot + offset, axis=1)  4.81 us
  transfers between devices with their start and end apart: 2, of which 2 were waited for; matrix products, arithmetic and copies ran while one was open for 6% of the time, Pallas kernels for 0%

profile of v3, /device:TPU:15, one launch (start us, length us, event | category | flops | bytes accessed | tf_op | source)
XLA Modules:
  0.0 230.7 jit_solution(11467691037405464905)
XLA Ops:
  1.5 3.9 %gather_fusion.3 = bf16[32,96,256]{2,1,0:T(8,128)(2,1)S(1)} fusion(bf16[160,96,256]{2,1,0:T(8,128)(2,1)} %param.16, s32[1024]{0:T(1024)S(1)} %pad_clamp_fusion.3), kind=kCustom, calls=%fused_computation.2.clone | custom fusion | bytes 3145856 | tf_op jit(solution)/shard_map/jit(_take)/gather | solution.py:56
  5.4 3.9 %gather_fusion.2 = bf16[32,96,256]{2,1,0:T(8,128)(2,1)S(1)} fusion(bf16[160,96,256]{2,1,0:T(8,128)(2,1)} %param.15, s32[1024]{0:T(1024)S(1)} %pad_clamp_fusion.3), kind=kCustom, calls=%fused_computation.clone | custom fusion | bytes 3145856 | tf_op jit(solution)/shard_map/jit(_take)/gather | solution.py:53
  11.6 6.7 %all-to-all-start = ((bf16[16,4,96,256]{3,2,1,0:T(8,128)(2,1)}), bf16[16,4,96,256]{3,2,1,0:T(8,128)(2,1)S(1)}, u32[]{:S(2)}, u32[]{:S(2)}) async-start(bf16[16,4,96,256]{3,2,1,0:T(8,128)(2,1)} %pad_maximum_fusion), calls=%async_computation | async-start | bytes 6291456 | tf_op jit(solution)/shard_map/all_to_all | solution.py:60
  20.4 2.5 %convert_reduce_fusion = f32[4,256]{1,0:T(4,128)S(1)} fusion(bf16[4,256,1536]{2,1,0:T(8,128)(2,1)} %param.12), kind=kLoop, calls=%fused_computation.7 | loop fusion | flops 3144704 | bytes 3149824 | tf_op jit(solution)/shard_map/reduce_sum | solution.py:9
  24.0 64.1 %all-to-all-done = bf16[16,4,96,256]{3,2,1,0:T(8,128)(2,1)S(1)} async-done(((bf16[16,4,96,256]{3,2,1,0:T(8,128)(2,1)}), bf16[16,4,96,256]{3,2,1,0:T(8,128)(2,1)S(1)}, u32[]{:S(2)}, u32[]{:S(2)}) %all-to-all-start) | async-done | bytes 3145760 | tf_op jit(solution)/shard_map/all_to_all | solution.py:60
  88.2 2.4 %gather_fusion.5 = bf16[4,16,96,256]{3,2,1,0:T(8,128)(2,1)} fusion(bf16[16,4,96,256]{3,2,1,0:T(8,128)(2,1)S(1)} %all-to-all-done, s32[1024]{0:T(1024)S(1)} %pad_clamp_fusion.1), kind=kCustom, calls=%fused_computation.3.clone | custom fusion | bytes 6291472 | tf_op jit(solution)/shard_map/jit(_take)/gather | solution.py:63
  90.6 2.4 %broadcast_select_fusion = bf16[4,16,96,256]{3,2,1,0:T(8,128)(2,1)S(1)} fusion(bf16[4,16,96,256]{3,2,1,0:T(8,128)(2,1)} %gather_fusion.5, pred[4]{0:T(512)(128)(4,1)S(1)} %get-tuple-element.19), kind=kLoop, calls=%fused_computation.31 | loop fusion | flops 1572864 | bytes 6291460 | tf_op jit(solution)/shard_map/jit(_take)/select_n | solution.py:63
  93.4 2.6 %multiply_convert_fusion = (bf16[4,256,256]{2,1,0:T(8,128)(2,1)}, f32[4,256,256]{2,1,0:T(8,128)}) fusion(bf16[4,1536,256]{2,1,0:T(8,128)(2,1)S(1)} %bitcast.75, bf16[4,256,1536]{2,1,0:T(8,128)(2,1)S(1)} %copy-done.2, f32[1536]{0:T(1024)S(1)} %copy-done.7, f32[4,256]{1,0:T(4,128)S(1)} %add_rsqrt_fusion, f32[4,256]{1,0:T(4,128)S(1)} %broadcast_multiply_fusion.2), kind=kOutput, calls=%fused_computation.50 | convolution fusion | flops 814481408 | bytes 7878656 | tf_op jit(solution)/shard_map/ufd,udr->ufr/dot_general | solution.py:15
  96.0 2.0 copy.41
  98.0 2.4 %gather_fusion.4 = bf16[4,16,96,256]{3,2,1,0:T(8,128)(2,1)} fusion(bf16[16,4,96,256]{3,2,1,0:T(8,128)(2,1)S(1)} %all-to-all-done, s32[1024]{0:T(1024)S(1)} %pad_clamp_fusion.2), kind=kCustom, calls=%fused_computation.1.clone | custom fusion | bytes 6291472 | tf_op jit(solution)/shard_map/jit(_take)/gather | solution.py:63
  100.4 2.4 %broadcast_select_fusion.1 = bf16[4,16,96,256]{3,2,1,0:T(8,128)(2,1)S(1)} fusion(bf16[4,16,96,256]{3,2,1,0:T(8,128)(2,1)} %gather_fusion.4, pred[4]{0:T(512)(128)(4,1)S(1)} %get-tuple-element.21), kind=kLoop, calls=%fused_computation.32 | loop fusion | flops 1572864 | bytes 6291460 | tf_op jit(solution)/shard_map/jit(_take)/select_n | solution.py:63
  107.6 4.1 %fusion.25 = bf16[2,1536,256]{1,2,0:T(8,128)(2,1)} fusion(bf16[4,256,1536]{2,1,0:T(8,128)(2,1)S(1)} %copy-done.5, pred[4,256]{1,0:T(4,128)(4,1)S(1)} %iota_compare_fusion.2, f32[2]{0:T(128)S(1)} %and_select_fusion.1, bf16[4,256,256]{1,2,0:T(8,128)(2,1)} %copy.41, bf16[2,4]{1,0:T(2,128)(2,1)S(1)} %compare_convert_fusion), kind=kOutput, calls=%fused_computation.39 | convolution fusion | flops 1614282752 | bytes 5243928 | tf_op jit(solution)/shard_map/ufd,sufr->sdr/dot_general | solution.py:20
  111.7 2.7 %copy.42 = bf16[2,1536,256]{2,1,0:T(8,128)(2,1)} copy(bf16[2,1536,256]{1,2,0:T(8,128)(2,1)} %fusion.25) | data formatting | bytes 3145728 | tf_op jit(solution)/shard_map/mul | solution.py:76
  114.4 4.2 %fusion.28 = bf16[2,1536,256]{1,2,0:T(8,128)(2,1)} fusion(bf16[4,256,1536]{2,1,0:T(8,128)(2,1)S(1)} %copy-done.3, f32[1536]{0:T(1024)S(1)} %copy-done.7, f32[4,256]{1,0:T(4,128)S(1)} %add_rsqrt_fusion, f32[4,256]{1,0:T(4,128)S(1)} %broadcast_multiply_fusion.2, f32[2]{0:T(128)S(1)} %and_select_fusion.1, bf16[2,4]{1,0:T(2,128)(2,1)S(1)} %compare_convert_fusion, ...), kind=kOutput, calls=%fused_computation.40 | convolution fusion | flops 1620574208 | bytes 5257240 | tf_op jit(solution)/shard_map/ufd,sufr->sdr/dot_general | solution.py:24
  118.6 2.6 %copy.40 = bf16[2,1536,256]{2,1,0:T(8,128)(2,1)} copy(bf16[2,1536,256]{1,2,0:T(8,128)(2,1)} %fusion.28) | data formatting | bytes 3145728 | tf_op jit(solution)/shard_map/mul | solution.py:76
  121.2 2.2 maximum_bitcast_fusion
  125.3 4.9 %all-to-all-start.1 = ((bf16[16,4,96,256]{3,2,1,0:T(8,128)(2,1)}), bf16[16,4,96,256]{3,2,1,0:T(8,128)(2,1)}, u32[]{:S(2)}, u32[]{:S(2)}) async-start(bf16[16,4,96,256]{3,2,1,0:T(8,128)(2,1)} %copy.43), calls=%async_computation.1 | async-start | bytes 6291456 | tf_op jit(solution)/shard_map/all_to_all | solution.py:78
  130.6 4.3 %multiply_reduce_fusion = (f32[4,256]{1,0:T(4,128)S(1)}, f32[4,256]{1,0:T(4,128)S(1)}, f32[4,256,1536]{2,1,0:T(8,128)S(1)}) fusion(f32[1536]{0:T(1024)S(1)} %copy-done.7, f32[4,256]{1,0:T(4,128)S(1)} %add_rsqrt_fusion, f32[4,256]{1,0:T(4,128)S(1)} %broadcast_multiply_fusion.2, bf16[4,256,1536]{2,1,0:T(8,128)(2,1)S(1)} %copy-done.3, ...), kind=kOutput, calls=%fused_computation.22 | convolution fusion | flops 816314368 | bytes 13129728 | tf_op jit(solution)/shard_map/ufr,udr->ufd/dot_general | solution.py:25
  134.9 3.9 %fusion.10 = bf16[4,256,1536]{2,1,0:T(8,128)(2,1)} fusion(bf16[4,256,1536]{2,1,0:T(8,128)(2,1)S(1)} %copy-done.3, bf16[4,256,1536]{2,1,0:T(8,128)(2,1)S(1)} %copy-done.6, f32[4,256,1536]{2,1,0:T(8,128)S(1)} %get-tuple-element.25, f32[4,256]{1,0:T(4,128)S(1)} %get-tuple-element.28, f32[4,256]{1,0:T(4,128)S(1)} %get-tuple-element.29, f32[1536]{0:T(1024)S(1)} %copy-done.7, ...), kind=kLoop, calls=%fused_computation.20 | loop fusion | flops 17301504 | bytes 15751168 | tf_op jit(solution)/shard_map/convert_element_type | solution.py:32
  138.8 61.4 %all-to-all-done.1 = bf16[16,4,96,256]{3,2,1,0:T(8,128)(2,1)} async-done(((bf16[16,4,96,256]{3,2,1,0:T(8,128)(2,1)}), bf16[16,4,96,256]{3,2,1,0:T(8,128)(2,1)}, u32[]{:S(2)}, u32[]{:S(2)}) %all-to-all-start.1) | async-done | bytes 3145760 | tf_op jit(solution)/shard_map/all_to_all | solution.py:78
  200.2 4.3 %convolution_convert_fusion.1 = bf16[160,96,256]{2,0,1:T(8,128)(2,1)S(1)} fusion(bf16[64,96,256]{2,1,0:T(8,128)(2,1)} %bitcast.23, s32[64]{0:T(128)S(1)} %eq.46, pred[64]{0:T(512)(128)(4,1)S(1)} %and.59), kind=kOutput, calls=%fused_computation.14 | convolution fusion | flops 507269120 | bytes 11010368 | tf_op jit(solution)/shard_map/lm,mkr->lkr/dot_general | solution.py:87
  204.5 7.5 %convolution_convert_fusion = bf16[160,96,256]{2,0,1:T(8,128)(2,1)} fusion(bf16[64,96,256]{2,1,0:T(8,128)(2,1)} %bitcast.23, s32[64]{0:T(128)S(1)} %eq.46, pred[64]{0:T(512)(128)(4,1)S(1)} %not.8), kind=kOutput, calls=%fused_computation.13 | convolution fusion | flops 507269120 | bytes 11010368 | tf_op jit(solution)/shard_map/lm,mkr->lkr/dot_general | solution.py:90
  212.1 10.9 %copy.46 = bf16[160,96,256]{2,1,0:T(8,128)(2,1)} copy(bf16[160,96,256]{2,0,1:T(8,128)(2,1)} %convolution_convert_fusion) | data formatting | bytes 15728640
  223.0 7.7 %copy.45 = bf16[160,96,256]{2,1,0:T(8,128)(2,1)} copy(bf16[160,96,256]{2,0,1:T(8,128)(2,1)S(1)} %convolution_convert_fusion.1) | data formatting | bytes 15728640
  (60 shorter events, 13.8 us)
Async XLA Ops:
  11.6 6.7 %copy-start = (s32[16,2]{0,1:T(2,128)S(1)}, s32[16,2]{0,1:T(2,128)}, u32[]{:S(2)}) copy-start(s32[16,2]{0,1:T(2,128)} %param.17) | copy-start | bytes 388
  11.6 6.9 %copy-start.9 = (s32[64]{0:T(128)S(1)}, s32[64]{0:T(128)}, u32[]{:S(2)}) copy-start(s32[64]{0:T(128)} %param.18) | copy-start | bytes 772
  11.6 7.8 %copy-start.8 = (s32[64]{0:T(128)S(1)}, s32[64]{0:T(128)}, u32[]{:S(2)}) copy-start(s32[64]{0:T(128)} %param.19) | copy-start | bytes 772
  11.6 76.6 %all-to-all-start = ((bf16[16,4,96,256]{3,2,1,0:T(8,128)(2,1)}), bf16[16,4,96,256]{3,2,1,0:T(8,128)(2,1)S(1)}, u32[]{:S(2)}, u32[]{:S(2)}) async-start(bf16[16,4,96,256]{3,2,1,0:T(8,128)(2,1)} %pad_maximum_fusion), calls=%async_computation | async-start | bytes 6291456 | tf_op jit(solution)/shard_map/all_to_all | solution.py:60
  20.2 2.8 %copy-start.1 = (bf16[4,256,1536]{2,1,0:T(8,128)(2,1)S(1)}, bf16[4,256,1536]{2,1,0:T(8,128)(2,1)}, u32[]{:S(2)}) copy-start(bf16[4,256,1536]{2,1,0:T(8,128)(2,1)} %param.12) | copy-start | bytes 9437188
  90.6 2.8 %copy-start.2 = (bf16[4,256,1536]{2,1,0:T(8,128)(2,1)S(1)}, bf16[4,256,1536]{2,1,0:T(8,128)(2,1)}, u32[]{:S(2)}) copy-start(bf16[4,256,1536]{2,1,0:T(8,128)(2,1)} %param.12) | copy-start | bytes 9437188
  90.6 2.8 %copy-start.7 = (f32[1536]{0:T(1024)S(1)}, f32[1536]{0:T(1024)}, u32[]{:S(2)}) copy-start(f32[1536]{0:T(1024)} %param.14) | copy-start | bytes 18436
  93.0 3.0 %copy-start.4 = (bf16[4,16,96,256]{3,2,1,0:T(8,128)(2,1)}, bf16[4,16,96,256]{3,2,1,0:T(8,128)(2,1)S(1)}, u32[]{:S(2)}) copy-start(bf16[4,16,96,256]{3,2,1,0:T(8,128)(2,1)S(1)} %broadcast_select_fusion) | copy-start | bytes 9437188
  100.4 2.8 %copy-start.5 = (bf16[4,256,1536]{2,1,0:T(8,128)(2,1)S(1)}, bf16[4,256,1536]{2,1,0:T(8,128)(2,1)}, u32[]{:S(2)}) copy-start(bf16[4,256,1536]{2,1,0:T(8,128)(2,1)} %param.13) | copy-start | bytes 9437188
  100.4 3.1 %copy-start.10 = (f32[4,256,256]{2,1,0:T(8,128)S(1)}, f32[4,256,256]{2,1,0:T(8,128)}, u32[]{:S(2)}) copy-start(f32[4,256,256]{2,1,0:T(8,128)} %get-tuple-element.27) | copy-start | bytes 3145732
  111.7 2.7 %copy-start.3 = (bf16[4,256,1536]{2,1,0:T(8,128)(2,1)S(1)}, bf16[4,256,1536]{2,1,0:T(8,128)(2,1)}, u32[]{:S(2)}) copy-start(bf16[4,256,1536]{2,1,0:T(8,128)(2,1)} %param.12) | copy-start | bytes 9437188
  125.3 74.9 %all-to-all-start.1 = ((bf16[16,4,96,256]{3,2,1,0:T(8,128)(2,1)}), bf16[16,4,96,256]{3,2,1,0:T(8,128)(2,1)}, u32[]{:S(2)}, u32[]{:S(2)}) async-start(bf16[16,4,96,256]{3,2,1,0:T(8,128)(2,1)} %copy.43), calls=%async_computation.1 | async-start | bytes 6291456 | tf_op jit(solution)/shard_map/all_to_all | solution.py:78
  130.5 4.4 %copy-start.6 = (bf16[4,256,1536]{2,1,0:T(8,128)(2,1)S(1)}, bf16[4,256,1536]{2,1,0:T(8,128)(2,1)}, u32[]{:S(2)}) copy-start(bf16[4,256,1536]{2,1,0:T(8,128)(2,1)} %param.13) | copy-start | bytes 9437188

commit v4 on v3

v4 whole, which is shorter than its diff:
```python
import functools

import jax
import jax.numpy as jnp
from jax import lax
from jax.experimental import pallas as pl
from jax.experimental.pallas import tpu as pltpu
from jax.sharding import PartitionSpec as P


def adapter_kernel(slot_ref, len_ref, frames_ref, cot_ref, gain_ref, wd_ref, wu_ref,
                   out_ref, gd_ref, gu_ref):
    u = pl.program_id(0)

    @pl.when(u == 0)
    def _():
        gd_ref[...] = jnp.zeros_like(gd_ref)
        gu_ref[...] = jnp.zeros_like(gu_ref)

    slot = slot_ref[u]
    length = len_ref[u]
    gain = gain_ref[...]
    values = frames_ref[0].astype(jnp.float32)
    centre_mean = jnp.mean(values, axis=1, keepdims=True)
    mean_removed = values - centre_mean
    variance = jnp.mean(mean_removed * mean_removed, axis=1, keepdims=True)
    reciprocal_deviation = lax.rsqrt(variance + 1e-06)
    standardized_input = mean_removed * reciprocal_deviation
    layer_normed = (standardized_input * gain).astype(jnp.bfloat16)
    w_down = wd_ref[0]
    w_up = wu_ref[0]
    pre_act = jnp.dot(layer_normed, w_down, preferred_element_type=jnp.float32)
    sigmoid_pre = 1.0 / (1.0 + jnp.exp(-pre_act))
    hidden = (pre_act * sigmoid_pre).astype(jnp.bfloat16)
    upstream = cot_ref[0]
    live = lax.broadcasted_iota(jnp.int32, (upstream.shape[0], 1), 0) < length
    masked_up = jnp.where(live, upstream, jnp.zeros_like(upstream))
    contract_rows = (((0,), (0,)), ((), ()))
    gu_ref[slot] += lax.dot_general(
        masked_up, hidden, contract_rows, preferred_element_type=jnp.float32
    )
    d_hidden = jnp.dot(masked_up, w_up, preferred_element_type=jnp.float32)
    d_pre = (d_hidden * sigmoid_pre * (1.0 + pre_act * (1.0 - sigmoid_pre))).astype(jnp.bfloat16)
    gd_ref[slot] += lax.dot_general(
        layer_normed, d_pre, contract_rows, preferred_element_type=jnp.float32
    )
    d_normed = lax.dot_general(
        d_pre, w_down, (((1,), (1,)), ((), ())), preferred_element_type=jnp.float32
    )
    scaled_rows = d_normed * gain
    inner_gradient = (
        scaled_rows
        - jnp.mean(scaled_rows, axis=1, keepdims=True)
        - standardized_input * jnp.mean(scaled_rows * standardized_input, axis=1, keepdims=True)
    ) * reciprocal_deviation
    out_ref[0] = (upstream.astype(jnp.float32) + inner_gradient).astype(out_ref.dtype)


def local_pass(frames, cotangent, gain, weights, own_slot, own_lengths, slots):
    utts, frame_count, width = frames.shape
    bottleneck = weights.shape[2]
    flops = 10 * utts * frame_count * width * bottleneck
    moved = 3 * frames.size * 2 + 2 * utts * width * bottleneck * 2 + 4 * slots * width * bottleneck * 4
    grid_spec = pltpu.PrefetchScalarGridSpec(
        num_scalar_prefetch=2,
        grid=(utts,),
        in_specs=[
            pl.BlockSpec((1, frame_count, width), lambda u, sl, ln: (u, 0, 0)),
            pl.BlockSpec((1, frame_count, width), lambda u, sl, ln: (u, 0, 0)),
            pl.BlockSpec((1, width), lambda u, sl, ln: (0, 0)),
            pl.BlockSpec((1, width, bottleneck), lambda u, sl, ln: (sl[u], 0, 0)),
            pl.BlockSpec((1, width, bottleneck), lambda u, sl, ln: (sl[u] + slots, 0, 0)),
        ],
        out_specs=[
            pl.BlockSpec((1, frame_count, width), lambda u, sl, ln: (u, 0, 0)),
            pl.BlockSpec((slots, width, bottleneck), lambda u, sl, ln: (0, 0, 0)),
            pl.BlockSpec((slots, width, bottleneck), lambda u, sl, ln: (0, 0, 0)),
        ],
    )
    return pl.pallas_call(
        adapter_kernel,
        grid_spec=grid_spec,
        out_shape=[
            jax.ShapeDtypeStruct(frames.shape, jnp.bfloat16),
            jax.ShapeDtypeStruct((slots, width, bottleneck), jnp.float32),
            jax.ShapeDtypeStruct((slots, width, bottleneck), jnp.float32),
        ],
        compiler_params=pltpu.CompilerParams(
            dimension_semantics=("arbitrary",), vmem_limit_bytes=60 * 1024 * 1024
        ),
        cost_estimate=pl.CostEstimate(flops=flops, bytes_accessed=moved, transcendentals=utts * frame_count * bottleneck),
    )(own_slot, own_lengths, frames, cotangent, gain.reshape(1, width), weights, weights)


def on_device(frames, cotangent, gain, down_weight, up_weight, slot_lang, utt_slot, lengths):
    devices = lax.axis_size("dp")
    self_index = lax.axis_index("dp")
    per_device = frames.shape[0]
    slots = slot_lang.shape[1]
    lang_count, row_count, bottleneck = down_weight.shape
    owners = jnp.arange(utt_slot.shape[0], dtype=jnp.int32) // per_device
    utt_lang = slot_lang[owners, utt_slot]
    own_lengths = lax.dynamic_slice_in_dim(lengths, self_index * per_device, per_device)
    own_slot = lax.dynamic_slice_in_dim(utt_slot, self_index * per_device, per_device)
    live_mask = (jnp.arange(frames.shape[1], dtype=jnp.int32)[None, :] < own_lengths[:, None])[
        :, :, None
    ]
    lang_ids = jnp.arange(lang_count, dtype=jnp.int32)
    counts = jnp.sum(jnp.where(utt_lang[None, :] == lang_ids[:, None], lengths[None, :], 0), axis=1)
    scaling = lax.rsqrt(jnp.maximum(counts, 1).astype(jnp.float32))
    member_langs = slot_lang.reshape(-1)
    send_down = jnp.take(down_weight, member_langs, axis=0).reshape(
        devices, slots, row_count, bottleneck
    )
    send_up = jnp.take(up_weight, member_langs, axis=0).reshape(
        devices, slots, row_count, bottleneck
    )
    sent = jnp.concatenate([send_down, send_up], axis=1)
    got = lax.all_to_all(sent, "dp", split_axis=0, concat_axis=0, tiled=True)

    weights = got.transpose(1, 0, 2, 3).reshape(2 * slots, devices * row_count, bottleneck)
    d_frames, grad_down, grad_up = local_pass(
        frames, cotangent, gain, weights, own_slot, own_lengths, slots
    )
    own_scale = jnp.take(scaling, lax.dynamic_index_in_dim(slot_lang, self_index, 0, False))
    own_scale = own_scale[:, None, None]
    lang_table = (lang_ids[:, None] == member_langs[None, :]).astype(jnp.bfloat16)

    def exchange_back(grad):
        scaled = (grad * own_scale).astype(jnp.bfloat16)
        scaled = scaled.reshape(slots, devices, row_count, bottleneck).transpose(1, 0, 2, 3)
        back = lax.all_to_all(scaled, "dp", split_axis=0, concat_axis=0, tiled=True)
        back = back.reshape(devices * slots, row_count, bottleneck)
        return jnp.einsum(
            "lm,mkr->lkr", lang_table, back, preferred_element_type=jnp.float32
        ).astype(jnp.bfloat16)

    down_grads = exchange_back(grad_down)
    up_grads = exchange_back(grad_up)
    return (d_frames, down_grads, up_grads)


def solution(mesh):
    placed = (
        P(("groups", "dp"), None, None),
        P(("groups", "dp"), None, None),
        P(),
        P("groups", "dp", None),
        P("groups", "dp", None),
        P("groups", None),
        P("groups"),
        P("groups"),
    )
    return jax.shard_map(
        on_device,
        mesh=mesh,
        in_specs=placed,
        out_specs=(
            P(("groups", "dp"), None, None),
            P("groups", "dp", None),
            P("groups", "dp", None),
        ),
        check_vma=False,
    )
```

time: 231 us -> 206 us (0.89)
  matrix products: 29 us -> 6.03 us
  Pallas kernels: 0 us -> 16.1 us
  local copies, waits for them, and re-layouts: 46.7 us -> 33.7 us
  other arithmetic: 17.1 us -> 7 us
  starting transfers between devices: 11.6 us -> 16.5 us
    dot_general x7 -> x2, matrix products: 29 us -> 6.03 us  [exchange_back(): jnp.einsum('lm,mkr->lkr', lang_table, back, preferred_element_type=jnp.fl...]
    pallas_call x0 -> x1, Pallas kernels: none -> 16.1 us  [local_pass(): pl.pallas_call(adapter_kernel, grid_spec=grid_spec, out_shape=[jax.ShapeD...]
    mul x2 -> x0, local copies, waits for them, and re-layouts: 5.3 us -> none  [the longest x1 2.72 us: on_device(): grad_up * own_scale]
    all_to_all x1 -> x2, starting transfers between devices: 4.91 us -> 9.82 us  [exchange_back(): back = lax.all_to_all(scaled, 'dp', split_axis=0, concat_axis=0, tiled=True)]
    gather x2 -> x0, local copies, waits for them, and re-layouts: 4.82 us -> none  [own_rows(): rows = jnp.take(got, own_slot + offset, axis=1)]
    select_n x3 -> x0, other arithmetic: 4.81 us -> none  [own_rows(): rows = jnp.take(got, own_slot + offset, axis=1)]
    reshape x0 -> x3, local copies, waits for them, and re-layouts: none -> 4.54 us  [the longest x2 3.95 us: exchange_back(): scaled.reshape(slots, devices, row_count, bottleneck).transpose(1, 0, 2, 3)]
    unnamed x25 -> x11, local copies, waits for them, and re-layouts: 20.6 us -> 16.4 us
  transfers between devices with their start and end apart: 2 -> 3, of which waited for: 2 -> 3; matrix products, arithmetic and copies ran while one was open for 6% -> 8% of each run, Pallas kernels for 0% -> 0%
where the time goes in v4:
time: 206 us
  waiting for transfers between devices  126 us (61%)
  local copies, waits for them, and re-layouts  33.7 us (16%)
  starting transfers between devices  16.5 us (8%)
  Pallas kernels  16.1 us (8%)
  other arithmetic  7 us (3%)
  matrix products  6.03 us (3%)
    all_to_all x1, waiting for transfers between devices, on_device(): got = lax.all_to_all(sent, 'dp', split_axis=0, concat_axis=0, tiled=True)  66.2 us
    all_to_all x2, waiting for transfers between devices, exchange_back(): back = lax.all_to_all(scaled, 'dp', split_axis=0, concat_axis=0, tiled=True)  59.6 us
    unnamed x11, local copies, waits for them, and re-layouts  16.4 us
    pallas_call x1, Pallas kernels, local_pass(): pl.pallas_call(adapter_kernel, grid_spec=grid_spec, out_shape=[jax.ShapeD...  16.1 us
    all_to_all x2, starting transfers between devices, exchange_back(): back = lax.all_to_all(scaled, 'dp', split_axis=0, concat_axis=0, tiled=True)  9.82 us
    all_to_all x1, starting transfers between devices, on_device(): got = lax.all_to_all(sent, 'dp', split_axis=0, concat_axis=0, tiled=True)  6.7 us
    dot_general x2, matrix products, exchange_back(): jnp.einsum('lm,mkr->lkr', lang_table, back, preferred_element_type=jnp.fl...  6.03 us
    convert_element_type x1, other arithmetic, exchange_back(): scaled = (grad * own_scale).astype(jnp.bfloat16)  4.57 us
  transfers between devices with their start and end apart: 3, of which 3 were waited for; matrix products, arithmetic and copies ran while one was open for 8% of the time, Pallas kernels for 0%

profile of v4, /device:TPU:15, one launch (start us, length us, event | category | flops | bytes accessed | tf_op | source)
XLA Modules:
  0.0 205.9 jit_solution(8626325140602269573)
XLA Ops:
  0.6 0.8 copy.33
  1.5 3.9 %gather_fusion.3 = bf16[32,96,256]{2,1,0:T(8,128)(2,1)S(1)} fusion(bf16[160,96,256]{2,1,0:T(8,128)(2,1)} %param.14, s32[1024]{0:T(1024)S(1)} %pad_clamp_fusion.1), kind=kCustom, calls=%fused_computation.1.clone | custom fusion | bytes 3145856 | tf_op jit(solution)/shard_map/jit(_take)/gather | solution.py:115
  5.4 3.9 %gather_fusion.2 = bf16[32,96,256]{2,1,0:T(8,128)(2,1)S(1)} fusion(bf16[160,96,256]{2,1,0:T(8,128)(2,1)} %param.13, s32[1024]{0:T(1024)S(1)} %pad_clamp_fusion.1), kind=kCustom, calls=%fused_computation.clone | custom fusion | bytes 3145856 | tf_op jit(solution)/shard_map/jit(_take)/gather | solution.py:112
  9.6 1.9 pad_maximum_fusion
  11.6 6.7 %all-to-all-start = ((bf16[16,4,96,256]{3,2,1,0:T(8,128)(2,1)}), bf16[16,4,96,256]{3,2,1,0:T(8,128)(2,1)S(1)}, u32[]{:S(2)}, u32[]{:S(2)}) async-start(bf16[16,4,96,256]{3,2,1,0:T(8,128)(2,1)} %pad_maximum_fusion), calls=%async_computation | async-start | bytes 6291456 | tf_op jit(solution)/shard_map/all_to_all | solution.py:119
  18.5 0.9 gather_fusion
  19.4 0.6 dynamic_slice.10.slot_ref
  20.0 0.6 dynamic_slice.11.len_ref
  20.6 0.6 reshape.137.gain_ref
  21.4 0.6 gather_fusion.1
  22.0 66.2 %all-to-all-done = bf16[16,4,96,256]{3,2,1,0:T(8,128)(2,1)S(1)} async-done(((bf16[16,4,96,256]{3,2,1,0:T(8,128)(2,1)}), bf16[16,4,96,256]{3,2,1,0:T(8,128)(2,1)S(1)}, u32[]{:S(2)}, u32[]{:S(2)}) %all-to-all-start) | async-done | bytes 3145760 | tf_op jit(solution)/shard_map/all_to_all | solution.py:119
  88.2 1.9 copy.34
  90.1 16.1 %shard_map.103 = (bf16[4,256,1536]{2,1,0:T(8,128)(2,1)}, f32[2,1536,256]{2,1,0:T(8,128)}, f32[2,1536,256]{2,1,0:T(8,128)}) custom-call(s32[4]{0:T(128)} %dynamic_slice.10.slot_ref, s32[4]{0:T(128)} %dynamic_slice.11.len_ref, bf16[4,256,1536]{2,1,0:T(8,128)(2,1)} %frames_ref.1, bf16[4,256,1536]{2,1,0:T(8,128)(2,1)} %cot_ref.1, f32[1,1536]{1,0:T(1,128)} %reshape.137.gain_ref, ...), custom_call_target="tpu_custom_call" | custom-call | flops 4026531840 | bytes 28311552 | tf_op jit(solution)/shard_map/pallas_call | solution.py:80
  106.2 4.6 %multiply_convert_fusion = (bf16[2,1536,256]{2,1,0:T(8,128)(2,1)S(1)}, bf16[2,1536,256]{2,1,0:T(8,128)(2,1)}) fusion(f32[2,1536,256]{2,1,0:T(8,128)} %get-tuple-element.9, f32[2]{0:T(128)S(1)} %and_select_fusion.1, f32[2,1536,256]{2,1,0:T(8,128)} %get-tuple-element.8), kind=kLoop, calls=%fused_computation.7 | loop fusion | flops 3145728 | bytes 9437192 | tf_op jit(solution)/shard_map/convert_element_type | solution.py:130
  110.8 1.3 copy.49
  112.1 4.9 %all-to-all-start.2 = ((bf16[16,2,96,256]{3,2,1,0:T(8,128)(2,1)}), bf16[16,2,96,256]{3,2,1,0:T(8,128)(2,1)S(1)}, u32[]{:S(2)}, u32[]{:S(2)}) async-start(bf16[16,2,96,256]{3,2,1,0:T(8,128)(2,1)} %bitcast.32), calls=%async_computation.2 | async-start | bytes 3145728 | tf_op jit(solution)/shard_map/all_to_all | solution.py:132
  117.0 2.7 %copy.50 = bf16[2,16,96,256]{3,2,0,1:T(8,128)(2,1)} copy(bf16[2,16,96,256]{3,2,1,0:T(8,128)(2,1)} %bitcast.31) | data formatting | bytes 3145728 | tf_op jit(solution)/shard_map/reshape | solution.py:131
  119.7 33.5 %all-to-all-done.2 = bf16[16,2,96,256]{3,2,1,0:T(8,128)(2,1)S(1)} async-done(((bf16[16,2,96,256]{3,2,1,0:T(8,128)(2,1)}), bf16[16,2,96,256]{3,2,1,0:T(8,128)(2,1)S(1)}, u32[]{:S(2)}, u32[]{:S(2)}) %all-to-all-start.2) | async-done | bytes 1572896 | tf_op jit(solution)/shard_map/all_to_all | solution.py:132
  153.2 4.9 %all-to-all-start.1 = ((bf16[16,2,96,256]{3,2,1,0:T(8,128)(2,1)}), bf16[16,2,96,256]{3,2,1,0:T(8,128)(2,1)}, u32[]{:S(2)}, u32[]{:S(2)}) async-start(bf16[16,2,96,256]{3,2,1,0:T(8,128)(2,1)} %bitcast.30), calls=%async_computation.1 | async-start | bytes 3145728 | tf_op jit(solution)/shard_map/all_to_all | solution.py:132
  158.1 2.3 %convolution_convert_fusion = bf16[160,96,256]{2,0,1:T(8,128)(2,1)S(1)} fusion(bf16[32,96,256]{2,1,0:T(8,128)(2,1)S(1)} %bitcast.29, s32[32]{0:T(128)S(1)} %reshape.138), kind=kOutput, calls=%fused_computation.4 | convolution fusion | flops 255595520 | bytes 9437312 | tf_op jit(solution)/shard_map/lm,mkr->lkr/dot_general | solution.py:134
  160.4 7.8 %copy.40 = bf16[160,96,256]{2,1,0:T(8,128)(2,1)} copy(bf16[160,96,256]{2,0,1:T(8,128)(2,1)S(1)} %convolution_convert_fusion) | data formatting | bytes 15728640
  168.2 26.1 %all-to-all-done.1 = bf16[16,2,96,256]{3,2,1,0:T(8,128)(2,1)} async-done(((bf16[16,2,96,256]{3,2,1,0:T(8,128)(2,1)}), bf16[16,2,96,256]{3,2,1,0:T(8,128)(2,1)}, u32[]{:S(2)}, u32[]{:S(2)}) %all-to-all-start.1) | async-done | bytes 1572896 | tf_op jit(solution)/shard_map/all_to_all | solution.py:132
  194.4 3.7 %convolution_convert_fusion.1 = bf16[160,96,256]{2,0,1:T(8,128)(2,1)S(1)} fusion(bf16[32,96,256]{2,1,0:T(8,128)(2,1)} %bitcast.10, s32[32]{0:T(128)S(1)} %reshape.138), kind=kOutput, calls=%fused_computation.5 | convolution fusion | flops 255595520 | bytes 9437312 | tf_op jit(solution)/shard_map/lm,mkr->lkr/dot_general | solution.py:134
  198.1 7.8 %copy.39 = bf16[160,96,256]{2,1,0:T(8,128)(2,1)} copy(bf16[160,96,256]{2,0,1:T(8,128)(2,1)S(1)} %convolution_convert_fusion.1) | data formatting | bytes 15728640
  (20 shorter events, 0.8 us)
Async XLA Ops:
  11.6 6.7 %copy-start = (s32[16,2]{0,1:T(2,128)S(1)}, s32[16,2]{0,1:T(2,128)}, u32[]{:S(2)}) copy-start(s32[16,2]{0,1:T(2,128)} %param.15) | copy-start | bytes 388
  11.6 6.9 %copy-start.3 = (s32[64]{0:T(128)S(1)}, s32[64]{0:T(128)}, u32[]{:S(2)}) copy-start(s32[64]{0:T(128)} %param.16) | copy-start | bytes 772
  11.6 8.4 %copy-start.2 = (s32[64]{0:T(128)S(1)}, s32[64]{0:T(128)}, u32[]{:S(2)}) copy-start(s32[64]{0:T(128)} %param.17) | copy-start | bytes 772
  11.6 9.0 %copy-start.1 = (f32[1536]{0:T(1024)S(1)}, f32[1536]{0:T(1024)}, u32[]{:S(2)}) copy-start(f32[1536]{0:T(1024)} %param.12) | copy-start | bytes 18436
  11.6 76.6 %all-to-all-start = ((bf16[16,4,96,256]{3,2,1,0:T(8,128)(2,1)}), bf16[16,4,96,256]{3,2,1,0:T(8,128)(2,1)S(1)}, u32[]{:S(2)}, u32[]{:S(2)}) async-start(bf16[16,4,96,256]{3,2,1,0:T(8,128)(2,1)} %pad_maximum_fusion), calls=%async_computation | async-start | bytes 6291456 | tf_op jit(solution)/shard_map/all_to_all | solution.py:119
  112.1 41.1 %all-to-all-start.2 = ((bf16[16,2,96,256]{3,2,1,0:T(8,128)(2,1)}), bf16[16,2,96,256]{3,2,1,0:T(8,128)(2,1)S(1)}, u32[]{:S(2)}, u32[]{:S(2)}) async-start(bf16[16,2,96,256]{3,2,1,0:T(8,128)(2,1)} %bitcast.32), calls=%async_computation.2 | async-start | bytes 3145728 | tf_op jit(solution)/shard_map/all_to_all | solution.py:132
  153.2 41.2 %all-to-all-start.1 = ((bf16[16,2,96,256]{3,2,1,0:T(8,128)(2,1)}), bf16[16,2,96,256]{3,2,1,0:T(8,128)(2,1)}, u32[]{:S(2)}, u32[]{:S(2)}) async-start(bf16[16,2,96,256]{3,2,1,0:T(8,128)(2,1)} %bitcast.30), calls=%async_computation.1 | async-start | bytes 3145728 | tf_op jit(solution)/shard_map/all_to_all | solution.py:132

commit v5 on v4

--- a/solution.py
+++ b/solution.py
@@ -8,8 +8,8 @@
 from jax.sharding import PartitionSpec as P
 
 
-def adapter_kernel(slot_ref, len_ref, frames_ref, cot_ref, gain_ref, wd_ref, wu_ref,
-                   out_ref, gd_ref, gu_ref):
+def adapter_kernel(slot_ref, len_ref, frames_ref, cot_ref, gain_ref, wd_ref, wu_ref, scale_ref,
+                   out_ref, gd_out, gu_out, gd_ref, gu_ref):
     u = pl.program_id(0)
 
     @pl.when(u == 0)
@@ -55,8 +55,53 @@
     ) * reciprocal_deviation
     out_ref[0] = (upstream.astype(jnp.float32) + inner_gradient).astype(out_ref.dtype)
 
-
-def local_pass(frames, cotangent, gain, weights, own_slot, own_lengths, slots):
+    @pl.when(u == pl.num_programs(0) - 1)
+    def _():
+        gd_out[...] = (gd_ref[...] * scale_ref[...]).astype(gd_out.dtype)
+        gu_out[...] = (gu_ref[...] * scale_ref[...]).astype(gu_out.dtype)
+
+
+def combine_kernel(lang_ref, back_ref, out_ref, acc_ref):
+    block = out_ref.shape[0]
+    base = pl.program_id(0) * block
+    acc_ref[...] = jnp.zeros_like(acc_ref)
+
+    def add_member(m, carry):
+        local = lang_ref[m] - base
+
+        @pl.when((local >= 0) & (local < block))
+        def _():
+            acc_ref[local] += back_ref[m].astype(jnp.float32)
+
+        return carry
+
+    lax.fori_loop(0, back_ref.shape[0], add_member, 0)
+    out_ref[...] = acc_ref[...].astype(out_ref.dtype)
+
+
+def combine(member_langs, back, lang_count):
+    members, row_count, bottleneck = back.shape
+    block = 16 if lang_count % 16 == 0 else (8 if lang_count % 8 == 0 else 1)
+    grid_spec = pltpu.PrefetchScalarGridSpec(
+        num_scalar_prefetch=1,
+        grid=(lang_count // block,),
+        in_specs=[pl.BlockSpec((members, row_count, bottleneck), lambda b, ml: (0, 0, 0))],
+        out_specs=pl.BlockSpec((block, row_count, bottleneck), lambda b, ml: (b, 0, 0)),
+        scratch_shapes=[pltpu.VMEM((block, row_count, bottleneck), jnp.float32)],
+    )
+    return pl.pallas_call(
+        combine_kernel,
+        grid_spec=grid_spec,
+        out_shape=jax.ShapeDtypeStruct((lang_count, row_count, bottleneck), jnp.bfloat16),
+        compiler_params=pltpu.CompilerParams(dimension_semantics=("arbitrary",)),
+        cost_estimate=pl.CostEstimate(
+            flops=back.size, bytes_accessed=back.size * 2 + lang_count * row_count * bottleneck * 2,
+            transcendentals=0,
+        ),
+    )(member_langs, back)
+
+
+def local_pass(frames, cotangent, gain, weights, own_slot, own_lengths, slots, own_scale):
     utts, frame_count, width = frames.shape
     bottleneck = weights.shape[2]
     flops = 10 * utts * frame_count * width * bottleneck
@@ -70,11 +115,16 @@
             pl.BlockSpec((1, width), lambda u, sl, ln: (0, 0)),
             pl.BlockSpec((1, width, bottleneck), lambda u, sl, ln: (sl[u], 0, 0)),
             pl.BlockSpec((1, width, bottleneck), lambda u, sl, ln: (sl[u] + slots, 0, 0)),
+            pl.BlockSpec((slots, 1, 1), lambda u, sl, ln: (0, 0, 0)),
         ],
         out_specs=[
             pl.BlockSpec((1, frame_count, width), lambda u, sl, ln: (u, 0, 0)),
             pl.BlockSpec((slots, width, bottleneck), lambda u, sl, ln: (0, 0, 0)),
             pl.BlockSpec((slots, width, bottleneck), lambda u, sl, ln: (0, 0, 0)),
+        ],
+        scratch_shapes=[
+            pltpu.VMEM((slots, width, bottleneck), jnp.float32),
+            pltpu.VMEM((slots, width, bottleneck), jnp.float32),
         ],
     )
     return pl.pallas_call(
@@ -82,14 +132,16 @@
         grid_spec=grid_spec,
         out_shape=[
             jax.ShapeDtypeStruct(frames.shape, jnp.bfloat16),
-            jax.ShapeDtypeStruct((slots, width, bottleneck), jnp.float32),
-            jax.ShapeDtypeStruct((slots, width, bottleneck), jnp.float32),
-        ],
+            jax.ShapeDtypeStruct((slots, width, bottleneck), jnp.bfloat16),
+            jax.ShapeDtypeStruct((slots, width, bottleneck), jnp.bfloat16),
+        ],
+
         compiler_params=pltpu.CompilerParams(
             dimension_semantics=("arbitrary",), vmem_limit_bytes=60 * 1024 * 1024
         ),
         cost_estimate=pl.CostEstimate(flops=flops, bytes_accessed=moved, transcendentals=utts * frame_count * bottleneck),
-    )(own_slot, own_lengths, frames, cotangent, gain.reshape(1, width), weights, weights)
+    )(own_slot, own_lengths, frames, cotangent, gain.reshape(1, width), weights, weights,
+      own_scale.reshape(slots, 1, 1))
 
 
 def on_device(frames, cotangent, gain, down_weight, up_weight, slot_lang, utt_slot, lengths):
@@ -102,9 +154,6 @@
     utt_lang = slot_lang[owners, utt_slot]
     own_lengths = lax.dynamic_slice_in_dim(lengths, self_index * per_device, per_device)
     own_slot = lax.dynamic_slice_in_dim(utt_slot, self_index * per_device, per_device)
-    live_mask = (jnp.arange(frames.shape[1], dtype=jnp.int32)[None, :] < own_lengths[:, None])[
-        :, :, None
-    ]
     lang_ids = jnp.arange(lang_count, dtype=jnp.int32)
     counts = jnp.sum(jnp.where(utt_lang[None, :] == lang_ids[:, None], lengths[None, :], 0), axis=1)
     scaling = lax.rsqrt(jnp.maximum(counts, 1).astype(jnp.float32))
@@ -119,21 +168,15 @@
     got = lax.all_to_all(sent, "dp", split_axis=0, concat_axis=0, tiled=True)
 
     weights = got.transpose(1, 0, 2, 3).reshape(2 * slots, devices * row_count, bottleneck)
+    own_scale = jnp.take(scaling, lax.dynamic_index_in_dim(slot_lang, self_index, 0, False))
     d_frames, grad_down, grad_up = local_pass(
-        frames, cotangent, gain, weights, own_slot, own_lengths, slots
-    )
-    own_scale = jnp.take(scaling, lax.dynamic_index_in_dim(slot_lang, self_index, 0, False))
-    own_scale = own_scale[:, None, None]
-    lang_table = (lang_ids[:, None] == member_langs[None, :]).astype(jnp.bfloat16)
+        frames, cotangent, gain, weights, own_slot, own_lengths, slots, own_scale
+    )
 
     def exchange_back(grad):
-        scaled = (grad * own_scale).astype(jnp.bfloat16)
-        scaled = scaled.reshape(slots, devices, row_count, bottleneck).transpose(1, 0, 2, 3)
+        scaled = grad.reshape(slots, devices, row_count, bottleneck).transpose(1, 0, 2, 3)
         back = lax.all_to_all(scaled, "dp", split_axis=0, concat_axis=0, tiled=True)
-        back = back.reshape(devices * slots, row_count, bottleneck)
-        return jnp.einsum(
-            "lm,mkr->lkr", lang_table, back, preferred_element_type=jnp.float32
-        ).astype(jnp.bfloat16)
+        return combine(member_langs, back.reshape(devices * slots, row_count, bottleneck), lang_count)
 
     down_grads = exchange_back(grad_down)
     up_grads = exchange_back(grad_up)

time: 206 us -> 205 us (level)
  Pallas kernels: 16.1 us -> 37.5 us
  local copies, waits for them, and re-layouts: 33.7 us -> 20.4 us
  matrix products: 6.03 us -> 0 us
  other arithmetic: 7 us -> 2.98 us
    pallas_call x0 -> x2, Pallas kernels: none -> 21.3 us  [combine(): pl.pallas_call(combine_kernel, grid_spec=grid_spec, out_shape=jax.ShapeDt...]
    unnamed x11 -> x17, local copies, waits for them, and re-layouts: 16.4 us -> 3.08 us
    dot_general x2 -> x0, matrix products: 6.03 us -> none  [exchange_back(): jnp.einsum('lm,mkr->lkr', lang_table, back, preferred_element_type=jnp.fl...]
    convert_element_type x1 -> x0, other arithmetic: 4.57 us -> none  [exchange_back(): scaled = (grad * own_scale).astype(jnp.bfloat16)]
  transfers between devices with their start and end apart: 3 -> 3, of which waited for: 3 -> 3; matrix products, arithmetic and copies ran while one was open for 8% -> 3% of each run, Pallas kernels for 0% -> 5%
where the time goes in v5:
time: 205 us; the launch traced here: 204 us
  waiting for transfers between devices  126 us (61%)
  Pallas kernels  37.5 us (18%)
  local copies, waits for them, and re-layouts  20.4 us (10%)
  starting transfers between devices  16.7 us (8%)
  other arithmetic  2.98 us (1%)
    all_to_all x1, waiting for transfers between devices, on_device(): got = lax.all_to_all(sent, 'dp', split_axis=0, concat_axis=0, tiled=True)  65.6 us
    all_to_all x2, waiting for transfers between devices, exchange_back(): back = lax.all_to_all(scaled, 'dp', split_axis=0, concat_axis=0, tiled=True)  60.4 us
    pallas_call x2, Pallas kernels, combine(): pl.pallas_call(combine_kernel, grid_spec=grid_spec, out_shape=jax.ShapeDt...  21.3 us
    pallas_call x1, Pallas kernels, local_pass(): pl.pallas_call(adapter_kernel, grid_spec=grid_spec, out_shape=[jax.ShapeD...  16.1 us
    all_to_all x2, starting transfers between devices, exchange_back(): back = lax.all_to_all(scaled, 'dp', split_axis=0, concat_axis=0, tiled=True)  9.95 us
    all_to_all x1, starting transfers between devices, on_device(): got = lax.all_to_all(sent, 'dp', split_axis=0, concat_axis=0, tiled=True)  6.7 us
  transfers between devices with their start and end apart: 3, of which 3 were waited for; matrix products, arithmetic and copies ran while one was open for 3% of the time, Pallas kernels for 5%

profile of v5, /device:TPU:15, one launch (start us, length us, event | category | flops | bytes accessed | tf_op | source)
XLA Modules:
  0.0 204.2 jit_solution(2553886365421262296)
XLA Ops:
  0.6 0.8 copy.37
  1.5 3.9 %gather_fusion.3 = bf16[32,96,256]{2,1,0:T(8,128)(2,1)S(1)} fusion(bf16[160,96,256]{2,1,0:T(8,128)(2,1)} %param.14, s32[1024]{0:T(1024)S(1)} %pad_clamp_fusion.1), kind=kCustom, calls=%fused_computation.1.clone | custom fusion | bytes 3145856 | tf_op jit(solution)/shard_map/jit(_take)/gather | solution.py:164
  5.4 3.9 %gather_fusion.2 = bf16[32,96,256]{2,1,0:T(8,128)(2,1)S(1)} fusion(bf16[160,96,256]{2,1,0:T(8,128)(2,1)} %param.13, s32[1024]{0:T(1024)S(1)} %pad_clamp_fusion.1), kind=kCustom, calls=%fused_computation.clone | custom fusion | bytes 3145856 | tf_op jit(solution)/shard_map/jit(_take)/gather | solution.py:161
  9.7 1.9 pad_maximum_fusion
  11.6 6.7 %all-to-all-start = ((bf16[16,4,96,256]{3,2,1,0:T(8,128)(2,1)}), bf16[16,4,96,256]{3,2,1,0:T(8,128)(2,1)S(1)}, u32[]{:S(2)}, u32[]{:S(2)}) async-start(bf16[16,4,96,256]{3,2,1,0:T(8,128)(2,1)} %pad_maximum_fusion), calls=%async_computation | async-start | bytes 6291456 | tf_op jit(solution)/shard_map/all_to_all | solution.py:168
  18.3 0.9 gather_fusion
  19.2 0.6 dynamic_slice.10.slot_ref
  19.8 0.6 dynamic_slice.11.len_ref
  20.7 0.6 gather_fusion.1
  21.5 0.6 reshape.162.gain_ref
  22.1 0.5 and_select_fusion.scale_ref
  22.6 65.6 %all-to-all-done = bf16[16,4,96,256]{3,2,1,0:T(8,128)(2,1)S(1)} async-done(((bf16[16,4,96,256]{3,2,1,0:T(8,128)(2,1)}), bf16[16,4,96,256]{3,2,1,0:T(8,128)(2,1)S(1)}, u32[]{:S(2)}, u32[]{:S(2)}) %all-to-all-start) | async-done | bytes 3145760 | tf_op jit(solution)/shard_map/all_to_all | solution.py:168
  88.2 1.9 copy.38
  90.1 16.1 %shard_map.103 = (bf16[4,256,1536]{2,1,0:T(8,128)(2,1)}, bf16[2,1536,256]{2,1,0:T(8,128)(2,1)}, bf16[2,1536,256]{2,1,0:T(8,128)(2,1)}) custom-call(s32[4]{0:T(128)} %dynamic_slice.10.slot_ref, s32[4]{0:T(128)} %dynamic_slice.11.len_ref, bf16[4,256,1536]{2,1,0:T(8,128)(2,1)} %frames_ref.1, bf16[4,256,1536]{2,1,0:T(8,128)(2,1)} %cot_ref.1, ...), custom_call_target="tpu_custom_call" | custom-call | flops 4026531840 | bytes 28311552 | tf_op jit(solution)/shard_map/pallas_call | solution.py:130
  106.3 2.7 %copy.47 = bf16[2,16,96,256]{3,2,0,1:T(8,128)(2,1)} copy(bf16[2,16,96,256]{3,2,1,0:T(8,128)(2,1)} %bitcast.34) | data formatting | bytes 3145728 | tf_op jit(solution)/shard_map/reshape | solution.py:177
  108.9 5.0 %all-to-all-start.2 = ((bf16[16,2,96,256]{3,2,1,0:T(8,128)(2,1)}), bf16[16,2,96,256]{3,2,1,0:T(8,128)(2,1)S(1)}, u32[]{:S(2)}, u32[]{:S(2)}) async-start(bf16[16,2,96,256]{3,2,1,0:T(8,128)(2,1)} %bitcast.24), calls=%async_computation.2 | async-start | bytes 3145728 | tf_op jit(solution)/shard_map/all_to_all | solution.py:178
  114.0 1.3 copy.48
  115.3 34.9 %all-to-all-done.2 = bf16[16,2,96,256]{3,2,1,0:T(8,128)(2,1)S(1)} async-done(((bf16[16,2,96,256]{3,2,1,0:T(8,128)(2,1)}), bf16[16,2,96,256]{3,2,1,0:T(8,128)(2,1)S(1)}, u32[]{:S(2)}, u32[]{:S(2)}) %all-to-all-start.2) | async-done | bytes 1572896 | tf_op jit(solution)/shard_map/all_to_all | solution.py:178
  150.2 1.2 copy-done.1
  151.3 4.9 %all-to-all-start.1 = ((bf16[16,2,96,256]{3,2,1,0:T(8,128)(2,1)}), bf16[16,2,96,256]{3,2,1,0:T(8,128)(2,1)S(1)}, u32[]{:S(2)}, u32[]{:S(2)}) async-start(bf16[16,2,96,256]{3,2,1,0:T(8,128)(2,1)} %bitcast.25), calls=%async_computation.1 | async-start | bytes 3145728 | tf_op jit(solution)/shard_map/all_to_all | solution.py:178
  156.2 10.7 %shard_map.105 = bf16[160,96,256]{2,1,0:T(8,128)(2,1)} custom-call(s32[32]{0:T(128)} %copy-done.5, bf16[32,96,256]{2,1,0:T(8,128)(2,1)} %bitcast.27), custom_call_target="tpu_custom_call" | custom-call | flops 786432 | bytes 9437184 | tf_op jit(solution)/shard_map/pallas_call | solution.py:92
  166.9 25.5 %all-to-all-done.1 = bf16[16,2,96,256]{3,2,1,0:T(8,128)(2,1)S(1)} async-done(((bf16[16,2,96,256]{3,2,1,0:T(8,128)(2,1)}), bf16[16,2,96,256]{3,2,1,0:T(8,128)(2,1)S(1)}, u32[]{:S(2)}, u32[]{:S(2)}) %all-to-all-start.1) | async-done | bytes 1572896 | tf_op jit(solution)/shard_map/all_to_all | solution.py:178
  192.4 1.2 copy-done.2
  193.6 10.7 %shard_map.104 = bf16[160,96,256]{2,1,0:T(8,128)(2,1)} custom-call(s32[32]{0:T(128)} %copy-done.5, bf16[32,96,256]{2,1,0:T(8,128)(2,1)} %bitcast.28), custom_call_target="tpu_custom_call" | custom-call | flops 786432 | bytes 9437184 | tf_op jit(solution)/shard_map/pallas_call | solution.py:92
  (26 shorter events, 0.9 us)
Async XLA Ops:
  1.5 3.9 %copy-start.5 = (s32[32]{0:T(128)}, s32[32]{0:T(128)S(1)}, u32[]{:S(2)}) copy-start(s32[32]{0:T(128)S(1)} %reshape.163.lang_ref) | copy-start | bytes 388
  11.6 6.7 %copy-start.7 = (s32[64]{0:T(128)S(1)}, s32[64]{0:T(128)}, u32[]{:S(2)}) copy-start(s32[64]{0:T(128)} %param.16) | copy-start | bytes 772
  11.6 6.7 %copy-start = (s32[16,2]{0,1:T(2,128)S(1)}, s32[16,2]{0,1:T(2,128)}, u32[]{:S(2)}) copy-start(s32[16,2]{0,1:T(2,128)} %param.15) | copy-start | bytes 388
  11.6 8.2 %copy-start.6 = (s32[64]{0:T(128)S(1)}, s32[64]{0:T(128)}, u32[]{:S(2)}) copy-start(s32[64]{0:T(128)} %param.17) | copy-start | bytes 772
  11.6 9.9 %copy-start.4 = (f32[1536]{0:T(1024)S(1)}, f32[1536]{0:T(1024)}, u32[]{:S(2)}) copy-start(f32[1536]{0:T(1024)} %param.12) | copy-start | bytes 18436
  11.6 76.6 %all-to-all-start = ((bf16[16,4,96,256]{3,2,1,0:T(8,128)(2,1)}), bf16[16,4,96,256]{3,2,1,0:T(8,128)(2,1)S(1)}, u32[]{:S(2)}, u32[]{:S(2)}) async-start(bf16[16,4,96,256]{3,2,1,0:T(8,128)(2,1)} %pad_maximum_fusion), calls=%async_computation | async-start | bytes 6291456 | tf_op jit(solution)/shard_map/all_to_all | solution.py:168
  108.9 5.0 %copy-start.3 = (bf16[2,1536,256]{2,1,0:T(8,128)(2,1)S(1)}, bf16[2,1536,256]{2,1,0:T(8,128)(2,1)}, u32[]{:S(2)}) copy-start(bf16[2,1536,256]{2,1,0:T(8,128)(2,1)} %get-tuple-element.8) | copy-start | bytes 4718596
  108.9 41.2 %all-to-all-start.2 = ((bf16[16,2,96,256]{3,2,1,0:T(8,128)(2,1)}), bf16[16,2,96,256]{3,2,1,0:T(8,128)(2,1)S(1)}, u32[]{:S(2)}, u32[]{:S(2)}) async-start(bf16[16,2,96,256]{3,2,1,0:T(8,128)(2,1)} %bitcast.24), calls=%async_computation.2 | async-start | bytes 3145728 | tf_op jit(solution)/shard_map/all_to_all | solution.py:178
  150.2 1.2 copy-start.1
  151.3 41.1 %all-to-all-start.1 = ((bf16[16,2,96,256]{3,2,1,0:T(8,128)(2,1)}), bf16[16,2,96,256]{3,2,1,0:T(8,128)(2,1)S(1)}, u32[]{:S(2)}, u32[]{:S(2)}) async-start(bf16[16,2,96,256]{3,2,1,0:T(8,128)(2,1)} %bitcast.25), calls=%async_computation.1 | async-start | bytes 3145728 | tf_op jit(solution)/shard_map/all_to_all | solution.py:178
  192.4 1.2 copy-start.2

commit v6 on v5

--- a/solution.py
+++ b/solution.py
@@ -9,7 +9,7 @@
 
 
 def adapter_kernel(slot_ref, len_ref, frames_ref, cot_ref, gain_ref, wd_ref, wu_ref, scale_ref,
-                   out_ref, gd_out, gu_out, gd_ref, gu_ref):
+                   out_ref, grads_out, gd_ref, gu_ref):
     u = pl.program_id(0)
 
     @pl.when(u == 0)
@@ -57,48 +57,91 @@
 
     @pl.when(u == pl.num_programs(0) - 1)
     def _():
-        gd_out[...] = (gd_ref[...] * scale_ref[...]).astype(gd_out.dtype)
-        gu_out[...] = (gu_ref[...] * scale_ref[...]).astype(gu_out.dtype)
-
-
-def combine_kernel(lang_ref, back_ref, out_ref, acc_ref):
-    block = out_ref.shape[0]
-    base = pl.program_id(0) * block
-    acc_ref[...] = jnp.zeros_like(acc_ref)
-
-    def add_member(m, carry):
-        local = lang_ref[m] - base
-
-        @pl.when((local >= 0) & (local < block))
+        slots = gd_ref.shape[0]
+        grads_out[pl.ds(0, slots)] = (gd_ref[...] * scale_ref[...]).astype(grads_out.dtype)
+        grads_out[pl.ds(slots, slots)] = (gu_ref[...] * scale_ref[...]).astype(grads_out.dtype)
+
+
+def combine_kernel(order_ref, lang_ref, start_ref, back_ref, down_ref, up_ref, acc_d, acc_u,
+                   *, slots):
+    block = down_ref.shape[0]
+    b = pl.program_id(0)
+    base = b * block
+    down_ref[...] = jnp.zeros_like(down_ref)
+    up_ref[...] = jnp.zeros_like(up_ref)
+    first_at = start_ref[b]
+    end_at = start_ref[b + 1]
+    last_member = lang_ref.shape[0] - 1
+
+    def add_member(i, carry):
+        m = order_ref[i]
+        lang = lang_ref[i]
+        first = (i == first_at) | (lang_ref[jnp.maximum(i - 1, 0)] != lang)
+        last = (i == end_at - 1) | (lang_ref[jnp.minimum(i + 1, last_member)] != lang)
+        val_d = back_ref[m].astype(jnp.float32)
+        val_u = back_ref[m + slots].astype(jnp.float32)
+
+        @pl.when(first)
         def _():
-            acc_ref[local] += back_ref[m].astype(jnp.float32)
+            acc_d[...] = val_d
+            acc_u[...] = val_u
+
+        @pl.when(jnp.logical_not(first))
+        def _():
+            acc_d[...] += val_d
+            acc_u[...] += val_u
+
+        @pl.when(last)
+        def _():
+            down_ref[lang - base] = acc_d[...].astype(down_ref.dtype)
+            up_ref[lang - base] = acc_u[...].astype(up_ref.dtype)
 
         return carry
 
-    lax.fori_loop(0, back_ref.shape[0], add_member, 0)
-    out_ref[...] = acc_ref[...].astype(out_ref.dtype)
-
-
-def combine(member_langs, back, lang_count):
+    lax.fori_loop(first_at, end_at, add_member, 0)
+
+
+def combine(slot_lang, back, lang_count):
+    devices, slots = slot_lang.shape
     members, row_count, bottleneck = back.shape
-    block = 16 if lang_count % 16 == 0 else (8 if lang_count % 8 == 0 else 1)
+    block = 32 if lang_count % 32 == 0 else (8 if lang_count % 8 == 0 else 1)
+    blocks = lang_count // block
+    langs = slot_lang.reshape(-1)
+    down_index = (
+        jnp.arange(devices, dtype=jnp.int32)[:, None] * (2 * slots)
+        + jnp.arange(slots, dtype=jnp.int32)[None, :]
+    ).reshape(-1)
+    order = jnp.argsort(langs, stable=True)
+    sorted_langs = langs[order]
+    member_order = down_index[order]
+    edges = jnp.arange(blocks + 1, dtype=jnp.int32) * block
+    starts = jnp.sum((sorted_langs[None, :] < edges[:, None]).astype(jnp.int32), axis=1)
     grid_spec = pltpu.PrefetchScalarGridSpec(
-        num_scalar_prefetch=1,
-        grid=(lang_count // block,),
-        in_specs=[pl.BlockSpec((members, row_count, bottleneck), lambda b, ml: (0, 0, 0))],
-        out_specs=pl.BlockSpec((block, row_count, bottleneck), lambda b, ml: (b, 0, 0)),
-        scratch_shapes=[pltpu.VMEM((block, row_count, bottleneck), jnp.float32)],
-    )
+        num_scalar_prefetch=3,
+        grid=(blocks,),
+        in_specs=[pl.BlockSpec((members, row_count, bottleneck), lambda b, o, l, st: (0, 0, 0))],
+        out_specs=[
+            pl.BlockSpec((block, row_count, bottleneck), lambda b, o, l, st: (b, 0, 0)),
+            pl.BlockSpec((block, row_count, bottleneck), lambda b, o, l, st: (b, 0, 0)),
+        ],
+        scratch_shapes=[
+            pltpu.VMEM((row_count, bottleneck), jnp.float32),
+            pltpu.VMEM((row_count, bottleneck), jnp.float32),
+        ],
+    )
+    out_shape = jax.ShapeDtypeStruct((lang_count, row_count, bottleneck), jnp.bfloat16)
     return pl.pallas_call(
-        combine_kernel,
+        functools.partial(combine_kernel, slots=slots),
         grid_spec=grid_spec,
-        out_shape=jax.ShapeDtypeStruct((lang_count, row_count, bottleneck), jnp.bfloat16),
-        compiler_params=pltpu.CompilerParams(dimension_semantics=("arbitrary",)),
+        out_shape=[out_shape, out_shape],
+        compiler_params=pltpu.CompilerParams(
+            dimension_semantics=("arbitrary",), vmem_limit_bytes=48 * 1024 * 1024
+        ),
         cost_estimate=pl.CostEstimate(
-            flops=back.size, bytes_accessed=back.size * 2 + lang_count * row_count * bottleneck * 2,
+            flops=back.size, bytes_accessed=back.size * 2 + 2 * lang_count * row_count * bottleneck * 2,
             transcendentals=0,
         ),
-    )(member_langs, back)
+    )(member_order.astype(jnp.int32), sorted_langs.astype(jnp.int32), starts, back)
 
 
 def local_pass(frames, cotangent, gain, weights, own_slot, own_lengths, slots, own_scale):
@@ -119,8 +162,7 @@
         ],
         out_specs=[
             pl.BlockSpec((1, frame_count, width), lambda u, sl, ln: (u, 0, 0)),
-            pl.BlockSpec((slots, width, bottleneck), lambda u, sl, ln: (0, 0, 0)),
-            pl.BlockSpec((slots, width, bottleneck), lambda u, sl, ln: (0, 0, 0)),
+            pl.BlockSpec((2 * slots, width, bottleneck), lambda u, sl, ln: (0, 0, 0)),
         ],
         scratch_shapes=[
             pltpu.VMEM((slots, width, bottleneck), jnp.float32),
@@ -132,8 +174,7 @@
         grid_spec=grid_spec,
         out_shape=[
             jax.ShapeDtypeStruct(frames.shape, jnp.bfloat16),
-            jax.ShapeDtypeStruct((slots, width, bottleneck), jnp.bfloat16),
-            jax.ShapeDtypeStruct((slots, width, bottleneck), jnp.bfloat16),
+            jax.ShapeDtypeStruct((2 * slots, width, bottleneck), jnp.bfloat16),
         ],
 
         compiler_params=pltpu.CompilerParams(
@@ -169,17 +210,13 @@
 
     weights = got.transpose(1, 0, 2, 3).reshape(2 * slots, devices * row_count, bottleneck)
     own_scale = jnp.take(scaling, lax.dynamic_index_in_dim(slot_lang, self_index, 0, False))
-    d_frames, grad_down, grad_up = local_pass(
+    d_frames, grads = local_pass(
         frames, cotangent, gain, weights, own_slot, own_lengths, slots, own_scale
     )
-
-    def exchange_back(grad):
-        scaled = grad.reshape(slots, devices, row_count, bottleneck).transpose(1, 0, 2, 3)
-        back = lax.all_to_all(scaled, "dp", split_axis=0, concat_axis=0, tiled=True)
-        return combine(member_langs, back.reshape(devices * slots, row_count, bottleneck), lang_count)
-
-    down_grads = exchange_back(grad_down)
-    up_grads = exchange_back(grad_up)
+    grads = grads.reshape(2 * slots, devices, row_count, bottleneck).transpose(1, 0, 2, 3)
+    back = lax.all_to_all(grads, "dp", split_axis=0, concat_axis=0, tiled=True)
+    back = back.reshape(devices * 2 * slots, row_count, bottleneck)
+    down_grads, up_grads = combine(slot_lang, back, lang_count)
     return (d_frames, down_grads, up_grads)
 
 

time: 205 us -> 192 us (0.937)
  Pallas kernels: 37.5 us -> 22.8 us
  waiting for transfers between devices: 126 us -> 132 us
  starting transfers between devices: 16.7 us -> 11.6 us
    pallas_call x2 -> x1, Pallas kernels: 21.3 us -> 6.77 us  [combine(): pl.pallas_call(functools.partial(combine_kernel, slots=slots), grid_spec=...]
    all_to_all x2 -> x1, waiting for transfers between devices: 60.4 us -> 66.5 us  [on_device(): back = lax.all_to_all(grads, 'dp', split_axis=0, concat_axis=0, tiled=True)]
    all_to_all x2 -> x1, starting transfers between devices: 9.95 us -> 4.88 us  [on_device(): back = lax.all_to_all(grads, 'dp', split_axis=0, concat_axis=0, tiled=True)]
    unnamed x17 -> x9, local copies, waits for them, and re-layouts: 3.08 us -> 0.77 us
  transfers between devices with their start and end apart: 3 -> 2, of which waited for: 3 -> 2; matrix products, arithmetic and copies ran while one was open for 3% -> 4% of each run, Pallas kernels for 5% -> 0%
where the time goes in v6:
time: 192 us
  waiting for transfers between devices  132 us (69%)
  Pallas kernels  22.8 us (12%)
  local copies, waits for them, and re-layouts  19.5 us (10%)
  starting transfers between devices  11.6 us (6%)
  other arithmetic  4.89 us (3%)
    all_to_all x1, waiting for transfers between devices, on_device(): back = lax.all_to_all(grads, 'dp', split_axis=0, concat_axis=0, tiled=True)  66.5 us
    all_to_all x1, waiting for transfers between devices, on_device(): got = lax.all_to_all(sent, 'dp', split_axis=0, concat_axis=0, tiled=True)  65.5 us
    pallas_call x1, Pallas kernels, local_pass(): pl.pallas_call(adapter_kernel, grid_spec=grid_spec, out_shape=[jax.ShapeD...  16 us
    pallas_call x1, Pallas kernels, combine(): pl.pallas_call(functools.partial(combine_kernel, slots=slots), grid_spec=...  6.77 us
    all_to_all x1, starting transfers between devices, on_device(): got = lax.all_to_all(sent, 'dp', split_axis=0, concat_axis=0, tiled=True)  6.7 us
    all_to_all x1, starting transfers between devices, on_device(): back = lax.all_to_all(grads, 'dp', split_axis=0, concat_axis=0, tiled=True)  4.88 us
    gather x1, local copies, waits for them, and re-layouts, on_device(): jnp.take(up_weight, member_langs, axis=0)  3.88 us
    gather x1, local copies, waits for them, and re-layouts, on_device(): jnp.take(down_weight, member_langs, axis=0)  3.88 us
  transfers between devices with their start and end apart: 2, of which 2 were waited for; matrix products, arithmetic and copies ran while one was open for 4% of the time, Pallas kernels for 0%

profile of v6, /device:TPU:15, one launch (start us, length us, event | category | flops | bytes accessed | tf_op | source)
XLA Modules:
  0.0 191.5 jit_solution(18183178604569617612)
XLA Ops:
  0.6 0.8 copy.34
  1.5 3.9 %gather_fusion.5 = bf16[32,96,256]{2,1,0:T(8,128)(2,1)S(1)} fusion(bf16[160,96,256]{2,1,0:T(8,128)(2,1)} %param.14, s32[1024]{0:T(1024)S(1)} %pad_clamp_fusion.2), kind=kCustom, calls=%fused_computation.1.clone | custom fusion | bytes 3145856 | tf_op jit(solution)/shard_map/jit(_take)/gather | solution.py:205
  5.4 3.9 %gather_fusion.4 = bf16[32,96,256]{2,1,0:T(8,128)(2,1)S(1)} fusion(bf16[160,96,256]{2,1,0:T(8,128)(2,1)} %param.13, s32[1024]{0:T(1024)S(1)} %pad_clamp_fusion.2), kind=kCustom, calls=%fused_computation.clone | custom fusion | bytes 3145856 | tf_op jit(solution)/shard_map/jit(_take)/gather | solution.py:202
  9.3 0.3 broadcast_select_fusion.1
  9.6 1.9 %pad_maximum_fusion = bf16[16,4,96,256]{3,2,1,0:T(8,128)(2,1)} fusion(bf16[16,2,96,256]{3,2,1,0:T(8,128)(2,1)S(1)} %bitcast.25, bf16[16,2,96,256]{3,2,1,0:T(8,128)(2,1)S(1)} %bitcast.24), kind=kLoop, calls=%fused_computation.6 | loop fusion | flops 1572864 | bytes 6291456 | tf_op jit(solution)/shard_map/concatenate | solution.py:208
  11.6 6.7 %all-to-all-start = ((bf16[16,4,96,256]{3,2,1,0:T(8,128)(2,1)}), bf16[16,4,96,256]{3,2,1,0:T(8,128)(2,1)S(1)}, u32[]{:S(2)}, u32[]{:S(2)}) async-start(bf16[16,4,96,256]{3,2,1,0:T(8,128)(2,1)} %pad_maximum_fusion), calls=%async_computation | async-start | bytes 6291456 | tf_op jit(solution)/shard_map/all_to_all | solution.py:209
  18.3 0.9 gather_fusion
  19.2 0.6 dynamic_slice.10.slot_ref
  19.8 0.6 dynamic_slice.11.len_ref
  20.5 0.2 fusion.8
  20.8 0.6 gather_fusion.1
  21.5 0.6 reshape.171.gain_ref
  22.1 0.6 and_select_fusion.scale_ref
  22.7 65.5 %all-to-all-done = bf16[16,4,96,256]{3,2,1,0:T(8,128)(2,1)S(1)} async-done(((bf16[16,4,96,256]{3,2,1,0:T(8,128)(2,1)}), bf16[16,4,96,256]{3,2,1,0:T(8,128)(2,1)S(1)}, u32[]{:S(2)}, u32[]{:S(2)}) %all-to-all-start) | async-done | bytes 3145760 | tf_op jit(solution)/shard_map/all_to_all | solution.py:209
  88.2 1.9 %copy.35 = bf16[4,16,96,256]{3,2,1,0:T(8,128)(2,1)} copy(bf16[4,16,96,256]{3,2,0,1:T(8,128)(2,1)S(1)} %bitcast.22) | data formatting | bytes 6291456 | tf_op jit(solution)/shard_map/transpose | solution.py:211
  90.1 16.0 %shard_map.103 = (bf16[4,256,1536]{2,1,0:T(8,128)(2,1)}, bf16[4,1536,256]{2,1,0:T(8,128)(2,1)}) custom-call(s32[4]{0:T(128)} %dynamic_slice.10.slot_ref, s32[4]{0:T(128)} %dynamic_slice.11.len_ref, bf16[4,256,1536]{2,1,0:T(8,128)(2,1)} %frames_ref.1, bf16[4,256,1536]{2,1,0:T(8,128)(2,1)} %cot_ref.1, f32[1,1536]{1,0:T(1,128)} %reshape.171.gain_ref, ...), custom_call_target="tpu_custom_call" | custom-call | flops 4026531840 | bytes 28311552 | tf_op jit(solution)/shard_map/pallas_call | solution.py:172
  106.1 3.8 %copy.42 = bf16[4,16,96,256]{3,2,0,1:T(8,128)(2,1)} copy(bf16[4,16,96,256]{3,2,1,0:T(8,128)(2,1)} %bitcast.28) | data formatting | bytes 6291456 | tf_op jit(solution)/shard_map/reshape | solution.py:216
  110.0 4.9 %all-to-all-start.1 = ((bf16[16,4,96,256]{3,2,1,0:T(8,128)(2,1)}), bf16[16,4,96,256]{3,2,1,0:T(8,128)(2,1)S(1)}, u32[]{:S(2)}, u32[]{:S(2)}) async-start(bf16[16,4,96,256]{3,2,1,0:T(8,128)(2,1)} %bitcast.23), calls=%async_computation.1 | async-start | bytes 6291456 | tf_op jit(solution)/shard_map/all_to_all | solution.py:217
  115.0 1.6 sort.17
  116.6 0.7 gather_fusion.3
  117.3 0.7 gather_fusion.2
  118.1 0.2 convert_reduce_fusion.start_ref
  118.2 66.5 %all-to-all-done.1 = bf16[16,4,96,256]{3,2,1,0:T(8,128)(2,1)S(1)} async-done(((bf16[16,4,96,256]{3,2,1,0:T(8,128)(2,1)}), bf16[16,4,96,256]{3,2,1,0:T(8,128)(2,1)S(1)}, u32[]{:S(2)}, u32[]{:S(2)}) %all-to-all-start.1) | async-done | bytes 3145760 | tf_op jit(solution)/shard_map/all_to_all | solution.py:217
  184.7 6.8 %shard_map.104 = (bf16[160,96,256]{2,1,0:T(8,128)(2,1)}, bf16[160,96,256]{2,1,0:T(8,128)(2,1)}) custom-call(s32[32]{0:T(128)S(1)} %gather_fusion.2, s32[32]{0:T(128)S(1)} %gather_fusion.3, s32[6]{0:T(128)S(1)} %convert_reduce_fusion.start_ref, bf16[64,96,256]{2,1,0:T(8,128)(2,1)S(1)} %bitcast.21), custom_call_target="tpu_custom_call" | custom-call | flops 1572864 | bytes 18874368 | tf_op jit(solution)/shard_map/pallas_call | solution.py:133
  (25 shorter events, 0.5 us)
Async XLA Ops:
  11.6 6.7 %copy-start.3 = (s32[64]{0:T(128)S(1)}, s32[64]{0:T(128)}, u32[]{:S(2)}) copy-start(s32[64]{0:T(128)} %param.16) | copy-start | bytes 772
  11.6 6.7 %copy-start = (s32[16,2]{0,1:T(2,128)S(1)}, s32[16,2]{0,1:T(2,128)}, u32[]{:S(2)}) copy-start(s32[16,2]{0,1:T(2,128)} %param.15) | copy-start | bytes 388
  11.6 8.2 %copy-start.2 = (s32[64]{0:T(128)S(1)}, s32[64]{0:T(128)}, u32[]{:S(2)}) copy-start(s32[64]{0:T(128)} %param.17) | copy-start | bytes 772
  11.6 9.9 %copy-start.1 = (f32[1536]{0:T(1024)S(1)}, f32[1536]{0:T(1024)}, u32[]{:S(2)}) copy-start(f32[1536]{0:T(1024)} %param.12) | copy-start | bytes 18436
  11.6 76.6 %all-to-all-start = ((bf16[16,4,96,256]{3,2,1,0:T(8,128)(2,1)}), bf16[16,4,96,256]{3,2,1,0:T(8,128)(2,1)S(1)}, u32[]{:S(2)}, u32[]{:S(2)}) async-start(bf16[16,4,96,256]{3,2,1,0:T(8,128)(2,1)} %pad_maximum_fusion), calls=%async_computation | async-start | bytes 6291456 | tf_op jit(solution)/shard_map/all_to_all | solution.py:209
  110.0 74.8 %all-to-all-start.1 = ((bf16[16,4,96,256]{3,2,1,0:T(8,128)(2,1)}), bf16[16,4,96,256]{3,2,1,0:T(8,128)(2,1)S(1)}, u32[]{:S(2)}, u32[]{:S(2)}) async-start(bf16[16,4,96,256]{3,2,1,0:T(8,128)(2,1)} %bitcast.23), calls=%async_computation.1 | async-start | bytes 6291456 | tf_op jit(solution)/shard_map/all_to_all | solution.py:217

commit v7 on v6

--- a/solution.py
+++ b/solution.py
@@ -9,7 +9,7 @@
 
 
 def adapter_kernel(slot_ref, len_ref, frames_ref, cot_ref, gain_ref, wd_ref, wu_ref, scale_ref,
-                   out_ref, grads_out, gd_ref, gu_ref):
+                   out_ref, grads_out, gd_ref, gu_ref, *, direct):
     u = pl.program_id(0)
 
     @pl.when(u == 0)
@@ -27,8 +27,13 @@
     reciprocal_deviation = lax.rsqrt(variance + 1e-06)
     standardized_input = mean_removed * reciprocal_deviation
     layer_normed = (standardized_input * gain).astype(jnp.bfloat16)
-    w_down = wd_ref[0]
-    w_up = wu_ref[0]
+    if direct:
+        devices, _, row_count, bottleneck = wd_ref.shape
+        w_down = wd_ref[:, 0].reshape(devices * row_count, bottleneck)
+        w_up = wu_ref[:, 0].reshape(devices * row_count, bottleneck)
+    else:
+        w_down = wd_ref[0]
+        w_up = wu_ref[0]
     pre_act = jnp.dot(layer_normed, w_down, preferred_element_type=jnp.float32)
     sigmoid_pre = 1.0 / (1.0 + jnp.exp(-pre_act))
     hidden = (pre_act * sigmoid_pre).astype(jnp.bfloat16)
@@ -58,8 +63,21 @@
     @pl.when(u == pl.num_programs(0) - 1)
     def _():
         slots = gd_ref.shape[0]
-        grads_out[pl.ds(0, slots)] = (gd_ref[...] * scale_ref[...]).astype(grads_out.dtype)
-        grads_out[pl.ds(slots, slots)] = (gu_ref[...] * scale_ref[...]).astype(grads_out.dtype)
+        if direct:
+            devices, _, row_count, _ = grads_out.shape
+            for dev in range(devices):
+                rows = pl.ds(dev * row_count, row_count)
+                grads_out[dev, pl.ds(0, slots)] = (
+                    gd_ref[:, rows, :] * scale_ref[...]
+                ).astype(grads_out.dtype)
+                grads_out[dev, pl.ds(slots, slots)] = (
+                    gu_ref[:, rows, :] * scale_ref[...]
+                ).astype(grads_out.dtype)
+        else:
+            grads_out[pl.ds(0, slots)] = (gd_ref[...] * scale_ref[...]).astype(grads_out.dtype)
+            grads_out[pl.ds(slots, slots)] = (gu_ref[...] * scale_ref[...]).astype(
+                grads_out.dtype
+            )
 
 
 def combine_kernel(order_ref, lang_ref, start_ref, back_ref, down_ref, up_ref, acc_d, acc_u,
@@ -144,9 +162,78 @@
     )(member_order.astype(jnp.int32), sorted_langs.astype(jnp.int32), starts, back)
 
 
-def local_pass(frames, cotangent, gain, weights, own_slot, own_lengths, slots, own_scale):
+def gather_kernel(lang_ref, down_hbm, up_hbm, out_ref, sems, *, slots):
+    members = lang_ref.shape[0]
+
+    def copies(m):
+        lang = lang_ref[m]
+        dev = m // slots
+        s = m % slots
+        return (
+            pltpu.make_async_copy(down_hbm.at[lang], out_ref.at[dev, s], sems.at[0, m]),
+            pltpu.make_async_copy(up_hbm.at[lang], out_ref.at[dev, slots + s], sems.at[1, m]),
+        )
+
+    def start(m, carry):
+        for c in copies(m):
+            c.start()
+        return carry
+
+    def finish(m, carry):
+        for c in copies(m):
+            c.wait()
+        return carry
+
+    lax.fori_loop(0, members, start, 0)
+    lax.fori_loop(0, members, finish, 0)
+
+
+def gather_rows(slot_lang, down_weight, up_weight):
+    devices, slots = slot_lang.shape
+    _, row_count, bottleneck = down_weight.shape
+    members = devices * slots
+    grid_spec = pltpu.PrefetchScalarGridSpec(
+        num_scalar_prefetch=1,
+        grid=(1,),
+        in_specs=[pl.BlockSpec(memory_space=pl.ANY), pl.BlockSpec(memory_space=pl.ANY)],
+        out_specs=pl.BlockSpec(
+            (devices, 2 * slots, row_count, bottleneck), lambda i, ml: (0, 0, 0, 0)
+        ),
+        scratch_shapes=[pltpu.SemaphoreType.DMA((2, members))],
+    )
+    size = members * 2 * row_count * bottleneck * 2
+    return pl.pallas_call(
+        functools.partial(gather_kernel, slots=slots),
+        grid_spec=grid_spec,
+        out_shape=jax.ShapeDtypeStruct((devices, 2 * slots, row_count, bottleneck), jnp.bfloat16),
+        compiler_params=pltpu.CompilerParams(vmem_limit_bytes=48 * 1024 * 1024),
+        cost_estimate=pl.CostEstimate(flops=0, bytes_accessed=2 * size, transcendentals=0),
+    )(slot_lang.reshape(-1), down_weight, up_weight)
+
+
+def local_pass(frames, cotangent, gain, got, own_slot, own_lengths, own_scale):
     utts, frame_count, width = frames.shape
-    bottleneck = weights.shape[2]
+    devices, double_slots, row_count, bottleneck = got.shape
+    slots = double_slots // 2
+    direct = row_count % 16 == 0
+    if direct:
+        weights = got
+        w_specs = [
+            pl.BlockSpec((devices, 1, row_count, bottleneck), lambda u, sl, ln: (0, sl[u], 0, 0)),
+            pl.BlockSpec(
+                (devices, 1, row_count, bottleneck), lambda u, sl, ln: (0, sl[u] + slots, 0, 0)
+            ),
+        ]
+        grads_shape = (devices, 2 * slots, row_count, bottleneck)
+        grads_spec = pl.BlockSpec(grads_shape, lambda u, sl, ln: (0, 0, 0, 0))
+    else:
+        weights = got.transpose(1, 0, 2, 3).reshape(2 * slots, width, bottleneck)
+        w_specs = [
+            pl.BlockSpec((1, width, bottleneck), lambda u, sl, ln: (sl[u], 0, 0)),
+            pl.BlockSpec((1, width, bottleneck), lambda u, sl, ln: (sl[u] + slots, 0, 0)),
+        ]
+        grads_shape = (2 * slots, width, bottleneck)
+        grads_spec = pl.BlockSpec(grads_shape, lambda u, sl, ln: (0, 0, 0))
     flops = 10 * utts * frame_count * width * bottleneck
     moved = 3 * frames.size * 2 + 2 * utts * width * bottleneck * 2 + 4 * slots * width * bottleneck * 4
     grid_spec = pltpu.PrefetchScalarGridSpec(
@@ -156,33 +243,34 @@
             pl.BlockSpec((1, frame_count, width), lambda u, sl, ln: (u, 0, 0)),
             pl.BlockSpec((1, frame_count, width), lambda u, sl, ln: (u, 0, 0)),
             pl.BlockSpec((1, width), lambda u, sl, ln: (0, 0)),
-            pl.BlockSpec((1, width, bottleneck), lambda u, sl, ln: (sl[u], 0, 0)),
-            pl.BlockSpec((1, width, bottleneck), lambda u, sl, ln: (sl[u] + slots, 0, 0)),
+            *w_specs,
             pl.BlockSpec((slots, 1, 1), lambda u, sl, ln: (0, 0, 0)),
         ],
         out_specs=[
             pl.BlockSpec((1, frame_count, width), lambda u, sl, ln: (u, 0, 0)),
-            pl.BlockSpec((2 * slots, width, bottleneck), lambda u, sl, ln: (0, 0, 0)),
+            grads_spec,
         ],
         scratch_shapes=[
             pltpu.VMEM((slots, width, bottleneck), jnp.float32),
             pltpu.VMEM((slots, width, bottleneck), jnp.float32),
         ],
     )
-    return pl.pallas_call(
-        adapter_kernel,
+    d_frames, grads = pl.pallas_call(
+        functools.partial(adapter_kernel, direct=direct),
         grid_spec=grid_spec,
         out_shape=[
             jax.ShapeDtypeStruct(frames.shape, jnp.bfloat16),
-            jax.ShapeDtypeStruct((2 * slots, width, bottleneck), jnp.bfloat16),
-        ],
-
+            jax.ShapeDtypeStruct(grads_shape, jnp.bfloat16),
+        ],
         compiler_params=pltpu.CompilerParams(
             dimension_semantics=("arbitrary",), vmem_limit_bytes=60 * 1024 * 1024
         ),
         cost_estimate=pl.CostEstimate(flops=flops, bytes_accessed=moved, transcendentals=utts * frame_count * bottleneck),
     )(own_slot, own_lengths, frames, cotangent, gain.reshape(1, width), weights, weights,
       own_scale.reshape(slots, 1, 1))
+    if not direct:
+        grads = grads.reshape(2 * slots, devices, row_count, bottleneck).transpose(1, 0, 2, 3)
+    return d_frames, grads
 
 
 def on_device(frames, cotangent, gain, down_weight, up_weight, slot_lang, utt_slot, lengths):
@@ -199,21 +287,11 @@
     counts = jnp.sum(jnp.where(utt_lang[None, :] == lang_ids[:, None], lengths[None, :], 0), axis=1)
     scaling = lax.rsqrt(jnp.maximum(counts, 1).astype(jnp.float32))
     member_langs = slot_lang.reshape(-1)
-    send_down = jnp.take(down_weight, member_langs, axis=0).reshape(
-        devices, slots, row_count, bottleneck
-    )
-    send_up = jnp.take(up_weight, member_langs, axis=0).reshape(
-        devices, slots, row_count, bottleneck
-    )
-    sent = jnp.concatenate([send_down, send_up], axis=1)
+    sent = gather_rows(slot_lang, down_weight, up_weight)
     got = lax.all_to_all(sent, "dp", split_axis=0, concat_axis=0, tiled=True)
 
-    weights = got.transpose(1, 0, 2, 3).reshape(2 * slots, devices * row_count, bottleneck)
     own_scale = jnp.take(scaling, lax.dynamic_index_in_dim(slot_lang, self_index, 0, False))
-    d_frames, grads = local_pass(
-        frames, cotangent, gain, weights, own_slot, own_lengths, slots, own_scale
-    )
-    grads = grads.reshape(2 * slots, devices, row_count, bottleneck).transpose(1, 0, 2, 3)
+    d_frames, grads = local_pass(frames, cotangent, gain, got, own_slot, own_lengths, own_scale)
     back = lax.all_to_all(grads, "dp", split_axis=0, concat_axis=0, tiled=True)
     back = back.reshape(devices * 2 * slots, row_count, bottleneck)
     down_grads, up_grads = combine(slot_lang, back, lang_count)

time: 192 us -> 182 us (0.948)
  local copies, waits for them, and re-layouts: 19.5 us -> 7.68 us
  Pallas kernels: 22.8 us -> 27.5 us
  other arithmetic: 4.89 us -> 2.59 us
    gather x2 -> x0, local copies, waits for them, and re-layouts: 7.76 us -> none  [the longest x1 3.88 us: on_device(): jnp.take(up_weight, member_langs, axis=0)]
    pallas_call x1 -> x2, Pallas kernels: 16 us -> 20.3 us  [the longest x1 15.7 us: local_pass(): pl.pallas_call(functools.partial(adapter_kernel, direct=direct), grid_spe...]
    reshape x2 -> x1, local copies, waits for them, and re-layouts: 3.91 us -> 0.09 us  [gather_rows(): slot_lang.reshape(-1)]
    concatenate x1 -> x0, other arithmetic: 1.94 us -> none  [on_device(): sent = jnp.concatenate([send_down, send_up], axis=1)]
    transpose x1 -> x0, local copies, waits for them, and re-layouts: 1.93 us -> none  [on_device(): got.transpose(1, 0, 2, 3)]
where the time goes in v7:
time: 182 us
  waiting for transfers between devices  132 us (73%)
  Pallas kernels  27.5 us (15%)
  starting transfers between devices  11.6 us (6%)
  local copies, waits for them, and re-layouts  7.68 us (4%)
  other arithmetic  2.59 us (1%)
    all_to_all x1, waiting for transfers between devices, on_device(): back = lax.all_to_all(grads, 'dp', split_axis=0, concat_axis=0, tiled=True)  66.5 us
    all_to_all x1, waiting for transfers between devices, on_device(): got = lax.all_to_all(sent, 'dp', split_axis=0, concat_axis=0, tiled=True)  65.5 us
    pallas_call x1, Pallas kernels, local_pass(): pl.pallas_call(functools.partial(adapter_kernel, direct=direct), grid_spe...  15.7 us
    pallas_call x1, Pallas kernels, combine(): pl.pallas_call(functools.partial(combine_kernel, slots=slots), grid_spec=...  7.11 us
    all_to_all x1, starting transfers between devices, on_device(): got = lax.all_to_all(sent, 'dp', split_axis=0, concat_axis=0, tiled=True)  6.7 us
    all_to_all x1, starting transfers between devices, on_device(): back = lax.all_to_all(grads, 'dp', split_axis=0, concat_axis=0, tiled=True)  4.91 us
    pallas_call x1, Pallas kernels, gather_rows(): pl.pallas_call(functools.partial(gather_kernel, slots=slots), grid_spec=g...  4.69 us
  transfers between devices with their start and end apart: 2, of which 2 were waited for; matrix products, arithmetic and copies ran while one was open for 4% of the time, Pallas kernels for 0%

profile of v7, /device:TPU:15, one launch (start us, length us, event | category | flops | bytes accessed | tf_op | source)
XLA Modules:
  0.0 182.0 jit_solution(12542673290712278677)
XLA Ops:
  0.6 0.8 copy.21
  1.4 0.1 reshape.155.lang_ref
  1.5 4.7 %shard_map.103 = bf16[16,4,96,256]{3,2,1,0:T(8,128)(2,1)} custom-call(s32[32]{0:T(128)S(1)} %reshape.155.lang_ref, bf16[160,96,256]{2,1,0:T(8,128)(2,1)} %down_hbm.1, bf16[160,96,256]{2,1,0:T(8,128)(2,1)} %up_hbm.1), custom_call_target="tpu_custom_call" | custom-call | bytes 6291456 | tf_op jit(solution)/shard_map/pallas_call | solution.py:205
  6.2 6.7 %all-to-all-start = ((bf16[16,4,96,256]{3,2,1,0:T(8,128)(2,1)}), bf16[16,4,96,256]{3,2,1,0:T(8,128)(2,1)S(1)}, u32[]{:S(2)}, u32[]{:S(2)}) async-start(bf16[16,4,96,256]{3,2,1,0:T(8,128)(2,1)} %shard_map.103), calls=%async_computation | async-start | bytes 6291456 | tf_op jit(solution)/shard_map/all_to_all | solution.py:291
  13.0 0.9 gather_fusion
  13.8 0.6 dynamic_slice.10.slot_ref
  14.5 0.6 dynamic_slice.11.len_ref
  15.1 0.2 fusion.8
  15.3 0.1 select_reduce_fusion
  15.4 0.6 gather_fusion.1
  16.1 0.1 copy.25
  16.2 0.6 reshape.154.gain_ref
  16.8 0.6 and_select_fusion.scale_ref
  17.3 65.5 %all-to-all-done.wd_ref.wu_ref = bf16[16,4,96,256]{3,2,1,0:T(8,128)(2,1)S(1)} async-done(((bf16[16,4,96,256]{3,2,1,0:T(8,128)(2,1)}), bf16[16,4,96,256]{3,2,1,0:T(8,128)(2,1)S(1)}, u32[]{:S(2)}, u32[]{:S(2)}) %all-to-all-start) | async-done | bytes 3145760 | tf_op jit(solution)/shard_map/all_to_all | solution.py:291
  82.8 1.7 copy-done.1
  84.5 15.7 %shard_map.104 = (bf16[4,256,1536]{2,1,0:T(8,128)(2,1)}, bf16[16,4,96,256]{3,2,1,0:T(8,128)(2,1)}) custom-call(s32[4]{0:T(128)} %dynamic_slice.10.slot_ref, s32[4]{0:T(128)} %dynamic_slice.11.len_ref, bf16[4,256,1536]{2,1,0:T(8,128)(2,1)} %frames_ref.1, bf16[4,256,1536]{2,1,0:T(8,128)(2,1)} %cot_ref.1, f32[1,1536]{1,0:T(1,128)} %reshape.154.gain_ref, ...), custom_call_target="tpu_custom_call" | custom-call | flops 4026531840 | bytes 28311552 | tf_op jit(solution)/shard_map/pallas_call | solution.py:258
  100.1 4.9 %all-to-all-start.1 = ((bf16[16,4,96,256]{3,2,1,0:T(8,128)(2,1)}), bf16[16,4,96,256]{3,2,1,0:T(8,128)(2,1)S(1)}, u32[]{:S(2)}, u32[]{:S(2)}) async-start(bf16[16,4,96,256]{3,2,1,0:T(8,128)(2,1)} %get-tuple-element.10), calls=%async_computation.1 | async-start | bytes 6291456 | tf_op jit(solution)/shard_map/all_to_all | solution.py:295
  105.1 0.1 add.89
  105.2 1.6 sort.17
  106.8 0.7 gather_fusion.3
  107.5 0.7 gather_fusion.2
  108.2 0.2 convert_reduce_fusion.start_ref
  108.4 66.5 %all-to-all-done.1 = bf16[16,4,96,256]{3,2,1,0:T(8,128)(2,1)S(1)} async-done(((bf16[16,4,96,256]{3,2,1,0:T(8,128)(2,1)}), bf16[16,4,96,256]{3,2,1,0:T(8,128)(2,1)S(1)}, u32[]{:S(2)}, u32[]{:S(2)}) %all-to-all-start.1) | async-done | bytes 3145760 | tf_op jit(solution)/shard_map/all_to_all | solution.py:295
  174.9 7.1 %shard_map.105 = (bf16[160,96,256]{2,1,0:T(8,128)(2,1)}, bf16[160,96,256]{2,1,0:T(8,128)(2,1)}) custom-call(s32[32]{0:T(128)S(1)} %gather_fusion.2, s32[32]{0:T(128)S(1)} %gather_fusion.3, s32[6]{0:T(128)S(1)} %convert_reduce_fusion.start_ref, bf16[64,96,256]{2,1,0:T(8,128)(2,1)S(1)} %bitcast.13), custom_call_target="tpu_custom_call" | custom-call | flops 1572864 | bytes 18874368 | tf_op jit(solution)/shard_map/pallas_call | solution.py:151
  (19 shorter events, 0.2 us)
Async XLA Ops:
  6.2 6.7 %copy-start.4 = (s32[64]{0:T(128)S(1)}, s32[64]{0:T(128)}, u32[]{:S(2)}) copy-start(s32[64]{0:T(128)} %param.14) | copy-start | bytes 772
  6.2 6.8 %copy-start = (s32[16,2]{0,1:T(2,128)S(1)}, s32[16,2]{0,1:T(2,128)}, u32[]{:S(2)}) copy-start(s32[16,2]{0,1:T(2,128)} %param.13) | copy-start | bytes 388
  6.2 8.3 %copy-start.3 = (s32[64]{0:T(128)S(1)}, s32[64]{0:T(128)}, u32[]{:S(2)}) copy-start(s32[64]{0:T(128)} %param.15) | copy-start | bytes 772
  6.2 9.9 %copy-start.2 = (f32[1536]{0:T(1024)S(1)}, f32[1536]{0:T(1024)}, u32[]{:S(2)}) copy-start(f32[1536]{0:T(1024)} %param.10) | copy-start | bytes 18436
  6.2 76.6 %all-to-all-start = ((bf16[16,4,96,256]{3,2,1,0:T(8,128)(2,1)}), bf16[16,4,96,256]{3,2,1,0:T(8,128)(2,1)S(1)}, u32[]{:S(2)}, u32[]{:S(2)}) async-start(bf16[16,4,96,256]{3,2,1,0:T(8,128)(2,1)} %shard_map.103), calls=%async_computation | async-start | bytes 6291456 | tf_op jit(solution)/shard_map/all_to_all | solution.py:291
  82.8 1.7 copy-start.1
  100.1 74.8 %all-to-all-start.1 = ((bf16[16,4,96,256]{3,2,1,0:T(8,128)(2,1)}), bf16[16,4,96,256]{3,2,1,0:T(8,128)(2,1)S(1)}, u32[]{:S(2)}, u32[]{:S(2)}) async-start(bf16[16,4,96,256]{3,2,1,0:T(8,128)(2,1)} %get-tuple-element.10), calls=%async_computation.1 | async-start | bytes 6291456 | tf_op jit(solution)/shard_map/all_to_all | solution.py:295

commit v8 on v5

v8 whole, which is shorter than its diff:
```python
import functools

import jax
import jax.numpy as jnp
from jax import lax
from jax.experimental import pallas as pl
from jax.experimental.pallas import tpu as pltpu
from jax.sharding import PartitionSpec as P


def _weights(ref, direct):
    if direct:
        devices, _, row_count, bottleneck = ref.shape
        return ref[:, 0].reshape(devices * row_count, bottleneck)
    return ref[0]


def _flush(acc_ref, scale_ref, out_ref, direct):
    if direct:
        devices, slots, row_count, _ = out_ref.shape
        for dev in range(devices):
            rows = pl.ds(dev * row_count, row_count)
            out_ref[dev] = (acc_ref[:, rows, :] * scale_ref[...]).astype(out_ref.dtype)
    else:
        out_ref[...] = (acc_ref[...] * scale_ref[...]).astype(out_ref.dtype)


def _normalize(frames_ref, gain):
    values = frames_ref[0].astype(jnp.float32)
    centre_mean = jnp.mean(values, axis=1, keepdims=True)
    mean_removed = values - centre_mean
    variance = jnp.mean(mean_removed * mean_removed, axis=1, keepdims=True)
    reciprocal_deviation = lax.rsqrt(variance + 1e-06)
    standardized_input = mean_removed * reciprocal_deviation
    layer_normed = (standardized_input * gain).astype(jnp.bfloat16)
    return reciprocal_deviation, standardized_input, layer_normed


def _masked(cot_ref, length):
    upstream = cot_ref[0]
    live = lax.broadcasted_iota(jnp.int32, (upstream.shape[0], 1), 0) < length
    return upstream, jnp.where(live, upstream, jnp.zeros_like(upstream))


CONTRACT_ROWS = (((0,), (0,)), ((), ()))


def forward_kernel(slot_ref, len_ref, frames_ref, cot_ref, gain_ref, wd_ref, scale_ref,
                   pre_ref, gu_out, gu_ref, *, direct):
    u = pl.program_id(0)

    @pl.when(u == 0)
    def _():
        gu_ref[...] = jnp.zeros_like(gu_ref)

    slot = slot_ref[u]
    _, _, layer_normed = _normalize(frames_ref, gain_ref[...])
    pre_act = jnp.dot(layer_normed, _weights(wd_ref, direct), preferred_element_type=jnp.float32)
    pre_ref[0] = pre_act
    sigmoid_pre = 1.0 / (1.0 + jnp.exp(-pre_act))
    hidden = (pre_act * sigmoid_pre).astype(jnp.bfloat16)
    _, masked_up = _masked(cot_ref, len_ref[u])
    gu_ref[slot] += lax.dot_general(
        masked_up, hidden, CONTRACT_ROWS, preferred_element_type=jnp.float32
    )

    @pl.when(u == pl.num_programs(0) - 1)
    def _():
        _flush(gu_ref, scale_ref, gu_out, direct)


def backward_kernel(slot_ref, len_ref, frames_ref, cot_ref, gain_ref, wd_ref, wu_ref, pre_ref,
                    scale_ref, out_ref, gd_out, gd_ref, *, direct):
    u = pl.program_id(0)

    @pl.when(u == 0)
    def _():
        gd_ref[...] = jnp.zeros_like(gd_ref)

    slot = slot_ref[u]
    gain = gain_ref[...]
    reciprocal_deviation, standardized_input, layer_normed = _normalize(frames_ref, gain)
    pre_act = pre_ref[0]
    sigmoid_pre = 1.0 / (1.0 + jnp.exp(-pre_act))
    upstream, masked_up = _masked(cot_ref, len_ref[u])
    d_hidden = jnp.dot(masked_up, _weights(wu_ref, direct), preferred_element_type=jnp.float32)
    d_pre = (d_hidden * sigmoid_pre * (1.0 + pre_act * (1.0 - sigmoid_pre))).astype(jnp.bfloat16)
    gd_ref[slot] += lax.dot_general(
        layer_normed, d_pre, CONTRACT_ROWS, preferred_element_type=jnp.float32
    )
    d_normed = lax.dot_general(
        d_pre, _weights(wd_ref, direct), (((1,), (1,)), ((), ())),
        preferred_element_type=jnp.float32,
    )
    scaled_rows = d_normed * gain
    inner_gradient = (
        scaled_rows
        - jnp.mean(scaled_rows, axis=1, keepdims=True)
        - standardized_input * jnp.mean(scaled_rows * standardized_input, axis=1, keepdims=True)
    ) * reciprocal_deviation
    out_ref[0] = (upstream.astype(jnp.float32) + inner_gradient).astype(out_ref.dtype)

    @pl.when(u == pl.num_programs(0) - 1)
    def _():
        _flush(gd_ref, scale_ref, gd_out, direct)


def combine_kernel(order_ref, lang_ref, start_ref, back_ref, out_ref, acc_ref):
    block = out_ref.shape[0]
    b = pl.program_id(0)
    base = b * block
    out_ref[...] = jnp.zeros_like(out_ref)
    first_at = start_ref[b]
    end_at = start_ref[b + 1]
    last_member = lang_ref.shape[0] - 1

    def add_member(i, carry):
        m = order_ref[i]
        lang = lang_ref[i]
        first = (i == first_at) | (lang_ref[jnp.maximum(i - 1, 0)] != lang)
        last = (i == end_at - 1) | (lang_ref[jnp.minimum(i + 1, last_member)] != lang)
        val = back_ref[m].astype(jnp.float32)

        @pl.when(first)
        def _():
            acc_ref[...] = val

        @pl.when(jnp.logical_not(first))
        def _():
            acc_ref[...] += val

        @pl.when(last)
        def _():
            out_ref[lang - base] = acc_ref[...].astype(out_ref.dtype)

        return carry

    lax.fori_loop(first_at, end_at, add_member, 0)


def combine_plan(slot_lang, lang_count):
    block = 32 if lang_count % 32 == 0 else (8 if lang_count % 8 == 0 else 1)
    langs = slot_lang.reshape(-1)
    order = jnp.argsort(langs, stable=True).astype(jnp.int32)
    sorted_langs = langs[order].astype(jnp.int32)
    edges = jnp.arange(lang_count // block + 1, dtype=jnp.int32) * block
    starts = jnp.sum((sorted_langs[None, :] < edges[:, None]).astype(jnp.int32), axis=1)
    return block, order, sorted_langs, starts


def combine(plan, back, lang_count):
    block, order, sorted_langs, starts = plan
    members, row_count, bottleneck = back.shape
    grid_spec = pltpu.PrefetchScalarGridSpec(
        num_scalar_prefetch=3,
        grid=(lang_count // block,),
        in_specs=[pl.BlockSpec((members, row_count, bottleneck), lambda b, o, l, st: (0, 0, 0))],
        out_specs=pl.BlockSpec((block, row_count, bottleneck), lambda b, o, l, st: (b, 0, 0)),
        scratch_shapes=[pltpu.VMEM((row_count, bottleneck), jnp.float32)],
    )
    return pl.pallas_call(
        combine_kernel,
        grid_spec=grid_spec,
        out_shape=jax.ShapeDtypeStruct((lang_count, row_count, bottleneck), jnp.bfloat16),
        compiler_params=pltpu.CompilerParams(
            dimension_semantics=("arbitrary",), vmem_limit_bytes=48 * 1024 * 1024
        ),
        cost_estimate=pl.CostEstimate(
            flops=back.size, bytes_accessed=back.size * 2 + lang_count * row_count * bottleneck * 2,
            transcendentals=0,
        ),
    )(order, sorted_langs, starts, back)


def gather_kernel(lang_ref, weight_hbm, out_ref, sems, *, slots):
    members = lang_ref.shape[0]

    def copy(m):
        return pltpu.make_async_copy(
            weight_hbm.at[lang_ref[m]], out_ref.at[m // slots, m % slots], sems.at[m]
        )

    def start(m, carry):
        copy(m).start()
        return carry

    def finish(m, carry):
        copy(m).wait()
        return carry

    lax.fori_loop(0, members, start, 0)
    lax.fori_loop(0, members, finish, 0)


def gather_rows(slot_lang, weight):
    devices, slots = slot_lang.shape
    _, row_count, bottleneck = weight.shape
    members = devices * slots
    grid_spec = pltpu.PrefetchScalarGridSpec(
        num_scalar_prefetch=1,
        grid=(1,),
        in_specs=[pl.BlockSpec(memory_space=pl.ANY)],
        out_specs=pl.BlockSpec((devices, slots, row_count, bottleneck), lambda i, ml: (0, 0, 0, 0)),
        scratch_shapes=[pltpu.SemaphoreType.DMA((members,))],
    )
    size = members * row_count * bottleneck * 2
    return pl.pallas_call(
        functools.partial(gather_kernel, slots=slots),
        grid_spec=grid_spec,
        out_shape=jax.ShapeDtypeStruct((devices, slots, row_count, bottleneck), jnp.bfloat16),
        compiler_params=pltpu.CompilerParams(vmem_limit_bytes=48 * 1024 * 1024),
        cost_estimate=pl.CostEstimate(flops=0, bytes_accessed=2 * size, transcendentals=0),
    )(slot_lang.reshape(-1), weight)


def _layouts(got):
    devices, slots, row_count, bottleneck = got.shape
    width = devices * row_count
    direct = row_count % 16 == 0
    if direct:
        weights = got
        w_spec = pl.BlockSpec((devices, 1, row_count, bottleneck), lambda u, sl, ln: (0, sl[u], 0, 0))
        g_shape = (devices, slots, row_count, bottleneck)
        g_spec = pl.BlockSpec(g_shape, lambda u, sl, ln: (0, 0, 0, 0))
    else:
        weights = got.transpose(1, 0, 2, 3).reshape(slots, width, bottleneck)
        w_spec = pl.BlockSpec((1, width, bottleneck), lambda u, sl, ln: (sl[u], 0, 0))
        g_shape = (slots, width, bottleneck)
        g_spec = pl.BlockSpec(g_shape, lambda u, sl, ln: (0, 0, 0))
    return direct, weights, w_spec, g_shape, g_spec


def _to_send(grads, got_shape, direct):
    if direct:
        return grads
    devices, slots, row_count, bottleneck = got_shape
    return grads.reshape(slots, devices, row_count, bottleneck).transpose(1, 0, 2, 3)


def _utt_spec(frame_count, width):
    return pl.BlockSpec((1, frame_count, width), lambda u, sl, ln: (u, 0, 0))


def forward_pass(frames, cotangent, gain, got_down, own_slot, own_lengths, own_scale):
    utts, frame_count, width = frames.shape
    slots, bottleneck = got_down.shape[1], got_down.shape[3]
    direct, w_down, w_spec, g_shape, g_spec = _layouts(got_down)
    grid_spec = pltpu.PrefetchScalarGridSpec(
        num_scalar_prefetch=2,
        grid=(utts,),
        in_specs=[
            _utt_spec(frame_count, width),
            _utt_spec(frame_count, width),
            pl.BlockSpec((1, width), lambda u, sl, ln: (0, 0)),
            w_spec,
            pl.BlockSpec((slots, 1, 1), lambda u, sl, ln: (0, 0, 0)),
        ],
        out_specs=[
            pl.BlockSpec((1, frame_count, bottleneck), lambda u, sl, ln: (u, 0, 0)),
            g_spec,
        ],
        scratch_shapes=[pltpu.VMEM((slots, width, bottleneck), jnp.float32)],
    )
    pre_act, grads = pl.pallas_call(
        functools.partial(forward_kernel, direct=direct),
        grid_spec=grid_spec,
        out_shape=[
            jax.ShapeDtypeStruct((utts, frame_count, bottleneck), jnp.float32),
            jax.ShapeDtypeStruct(g_shape, jnp.bfloat16),
        ],
        compiler_params=pltpu.CompilerParams(
            dimension_semantics=("arbitrary",), vmem_limit_bytes=60 * 1024 * 1024
        ),
        cost_estimate=pl.CostEstimate(
            flops=4 * utts * frame_count * width * bottleneck,
            bytes_accessed=2 * frames.size * 2 + utts * width * bottleneck * 2,
            transcendentals=utts * frame_count * bottleneck,
        ),
    )(own_slot, own_lengths, frames, cotangent, gain.reshape(1, width), w_down,
      own_scale.reshape(slots, 1, 1))
    return pre_act, _to_send(grads, got_down.shape, direct)


def backward_pass(frames, cotangent, gain, got_down, got_up, pre_act, own_slot, own_lengths,
                  own_scale):
    utts, frame_count, width = frames.shape
    slots, bottleneck = got_down.shape[1], got_down.shape[3]
    direct, w_down, w_spec, g_shape, g_spec = _layouts(got_down)
    _, w_up, _, _, _ = _layouts(got_up)
    grid_spec = pltpu.PrefetchScalarGridSpec(
        num_scalar_prefetch=2,
        grid=(utts,),
        in_specs=[
            _utt_spec(frame_count, width),
            _utt_spec(frame_count, width),
            pl.BlockSpec((1, width), lambda u, sl, ln: (0, 0)),
            w_spec,
            w_spec,
            pl.BlockSpec((1, frame_count, bottleneck), lambda u, sl, ln: (u, 0, 0)),
            pl.BlockSpec((slots, 1, 1), lambda u, sl, ln: (0, 0, 0)),
        ],
        out_specs=[_utt_spec(frame_count, width), g_spec],
        scratch_shapes=[pltpu.VMEM((slots, width, bottleneck), jnp.float32)],
    )
    d_frames, grads = pl.pallas_call(
        functools.partial(backward_kernel, direct=direct),
        grid_spec=grid_spec,
        out_shape=[
            jax.ShapeDtypeStruct(frames.shape, jnp.bfloat16),
            jax.ShapeDtypeStruct(g_shape, jnp.bfloat16),
        ],
        compiler_params=pltpu.CompilerParams(
            dimension_semantics=("arbitrary",), vmem_limit_bytes=60 * 1024 * 1024
        ),
        cost_estimate=pl.CostEstimate(
            flops=6 * utts * frame_count * width * bottleneck,
            bytes_accessed=3 * frames.size * 2 + 2 * utts * width * bottleneck * 2,
            transcendentals=utts * frame_count * bottleneck,
        ),
    )(own_slot, own_lengths, frames, cotangent, gain.reshape(1, width), w_down, w_up, pre_act,
      own_scale.reshape(slots, 1, 1))
    return d_frames, _to_send(grads, got_down.shape, direct)


def on_device(frames, cotangent, gain, down_weight, up_weight, slot_lang, utt_slot, lengths):
    devices = lax.axis_size("dp")
    self_index = lax.axis_index("dp")
    per_device = frames.shape[0]
    slots = slot_lang.shape[1]
    lang_count, row_count, bottleneck = down_weight.shape
    owners = jnp.arange(utt_slot.shape[0], dtype=jnp.int32) // per_device
    utt_lang = slot_lang[owners, utt_slot]
    own_lengths = lax.dynamic_slice_in_dim(lengths, self_index * per_device, per_device)
    own_slot = lax.dynamic_slice_in_dim(utt_slot, self_index * per_device, per_device)
    lang_ids = jnp.arange(lang_count, dtype=jnp.int32)
    counts = jnp.sum(jnp.where(utt_lang[None, :] == lang_ids[:, None], lengths[None, :], 0), axis=1)
    scaling = lax.rsqrt(jnp.maximum(counts, 1).astype(jnp.float32))
    member_langs = slot_lang.reshape(-1)
    own_scale = jnp.take(scaling, lax.dynamic_index_in_dim(slot_lang, self_index, 0, False))
    exchange = functools.partial(lax.all_to_all, axis_name="dp", split_axis=0, concat_axis=0, tiled=True)
    got_down = exchange(gather_rows(slot_lang, down_weight))
    got_up = exchange(gather_rows(slot_lang, up_weight))
    pre_act, send_up = forward_pass(
        frames, cotangent, gain, got_down, own_slot, own_lengths, own_scale
    )
    back_up = exchange(send_up).reshape(devices * slots, row_count, bottleneck)
    d_frames, send_down = backward_pass(
        frames, cotangent, gain, got_down, got_up, pre_act, own_slot, own_lengths, own_scale
    )
    send_down, back_up = lax.optimization_barrier((send_down, back_up))
    back_down = exchange(send_down).reshape(devices * slots, row_count, bottleneck)
    plan = combine_plan(slot_lang, lang_count)
    up_grads = combine(plan, back_up, lang_count)
    down_grads = combine(plan, back_down, lang_count)
    return (d_frames, down_grads, up_grads)


def solution(mesh):
    placed = (
        P(("groups", "dp"), None, None),
        P(("groups", "dp"), None, None),
        P(),
        P("groups", "dp", None),
        P("groups", "dp", None),
        P("groups", None),
        P("groups"),
        P("groups"),
    )
    return jax.shard_map(
        on_device,
        mesh=mesh,
        in_specs=placed,
        out_specs=(
            P(("groups", "dp"), None, None),
            P("groups", "dp", None),
            P("groups", "dp", None),
        ),
        check_vma=False,
    )
```

time: 205 us -> 178 us (0.87)
  waiting for transfers between devices: 126 us -> 107 us
  local copies, waits for them, and re-layouts: 20.4 us -> 6.36 us
  starting transfers between devices: 16.7 us -> 21.3 us
    all_to_all x3 -> x4, waiting for transfers between devices: 126 us -> 107 us  [the longest x1 32.5 us: on_device(): got_down = exchange(gather_rows(slot_lang, down_weight))]
    pallas_call x1 -> x4, Pallas kernels: 16.1 us -> 29.7 us  [the longest x1 12.6 us: backward_pass(): pl.pallas_call(functools.partial(backward_kernel, direct=direct), grid_sp...]
    pallas_call x2, Pallas kernels: 21.3 us -> 9.49 us  [combine(): pl.pallas_call(combine_kernel, grid_spec=grid_spec, out_shape=jax.ShapeDt...]
    gather x2 -> x1, local copies, waits for them, and re-layouts: 7.76 us -> 0.7 us  [combine_plan(): sorted_langs = langs[order].astype(jnp.int32)]
    all_to_all x3 -> x4, starting transfers between devices: 16.7 us -> 21.3 us  [the longest x1 6.57 us: on_device(): got_down = exchange(gather_rows(slot_lang, down_weight))]
    reshape x4 -> x2, local copies, waits for them, and re-layouts: 4.63 us -> 0.69 us  [the longest x1 0.6 us: backward_pass(): gain.reshape(1, width)]
  transfers between devices with their start and end apart: 3 -> 4, of which waited for: 3 -> 4; matrix products, arithmetic and copies ran while one was open for 3% -> 4% of each run, Pallas kernels for 5% -> 17%
where the time goes in v8:
time: 178 us; the launch traced here: 177 us
  waiting for transfers between devices  107 us (60%)
  Pallas kernels  39.2 us (22%)
  starting transfers between devices  21.3 us (12%)
  local copies, waits for them, and re-layouts  6.36 us (4%)
  other arithmetic  2.48 us (1%)
    all_to_all x1, waiting for transfers between devices, on_device(): got_down = exchange(gather_rows(slot_lang, down_weight))  32.5 us
    all_to_all x1, waiting for transfers between devices, on_device(): exchange(send_down).reshape(devices * slots, row_count, bottleneck)  28.9 us
    all_to_all x1, waiting for transfers between devices, on_device(): back_up = exchange(send_up).reshape(devices * slots, row_count, bottleneck)  23.6 us
    all_to_all x1, waiting for transfers between devices, on_device(): got_up = exchange(gather_rows(slot_lang, up_weight))  22 us
    pallas_call x1, Pallas kernels, backward_pass(): pl.pallas_call(functools.partial(backward_kernel, direct=direct), grid_sp...  12.6 us
    pallas_call x1, Pallas kernels, forward_pass(): pl.pallas_call(functools.partial(forward_kernel, direct=direct), grid_spe...  9.93 us
    pallas_call x2, Pallas kernels, combine(): pl.pallas_call(combine_kernel, grid_spec=grid_spec, out_shape=jax.ShapeDt...  9.49 us
    pallas_call x2, Pallas kernels, gather_rows(): pl.pallas_call(functools.partial(gather_kernel, slots=slots), grid_spec=g...  7.22 us
  transfers between devices with their start and end apart: 4, of which 4 were waited for; matrix products, arithmetic and copies ran while one was open for 4% of the time, Pallas kernels for 17%

profile of v8, /device:TPU:15, one launch (start us, length us, event | category | flops | bytes accessed | tf_op | source)
XLA Modules:
  0.0 177.1 jit_solution(4708061486919283081)
XLA Ops:
  0.6 0.8 copy.21
  1.5 3.6 %shard_map.103 = bf16[16,2,96,256]{3,2,1,0:T(8,128)(2,1)} custom-call(s32[32]{0:T(128)S(1)} %reshape.152.lang_ref, bf16[160,96,256]{2,1,0:T(8,128)(2,1)} %weight_hbm.2), custom_call_target="tpu_custom_call" | custom-call | bytes 3145728 | tf_op jit(solution)/shard_map/pallas_call | solution.py:207
  5.1 6.6 %all-to-all-start = ((bf16[16,2,96,256]{3,2,1,0:T(8,128)(2,1)}), bf16[16,2,96,256]{3,2,1,0:T(8,128)(2,1)S(1)}, u32[]{:S(2)}, u32[]{:S(2)}) async-start(bf16[16,2,96,256]{3,2,1,0:T(8,128)(2,1)} %shard_map.103), calls=%async_computation | async-start | bytes 3145728 | tf_op jit(solution)/shard_map/all_to_all | solution.py:341
  11.7 3.6 %shard_map.104 = bf16[16,2,96,256]{3,2,1,0:T(8,128)(2,1)} custom-call(s32[32]{0:T(128)S(1)} %reshape.152.lang_ref, bf16[160,96,256]{2,1,0:T(8,128)(2,1)} %weight_hbm.3), custom_call_target="tpu_custom_call" | custom-call | bytes 3145728 | tf_op jit(solution)/shard_map/pallas_call | solution.py:207
  15.3 32.5 %all-to-all-done.wd_ref = bf16[16,2,96,256]{3,2,1,0:T(8,128)(2,1)S(1)} async-done(((bf16[16,2,96,256]{3,2,1,0:T(8,128)(2,1)}), bf16[16,2,96,256]{3,2,1,0:T(8,128)(2,1)S(1)}, u32[]{:S(2)}, u32[]{:S(2)}) %all-to-all-start) | async-done | bytes 1572896 | tf_op jit(solution)/shard_map/all_to_all | solution.py:341
  47.9 1.1 copy-done.1
  49.0 4.9 %all-to-all-start.1 = ((bf16[16,2,96,256]{3,2,1,0:T(8,128)(2,1)}), bf16[16,2,96,256]{3,2,1,0:T(8,128)(2,1)}, u32[]{:S(2)}, u32[]{:S(2)}) async-start(bf16[16,2,96,256]{3,2,1,0:T(8,128)(2,1)} %shard_map.104), calls=%async_computation.1 | async-start | bytes 3145728 | tf_op jit(solution)/shard_map/all_to_all | solution.py:342
  53.9 0.7 dynamic_slice.10.slot_ref
  54.6 0.6 dynamic_slice.11.len_ref
  55.2 0.9 gather_fusion
  56.4 0.6 gather_fusion.1
  57.1 0.6 reshape.151.gain_ref
  57.7 0.5 and_select_fusion.scale_ref
  58.3 9.9 %shard_map.105 = (f32[4,256,256]{2,1,0:T(8,128)}, bf16[16,2,96,256]{3,2,1,0:T(8,128)(2,1)}) custom-call(s32[4]{0:T(128)} %dynamic_slice.10.slot_ref, s32[4]{0:T(128)} %dynamic_slice.11.len_ref, bf16[4,256,1536]{2,1,0:T(8,128)(2,1)} %frames_ref.3, bf16[4,256,1536]{2,1,0:T(8,128)(2,1)} %cot_ref.3, f32[1,1536]{1,0:T(1,128)} %reshape.151.gain_ref, ...), custom_call_target="tpu_custom_call" | custom-call | flops 1610612736 | bytes 9437184 | tf_op jit(solution)/shard_map/pallas_call | solution.py:264
  68.2 22.0 %all-to-all-done.1.wu_ref = bf16[16,2,96,256]{3,2,1,0:T(8,128)(2,1)} async-done(((bf16[16,2,96,256]{3,2,1,0:T(8,128)(2,1)}), bf16[16,2,96,256]{3,2,1,0:T(8,128)(2,1)}, u32[]{:S(2)}, u32[]{:S(2)}) %all-to-all-start.1) | async-done | bytes 1572896 | tf_op jit(solution)/shard_map/all_to_all | solution.py:342
  90.2 4.9 %all-to-all-start.2 = ((bf16[16,2,96,256]{3,2,1,0:T(8,128)(2,1)}), bf16[16,2,96,256]{3,2,1,0:T(8,128)(2,1)S(1)}, u32[]{:S(2)}, u32[]{:S(2)}) async-start(bf16[16,2,96,256]{3,2,1,0:T(8,128)(2,1)} %get-tuple-element.14), calls=%async_computation.2 | async-start | bytes 3145728 | tf_op jit(solution)/shard_map/all_to_all | solution.py:346
  95.1 12.6 %shard_map.106 = (bf16[4,256,1536]{2,1,0:T(8,128)(2,1)}, bf16[16,2,96,256]{3,2,1,0:T(8,128)(2,1)}) custom-call(s32[4]{0:T(128)} %dynamic_slice.10.slot_ref, s32[4]{0:T(128)} %dynamic_slice.11.len_ref, bf16[4,256,1536]{2,1,0:T(8,128)(2,1)} %frames_ref.3, bf16[4,256,1536]{2,1,0:T(8,128)(2,1)} %cot_ref.3, f32[1,1536]{1,0:T(1,128)} %reshape.151.gain_ref, ...), custom_call_target="tpu_custom_call" | custom-call | flops 2415919104 | bytes 15728640 | tf_op jit(solution)/shard_map/pallas_call | solution.py:305
  107.7 23.6 %all-to-all-done.2 = bf16[16,2,96,256]{3,2,1,0:T(8,128)(2,1)S(1)} async-done(((bf16[16,2,96,256]{3,2,1,0:T(8,128)(2,1)}), bf16[16,2,96,256]{3,2,1,0:T(8,128)(2,1)S(1)}, u32[]{:S(2)}, u32[]{:S(2)}) %all-to-all-start.2) | async-done | bytes 1572896 | tf_op jit(solution)/shard_map/all_to_all | solution.py:346
  131.3 4.9 %all-to-all-start.3 = ((bf16[16,2,96,256]{3,2,1,0:T(8,128)(2,1)}), bf16[16,2,96,256]{3,2,1,0:T(8,128)(2,1)S(1)}, u32[]{:S(2)}, u32[]{:S(2)}) async-start(bf16[16,2,96,256]{3,2,1,0:T(8,128)(2,1)} %get-tuple-element.15), calls=%async_computation.3 | async-start | bytes 3145728 | tf_op jit(solution)/shard_map/all_to_all | solution.py:351
  136.2 1.6 sort.17
  137.8 0.7 gather_fusion.2
  138.7 4.8 %shard_map.108 = bf16[160,96,256]{2,1,0:T(8,128)(2,1)} custom-call(s32[32]{0:T(128)S(1)} %get-tuple-element.12.order_ref, s32[32]{0:T(128)S(1)} %gather_fusion.2, s32[6]{0:T(128)S(1)} %convert_reduce_fusion.start_ref, bf16[32,96,256]{2,1,0:T(8,128)(2,1)S(1)} %bitcast.14), custom_call_target="tpu_custom_call" | custom-call | flops 786432 | bytes 9437184 | tf_op jit(solution)/shard_map/pallas_call | solution.py:161
  143.5 28.9 %all-to-all-done.3 = bf16[16,2,96,256]{3,2,1,0:T(8,128)(2,1)S(1)} async-done(((bf16[16,2,96,256]{3,2,1,0:T(8,128)(2,1)}), bf16[16,2,96,256]{3,2,1,0:T(8,128)(2,1)S(1)}, u32[]{:S(2)}, u32[]{:S(2)}) %all-to-all-start.3) | async-done | bytes 1572896 | tf_op jit(solution)/shard_map/all_to_all | solution.py:351
  172.4 4.7 %shard_map.107 = bf16[160,96,256]{2,1,0:T(8,128)(2,1)} custom-call(s32[32]{0:T(128)S(1)} %get-tuple-element.12.order_ref, s32[32]{0:T(128)S(1)} %gather_fusion.2, s32[6]{0:T(128)S(1)} %convert_reduce_fusion.start_ref, bf16[32,96,256]{2,1,0:T(8,128)(2,1)S(1)} %bitcast.15), custom_call_target="tpu_custom_call" | custom-call | flops 786432 | bytes 9437184 | tf_op jit(solution)/shard_map/pallas_call | solution.py:161
  (22 shorter events, 0.7 us)
Async XLA Ops:
  5.1 42.8 %all-to-all-start = ((bf16[16,2,96,256]{3,2,1,0:T(8,128)(2,1)}), bf16[16,2,96,256]{3,2,1,0:T(8,128)(2,1)S(1)}, u32[]{:S(2)}, u32[]{:S(2)}) async-start(bf16[16,2,96,256]{3,2,1,0:T(8,128)(2,1)} %shard_map.103), calls=%async_computation | async-start | bytes 3145728 | tf_op jit(solution)/shard_map/all_to_all | solution.py:341
  15.3 38.6 %copy-start.4 = (s32[64]{0:T(128)S(1)}, s32[64]{0:T(128)}, u32[]{:S(2)}) copy-start(s32[64]{0:T(128)} %param.14) | copy-start | bytes 772
  15.3 39.3 %copy-start.3 = (s32[64]{0:T(128)S(1)}, s32[64]{0:T(128)}, u32[]{:S(2)}) copy-start(s32[64]{0:T(128)} %param.15) | copy-start | bytes 772
  15.3 39.9 %copy-start = (s32[16,2]{0,1:T(2,128)S(1)}, s32[16,2]{0,1:T(2,128)}, u32[]{:S(2)}) copy-start(s32[16,2]{0,1:T(2,128)} %param.13) | copy-start | bytes 388
  15.3 41.8 %copy-start.2 = (f32[1536]{0:T(1024)S(1)}, f32[1536]{0:T(1024)}, u32[]{:S(2)}) copy-start(f32[1536]{0:T(1024)} %param.10) | copy-start | bytes 18436
  47.9 1.1 copy-start.1
  49.0 41.2 %all-to-all-start.1 = ((bf16[16,2,96,256]{3,2,1,0:T(8,128)(2,1)}), bf16[16,2,96,256]{3,2,1,0:T(8,128)(2,1)}, u32[]{:S(2)}, u32[]{:S(2)}) async-start(bf16[16,2,96,256]{3,2,1,0:T(8,128)(2,1)} %shard_map.104), calls=%async_computation.1 | async-start | bytes 3145728 | tf_op jit(solution)/shard_map/all_to_all | solution.py:342
  90.2 41.1 %all-to-all-start.2 = ((bf16[16,2,96,256]{3,2,1,0:T(8,128)(2,1)}), bf16[16,2,96,256]{3,2,1,0:T(8,128)(2,1)S(1)}, u32[]{:S(2)}, u32[]{:S(2)}) async-start(bf16[16,2,96,256]{3,2,1,0:T(8,128)(2,1)} %get-tuple-element.14), calls=%async_computation.2 | async-start | bytes 3145728 | tf_op jit(solution)/shard_map/all_to_all | solution.py:346
  131.3 41.1 %all-to-all-start.3 = ((bf16[16,2,96,256]{3,2,1,0:T(8,128)(2,1)}), bf16[16,2,96,256]{3,2,1,0:T(8,128)(2,1)S(1)}, u32[]{:S(2)}, u32[]{:S(2)}) async-start(bf16[16,2,96,256]{3,2,1,0:T(8,128)(2,1)} %get-tuple-element.15), calls=%async_computation.3 | async-start | bytes 3145728 | tf_op jit(solution)/shard_map/all_to_all | solution.py:351

commit v9 on v8

--- a/solution.py
+++ b/solution.py
@@ -322,6 +322,20 @@
     return d_frames, _to_send(grads, got_down.shape, direct)
 
 
+def exchange_blocks(x, axis):
+    n = x.shape[0]
+    if n > 16:
+        return lax.all_to_all(x, axis, split_axis=0, concat_axis=0, tiled=True)
+    me = lax.axis_index(axis)
+    ahead = jnp.take(x, (me + jnp.arange(n, dtype=jnp.int32)) % n, axis=0)
+    parts = [ahead[0]]
+    for shift in range(1, n):
+        pairs = [(j, (j + shift) % n) for j in range(n)]
+        parts.append(lax.ppermute(ahead[shift], axis, perm=pairs))
+    behind = jnp.stack(parts)
+    return jnp.take(behind, (me - jnp.arange(n, dtype=jnp.int32)) % n, axis=0)
+
+
 def on_device(frames, cotangent, gain, down_weight, up_weight, slot_lang, utt_slot, lengths):
     devices = lax.axis_size("dp")
     self_index = lax.axis_index("dp")
@@ -337,7 +351,7 @@
     scaling = lax.rsqrt(jnp.maximum(counts, 1).astype(jnp.float32))
     member_langs = slot_lang.reshape(-1)
     own_scale = jnp.take(scaling, lax.dynamic_index_in_dim(slot_lang, self_index, 0, False))
-    exchange = functools.partial(lax.all_to_all, axis_name="dp", split_axis=0, concat_axis=0, tiled=True)
+    exchange = functools.partial(exchange_blocks, axis="dp")
     got_down = exchange(gather_rows(slot_lang, down_weight))
     got_up = exchange(gather_rows(slot_lang, up_weight))
     pre_act, send_up = forward_pass(

time: 178 us -> 363 us (2.04)
  starting transfers between devices: 21.3 us -> 118 us
  waiting for transfers between devices: 107 us -> 161 us
  local copies, waits for them, and re-layouts: 6.36 us -> 34.2 us
  other arithmetic: 2.48 us -> 9.7 us
    ppermute x0 -> x60, waiting for transfers between devices: none -> 161 us  [exchange_blocks(): parts.append(lax.ppermute(ahead[shift], axis, perm=pairs))]
    ppermute x0 -> x60, starting transfers between devices: none -> 118 us  [exchange_blocks(): parts.append(lax.ppermute(ahead[shift], axis, perm=pairs))]
    all_to_all x4 -> x0, waiting for transfers between devices: 107 us -> none  [the longest x1 32.5 us: on_device(): got_down = exchange(gather_rows(slot_lang, down_weight))]
    all_to_all x4 -> x0, starting transfers between devices: 21.3 us -> none  [the longest x1 6.57 us: on_device(): got_down = exchange(gather_rows(slot_lang, down_weight))]
    gather x0 -> x8, local copies, waits for them, and re-layouts: none -> 12 us  [the longest x4 6.55 us: exchange_blocks(): return jnp.take(behind, (me - jnp.arange(n, dtype=jnp.int32)) % n, axis=0)]
    unnamed x11 -> x79, local copies, waits for them, and re-layouts: 1.93 us -> 13.8 us
    select_n x0 -> x8, other arithmetic: none -> 5.26 us  [the longest x4 4.48 us: exchange_blocks(): return jnp.take(behind, (me - jnp.arange(n, dtype=jnp.int32)) % n, axis=0)]
  transfers between devices with their start and end apart: 4 -> 60, of which waited for: 4 -> 42; matrix products, arithmetic and copies ran while one was open for 4% -> 7% of each run, Pallas kernels for 17% -> 2%
where the time goes in v9:
time: 363 us; the launch traced here: 360 us
  waiting for transfers between devices  161 us (44%)
  starting transfers between devices  118 us (33%)
  Pallas kernels  36.9 us (10%)
  local copies, waits for them, and re-layouts  34.2 us (9%)
  other arithmetic  9.7 us (3%)
    ppermute x60, waiting for transfers between devices, exchange_blocks(): parts.append(lax.ppermute(ahead[shift], axis, perm=pairs))  161 us
    ppermute x60, starting transfers between devices, exchange_blocks(): parts.append(lax.ppermute(ahead[shift], axis, perm=pairs))  118 us
    unnamed x79, local copies, waits for them, and re-layouts  13.8 us
    pallas_call x1, Pallas kernels, backward_pass(): pl.pallas_call(functools.partial(backward_kernel, direct=direct), grid_sp...  12.7 us
    pallas_call x1, Pallas kernels, forward_pass(): pl.pallas_call(functools.partial(forward_kernel, direct=direct), grid_spe...  10.1 us
    pallas_call x2, Pallas kernels, combine(): pl.pallas_call(combine_kernel, grid_spec=grid_spec, out_shape=jax.ShapeDt...  9.55 us
  transfers between devices with their start and end apart: 60, of which 42 were waited for; matrix products, arithmetic and copies ran while one was open for 7% of the time, Pallas kernels for 2%

profile of v9, /device:TPU:15, one launch (start us, length us, event | category | flops | bytes accessed | tf_op | source)
XLA Modules:
  0.0 360.5 jit_solution(12488197568361854621)
XLA Ops:
  39.7 5.2 %collective-permute-start.4 = (bf16[2,96,256]{2,1,0:T(8,128)(2,1)}, bf16[2,96,256]{2,1,0:T(8,128)(2,1)S(1)}, u32[]{:S(2)}, u32[]{:S(2)}) collective-permute-start(bf16[2,96,256]{2,1,0:T(8,128)(2,1)} %get-tuple-element.78), channel_id=1, source_target_pairs={{0,5},{1,6},{2,7},{3,8},{4,9},{5,10},{6,11},{7,12},{8,13},{9,14},{... | collective-permute-start | bytes 294920 | tf_op jit(solution)/shard_map/ppermute | solution.py:334
  49.2 6.2 %collective-permute-done.5 = bf16[2,96,256]{2,1,0:T(8,128)(2,1)S(1)} collective-permute-done((bf16[2,96,256]{2,1,0:T(8,128)(2,1)}, bf16[2,96,256]{2,1,0:T(8,128)(2,1)S(1)}, u32[]{:S(2)}, u32[]{:S(2)}) %collective-permute-start.5) | collective-permute-done | bytes 98336 | tf_op jit(solution)/shard_map/ppermute | solution.py:334
  56.1 6.6 %collective-permute-done.6 = bf16[2,96,256]{2,1,0:T(8,128)(2,1)S(1)} collective-permute-done((bf16[2,96,256]{2,1,0:T(8,128)(2,1)}, bf16[2,96,256]{2,1,0:T(8,128)(2,1)S(1)}, u32[]{:S(2)}, u32[]{:S(2)}) %collective-permute-start.6) | collective-permute-done | bytes 98336 | tf_op jit(solution)/shard_map/ppermute | solution.py:334
  63.4 5.1 %collective-permute-done.7 = bf16[2,96,256]{2,1,0:T(8,128)(2,1)S(1)} collective-permute-done((bf16[2,96,256]{2,1,0:T(8,128)(2,1)}, bf16[2,96,256]{2,1,0:T(8,128)(2,1)S(1)}, u32[]{:S(2)}, u32[]{:S(2)}) %collective-permute-start.7) | collective-permute-done | bytes 98336 | tf_op jit(solution)/shard_map/ppermute | solution.py:334
  80.2 5.5 %collective-permute-start.10 = (bf16[2,96,256]{2,1,0:T(8,128)(2,1)S(1)}, bf16[2,96,256]{2,1,0:T(8,128)(2,1)S(1)}, u32[]{:S(2)}, u32[]{:S(2)}) collective-permute-start(bf16[2,96,256]{2,1,0:T(8,128)(2,1)S(1)} %copy-done.2), channel_id=1, source_target_pairs={{0,11},{1,12},{2,13},{3,14},{4,15},{5,0},{6,1},{7,2},{8,3},{9,4},{... | collective-permute-start | bytes 294920 | tf_op jit(solution)/shard_map/ppermute | solution.py:334
  99.4 10.1 %shard_map.105 = (f32[4,256,256]{2,1,0:T(8,128)}, bf16[16,2,96,256]{3,2,1,0:T(8,128)(2,1)}) custom-call(s32[4]{0:T(128)} %dynamic_slice.10.slot_ref, s32[4]{0:T(128)} %dynamic_slice.11.len_ref, bf16[4,256,1536]{2,1,0:T(8,128)(2,1)} %frames_ref.3, bf16[4,256,1536]{2,1,0:T(8,128)(2,1)} %cot_ref.3, f32[1,1536]{1,0:T(1,128)} %reshape.156.gain_ref, ...), custom_call_target="tpu_custom_call" | custom-call | flops 1610612736 | bytes 9437184 | tf_op jit(solution)/shard_map/pallas_call | solution.py:264
  137.2 4.7 %collective-permute-start.34 = (bf16[2,96,256]{2,1,0:T(8,128)(2,1)S(1)}, bf16[2,96,256]{2,1,0:T(8,128)(2,1)S(1)}, u32[]{:S(2)}, u32[]{:S(2)}) collective-permute-start(bf16[2,96,256]{2,1,0:T(8,128)(2,1)S(1)} %get-tuple-element.46), channel_id=1, source_target_pairs={{0,5},{1,6},{2,7},{3,8},{4,9},{5,10},{6,11},{7,12},{8,13},{9,14},{... | collective-permute-start | bytes 294920 | tf_op jit(solution)/shard_map/ppermute | solution.py:334
  151.8 6.5 %collective-permute-done.36 = bf16[2,96,256]{2,1,0:T(8,128)(2,1)S(1)} collective-permute-done((bf16[2,96,256]{2,1,0:T(8,128)(2,1)S(1)}, bf16[2,96,256]{2,1,0:T(8,128)(2,1)S(1)}, u32[]{:S(2)}, u32[]{:S(2)}) %collective-permute-start.36) | collective-permute-done | bytes 98336 | tf_op jit(solution)/shard_map/ppermute | solution.py:334
  158.3 5.2 %collective-permute-done.37 = bf16[2,96,256]{2,1,0:T(8,128)(2,1)S(1)} collective-permute-done((bf16[2,96,256]{2,1,0:T(8,128)(2,1)S(1)}, bf16[2,96,256]{2,1,0:T(8,128)(2,1)S(1)}, u32[]{:S(2)}, u32[]{:S(2)}) %collective-permute-start.37) | collective-permute-done | bytes 98336 | tf_op jit(solution)/shard_map/ppermute | solution.py:334
  170.1 5.0 %collective-permute-done.39 = bf16[2,96,256]{2,1,0:T(8,128)(2,1)S(1)} collective-permute-done((bf16[2,96,256]{2,1,0:T(8,128)(2,1)S(1)}, bf16[2,96,256]{2,1,0:T(8,128)(2,1)S(1)}, u32[]{:S(2)}, u32[]{:S(2)}) %collective-permute-start.39) | collective-permute-done | bytes 98336 | tf_op jit(solution)/shard_map/ppermute | solution.py:334
  175.2 5.3 %collective-permute-start.40 = (bf16[2,96,256]{2,1,0:T(8,128)(2,1)S(1)}, bf16[2,96,256]{2,1,0:T(8,128)(2,1)S(1)}, u32[]{:S(2)}, u32[]{:S(2)}) collective-permute-start(bf16[2,96,256]{2,1,0:T(8,128)(2,1)S(1)} %get-tuple-element.40), channel_id=1, source_target_pairs={{0,11},{1,12},{2,13},{3,14},{4,15},{5,0},{6,1},{7,2},{8,3},{9,4},{... | collective-permute-start | bytes 294920 | tf_op jit(solution)/shard_map/ppermute | solution.py:334
  224.1 6.7 %collective-permute-done.21 = bf16[2,96,256]{2,1,0:T(8,128)(2,1)S(1)} collective-permute-done((bf16[2,96,256]{2,1,0:T(8,128)(2,1)S(1)}, bf16[2,96,256]{2,1,0:T(8,128)(2,1)S(1)}, u32[]{:S(2)}, u32[]{:S(2)}) %collective-permute-start.21) | collective-permute-done | bytes 98336 | tf_op jit(solution)/shard_map/ppermute | solution.py:334
  230.8 5.0 %collective-permute-done.22 = bf16[2,96,256]{2,1,0:T(8,128)(2,1)S(1)} collective-permute-done((bf16[2,96,256]{2,1,0:T(8,128)(2,1)S(1)}, bf16[2,96,256]{2,1,0:T(8,128)(2,1)S(1)}, u32[]{:S(2)}, u32[]{:S(2)}) %collective-permute-start.22) | collective-permute-done | bytes 98336 | tf_op jit(solution)/shard_map/ppermute | solution.py:334
  242.6 5.0 %collective-permute-done.24 = bf16[2,96,256]{2,1,0:T(8,128)(2,1)S(1)} collective-permute-done((bf16[2,96,256]{2,1,0:T(8,128)(2,1)S(1)}, bf16[2,96,256]{2,1,0:T(8,128)(2,1)S(1)}, u32[]{:S(2)}, u32[]{:S(2)}) %collective-permute-start.24) | collective-permute-done | bytes 98336 | tf_op jit(solution)/shard_map/ppermute | solution.py:334
  247.6 5.2 %collective-permute-start.25 = (bf16[2,96,256]{2,1,0:T(8,128)(2,1)S(1)}, bf16[2,96,256]{2,1,0:T(8,128)(2,1)S(1)}, u32[]{:S(2)}, u32[]{:S(2)}) collective-permute-start(bf16[2,96,256]{2,1,0:T(8,128)(2,1)S(1)} %get-tuple-element.56), channel_id=1, source_target_pairs={{0,11},{1,12},{2,13},{3,14},{4,15},{5,0},{6,1},{7,2},{8,3},{9,4},{... | collective-permute-start | bytes 294920 | tf_op jit(solution)/shard_map/ppermute | solution.py:334
  263.6 12.7 %shard_map.106 = (bf16[4,256,1536]{2,1,0:T(8,128)(2,1)}, bf16[16,2,96,256]{3,2,1,0:T(8,128)(2,1)}) custom-call(s32[4]{0:T(128)} %dynamic_slice.10.slot_ref, s32[4]{0:T(128)} %dynamic_slice.11.len_ref, bf16[4,256,1536]{2,1,0:T(8,128)(2,1)} %frames_ref.3, bf16[4,256,1536]{2,1,0:T(8,128)(2,1)} %cot_ref.3, f32[1,1536]{1,0:T(1,128)} %reshape.156.gain_ref, ...), custom_call_target="tpu_custom_call" | custom-call | flops 2415919104 | bytes 15728640 | tf_op jit(solution)/shard_map/pallas_call | solution.py:305
  285.7 4.8 %shard_map.108 = bf16[160,96,256]{2,1,0:T(8,128)(2,1)} custom-call(s32[32]{0:T(128)S(1)} %get-tuple-element.13.order_ref, s32[32]{0:T(128)S(1)} %gather_fusion.2, s32[6]{0:T(128)S(1)} %convert_reduce_fusion.start_ref, bf16[32,96,256]{2,1,0:T(8,128)(2,1)S(1)} %bitcast.254), custom_call_target="tpu_custom_call" | custom-call | flops 786432 | bytes 9437184 | tf_op jit(solution)/shard_map/pallas_call | solution.py:161
  295.0 5.0 %collective-permute-done.47 = bf16[2,96,256]{2,1,0:T(8,128)(2,1)S(1)} collective-permute-done((bf16[2,96,256]{2,1,0:T(8,128)(2,1)S(1)}, bf16[2,96,256]{2,1,0:T(8,128)(2,1)S(1)}, u32[]{:S(2)}, u32[]{:S(2)}) %collective-permute-start.47) | collective-permute-done | bytes 98336 | tf_op jit(solution)/shard_map/ppermute | solution.py:334
  304.8 5.4 %collective-permute-start.49 = (bf16[2,96,256]{2,1,0:T(8,128)(2,1)S(1)}, bf16[2,96,256]{2,1,0:T(8,128)(2,1)S(1)}, u32[]{:S(2)}, u32[]{:S(2)}) collective-permute-start(bf16[2,96,256]{2,1,0:T(8,128)(2,1)S(1)} %get-tuple-element.30), channel_id=1, source_target_pairs={{0,5},{1,6},{2,7},{3,8},{4,9},{5,10},{6,11},{7,12},{8,13},{9,14},{... | collective-permute-start | bytes 294920 | tf_op jit(solution)/shard_map/ppermute | solution.py:334
  314.3 6.3 %collective-permute-done.50 = bf16[2,96,256]{2,1,0:T(8,128)(2,1)S(1)} collective-permute-done((bf16[2,96,256]{2,1,0:T(8,128)(2,1)S(1)}, bf16[2,96,256]{2,1,0:T(8,128)(2,1)S(1)}, u32[]{:S(2)}, u32[]{:S(2)}) %collective-permute-start.50) | collective-permute-done | bytes 98336 | tf_op jit(solution)/shard_map/ppermute | solution.py:334
  320.6 7.0 %collective-permute-done.51 = bf16[2,96,256]{2,1,0:T(8,128)(2,1)S(1)} collective-permute-done((bf16[2,96,256]{2,1,0:T(8,128)(2,1)S(1)}, bf16[2,96,256]{2,1,0:T(8,128)(2,1)S(1)}, u32[]{:S(2)}, u32[]{:S(2)}) %collective-permute-start.51) | collective-permute-done | bytes 98336 | tf_op jit(solution)/shard_map/ppermute | solution.py:334
  327.6 5.5 %collective-permute-done.52 = bf16[2,96,256]{2,1,0:T(8,128)(2,1)S(1)} collective-permute-done((bf16[2,96,256]{2,1,0:T(8,128)(2,1)S(1)}, bf16[2,96,256]{2,1,0:T(8,128)(2,1)S(1)}, u32[]{:S(2)}, u32[]{:S(2)}) %collective-permute-start.52) | collective-permute-done | bytes 98336 | tf_op jit(solution)/shard_map/ppermute | solution.py:334
  339.2 5.0 %collective-permute-start.54 = (bf16[2,96,256]{2,1,0:T(8,128)(2,1)S(1)}, bf16[2,96,256]{2,1,0:T(8,128)(2,1)S(1)}, u32[]{:S(2)}, u32[]{:S(2)}) collective-permute-start(bf16[2,96,256]{2,1,0:T(8,128)(2,1)S(1)} %get-tuple-element.25), channel_id=1, source_target_pairs={{0,10},{1,11},{2,12},{3,13},{4,14},{5,15},{6,0},{7,1},{8,2},{9,3},... | collective-permute-start | bytes 294920 | tf_op jit(solution)/shard_map/ppermute | solution.py:334
  355.7 4.8 %shard_map.107 = bf16[160,96,256]{2,1,0:T(8,128)(2,1)} custom-call(s32[32]{0:T(128)S(1)} %get-tuple-element.13.order_ref, s32[32]{0:T(128)S(1)} %gather_fusion.2, s32[6]{0:T(128)S(1)} %convert_reduce_fusion.start_ref, bf16[32,96,256]{2,1,0:T(8,128)(2,1)S(1)} %bitcast.255), custom_call_target="tpu_custom_call" | custom-call | flops 786432 | bytes 9437184 | tf_op jit(solution)/shard_map/pallas_call | solution.py:161
  (229 shorter events, 215.2 us)
Async XLA Ops:
  5.8 88.6 %collective-permute-start.14 = (bf16[2,96,256]{2,1,0:T(8,128)(2,1)S(1)}, bf16[2,96,256]{2,1,0:T(8,128)(2,1)}, u32[]{:S(2)}, u32[]{:S(2)}) collective-permute-start(bf16[2,96,256]{2,1,0:T(8,128)(2,1)S(1)} %get-tuple-element.68), channel_id=1, source_target_pairs={{0,15},{1,0},{2,1},{3,2},{4,3},{5,4},{6,5},{7,6},{8,7},{9,8},{10,9... | collective-permute-start | bytes 294920 | tf_op jit(solution)/shard_map/ppermute | solution.py:334
  6.5 86.4 %collective-permute-start.13 = (bf16[2,96,256]{2,1,0:T(8,128)(2,1)S(1)}, bf16[2,96,256]{2,1,0:T(8,128)(2,1)}, u32[]{:S(2)}, u32[]{:S(2)}) collective-permute-start(bf16[2,96,256]{2,1,0:T(8,128)(2,1)S(1)} %get-tuple-element.69), channel_id=1, source_target_pairs={{0,14},{1,15},{2,0},{3,1},{4,2},{5,3},{6,4},{7,5},{8,6},{9,7},{10,... | collective-permute-start | bytes 294920 | tf_op jit(solution)/shard_map/ppermute | solution.py:334
  6.7 84.6 %collective-permute-start.12 = (bf16[2,96,256]{2,1,0:T(8,128)(2,1)S(1)}, bf16[2,96,256]{2,1,0:T(8,128)(2,1)}, u32[]{:S(2)}, u32[]{:S(2)}) collective-permute-start(bf16[2,96,256]{2,1,0:T(8,128)(2,1)S(1)} %get-tuple-element.70), channel_id=1, source_target_pairs={{0,13},{1,14},{2,15},{3,0},{4,1},{5,2},{6,3},{7,4},{8,5},{9,6},{10... | collective-permute-start | bytes 294920 | tf_op jit(solution)/shard_map/ppermute | solution.py:334
  8.0 81.7 %collective-permute-start.11 = (bf16[2,96,256]{2,1,0:T(8,128)(2,1)S(1)}, bf16[2,96,256]{2,1,0:T(8,128)(2,1)}, u32[]{:S(2)}, u32[]{:S(2)}) collective-permute-start(bf16[2,96,256]{2,1,0:T(8,128)(2,1)S(1)} %get-tuple-element.71), channel_id=1, source_target_pairs={{0,12},{1,13},{2,14},{3,15},{4,0},{5,1},{6,2},{7,3},{8,4},{9,5},{1... | collective-permute-start | bytes 294920 | tf_op jit(solution)/shard_map/ppermute | solution.py:334
  11.3 14.3 %collective-permute-start = (bf16[2,96,256]{2,1,0:T(8,128)(2,1)}, bf16[2,96,256]{2,1,0:T(8,128)(2,1)}, u32[]{:S(2)}, u32[]{:S(2)}) collective-permute-start(bf16[2,96,256]{2,1,0:T(8,128)(2,1)} %get-tuple-element.82), channel_id=1, source_target_pairs={{0,1},{1,2},{2,3},{3,4},{4,5},{5,6},{6,7},{7,8},{8,9},{9,10},{10,1... | collective-permute-start | bytes 294920 | tf_op jit(solution)/shard_map/ppermute | solution.py:334
  80.2 8.9 %collective-permute-start.10 = (bf16[2,96,256]{2,1,0:T(8,128)(2,1)S(1)}, bf16[2,96,256]{2,1,0:T(8,128)(2,1)S(1)}, u32[]{:S(2)}, u32[]{:S(2)}) collective-permute-start(bf16[2,96,256]{2,1,0:T(8,128)(2,1)S(1)} %copy-done.2), channel_id=1, source_target_pairs={{0,11},{1,12},{2,13},{3,14},{4,15},{5,0},{6,1},{7,2},{8,3},{9,4},{... | collective-permute-start | bytes 294920 | tf_op jit(solution)/shard_map/ppermute | solution.py:334
  112.0 77.5 %collective-permute-start.44 = (bf16[2,96,256]{2,1,0:T(8,128)(2,1)S(1)}, bf16[2,96,256]{2,1,0:T(8,128)(2,1)S(1)}, u32[]{:S(2)}, u32[]{:S(2)}) collective-permute-start(bf16[2,96,256]{2,1,0:T(8,128)(2,1)S(1)} %get-tuple-element.36), channel_id=1, source_target_pairs={{0,15},{1,0},{2,1},{3,2},{4,3},{5,4},{6,5},{7,6},{8,7},{9,8},{10,9... | collective-permute-start | bytes 294920 | tf_op jit(solution)/shard_map/ppermute | solution.py:334
  112.1 75.9 %collective-permute-start.43 = (bf16[2,96,256]{2,1,0:T(8,128)(2,1)S(1)}, bf16[2,96,256]{2,1,0:T(8,128)(2,1)S(1)}, u32[]{:S(2)}, u32[]{:S(2)}) collective-permute-start(bf16[2,96,256]{2,1,0:T(8,128)(2,1)S(1)} %get-tuple-element.37), channel_id=1, source_target_pairs={{0,14},{1,15},{2,0},{3,1},{4,2},{5,3},{6,4},{7,5},{8,6},{9,7},{10,... | collective-permute-start | bytes 294920 | tf_op jit(solution)/shard_map/ppermute | solution.py:334
  112.1 72.2 %collective-permute-start.42 = (bf16[2,96,256]{2,1,0:T(8,128)(2,1)S(1)}, bf16[2,96,256]{2,1,0:T(8,128)(2,1)S(1)}, u32[]{:S(2)}, u32[]{:S(2)}) collective-permute-start(bf16[2,96,256]{2,1,0:T(8,128)(2,1)S(1)} %get-tuple-element.38), channel_id=1, source_target_pairs={{0,13},{1,14},{2,15},{3,0},{4,1},{5,2},{6,3},{7,4},{8,5},{9,6},{10... | collective-permute-start | bytes 294920 | tf_op jit(solution)/shard_map/ppermute | solution.py:334
  114.6 69.7 %collective-permute-start.41 = (bf16[2,96,256]{2,1,0:T(8,128)(2,1)S(1)}, bf16[2,96,256]{2,1,0:T(8,128)(2,1)S(1)}, u32[]{:S(2)}, u32[]{:S(2)}) collective-permute-start(bf16[2,96,256]{2,1,0:T(8,128)(2,1)S(1)} %get-tuple-element.39), channel_id=1, source_target_pairs={{0,12},{1,13},{2,14},{3,15},{4,0},{5,1},{6,2},{7,3},{8,4},{9,5},{1... | collective-permute-start | bytes 294920 | tf_op jit(solution)/shard_map/ppermute | solution.py:334
  147.9 10.4 %collective-permute-start.36 = (bf16[2,96,256]{2,1,0:T(8,128)(2,1)S(1)}, bf16[2,96,256]{2,1,0:T(8,128)(2,1)S(1)}, u32[]{:S(2)}, u32[]{:S(2)}) collective-permute-start(bf16[2,96,256]{2,1,0:T(8,128)(2,1)S(1)} %get-tuple-element.44), channel_id=1, source_target_pairs={{0,7},{1,8},{2,9},{3,10},{4,11},{5,12},{6,13},{7,14},{8,15},{9,0},... | collective-permute-start | bytes 294920 | tf_op jit(solution)/shard_map/ppermute | solution.py:334
  175.2 9.1 %collective-permute-start.40 = (bf16[2,96,256]{2,1,0:T(8,128)(2,1)S(1)}, bf16[2,96,256]{2,1,0:T(8,128)(2,1)S(1)}, u32[]{:S(2)}, u32[]{:S(2)}) collective-permute-start(bf16[2,96,256]{2,1,0:T(8,128)(2,1)S(1)} %get-tuple-element.40), channel_id=1, source_target_pairs={{0,11},{1,12},{2,13},{3,14},{4,15},{5,0},{6,1},{7,2},{8,3},{9,4},{... | collective-permute-start | bytes 294920 | tf_op jit(solution)/shard_map/ppermute | solution.py:334
  184.2 74.6 %collective-permute-start.29 = (bf16[2,96,256]{2,1,0:T(8,128)(2,1)S(1)}, bf16[2,96,256]{2,1,0:T(8,128)(2,1)S(1)}, u32[]{:S(2)}, u32[]{:S(2)}) collective-permute-start(bf16[2,96,256]{2,1,0:T(8,128)(2,1)S(1)} %get-tuple-element.52), channel_id=1, source_target_pairs={{0,15},{1,0},{2,1},{3,2},{4,3},{5,4},{6,5},{7,6},{8,7},{9,8},{10,9... | collective-permute-start | bytes 294920 | tf_op jit(solution)/shard_map/ppermute | solution.py:334
  184.3 72.5 %collective-permute-start.28 = (bf16[2,96,256]{2,1,0:T(8,128)(2,1)S(1)}, bf16[2,96,256]{2,1,0:T(8,128)(2,1)S(1)}, u32[]{:S(2)}, u32[]{:S(2)}) collective-permute-start(bf16[2,96,256]{2,1,0:T(8,128)(2,1)S(1)} %get-tuple-element.53), channel_id=1, source_target_pairs={{0,14},{1,15},{2,0},{3,1},{4,2},{5,3},{6,4},{7,5},{8,6},{9,7},{10,... | collective-permute-start | bytes 294920 | tf_op jit(solution)/shard_map/ppermute | solution.py:334
  184.4 72.4 %collective-permute-start.27 = (bf16[2,96,256]{2,1,0:T(8,128)(2,1)S(1)}, bf16[2,96,256]{2,1,0:T(8,128)(2,1)S(1)}, u32[]{:S(2)}, u32[]{:S(2)}) collective-permute-start(bf16[2,96,256]{2,1,0:T(8,128)(2,1)S(1)} %get-tuple-element.54), channel_id=1, source_target_pairs={{0,13},{1,14},{2,15},{3,0},{4,1},{5,2},{6,3},{7,4},{8,5},{9,6},{10... | collective-permute-start | bytes 294920 | tf_op jit(solution)/shard_map/ppermute | solution.py:334
  188.0 68.7 %collective-permute-start.26 = (bf16[2,96,256]{2,1,0:T(8,128)(2,1)S(1)}, bf16[2,96,256]{2,1,0:T(8,128)(2,1)S(1)}, u32[]{:S(2)}, u32[]{:S(2)}) collective-permute-start(bf16[2,96,256]{2,1,0:T(8,128)(2,1)S(1)} %get-tuple-element.55), channel_id=1, source_target_pairs={{0,12},{1,13},{2,14},{3,15},{4,0},{5,1},{6,2},{7,3},{8,4},{9,5},{1... | collective-permute-start | bytes 294920 | tf_op jit(solution)/shard_map/ppermute | solution.py:334
  220.6 10.2 %collective-permute-start.21 = (bf16[2,96,256]{2,1,0:T(8,128)(2,1)S(1)}, bf16[2,96,256]{2,1,0:T(8,128)(2,1)S(1)}, u32[]{:S(2)}, u32[]{:S(2)}) collective-permute-start(bf16[2,96,256]{2,1,0:T(8,128)(2,1)S(1)} %get-tuple-element.60), channel_id=1, source_target_pairs={{0,7},{1,8},{2,9},{3,10},{4,11},{5,12},{6,13},{7,14},{8,15},{9,0},... | collective-permute-start | bytes 294920 | tf_op jit(solution)/shard_map/ppermute | solution.py:334
  247.6 9.1 %collective-permute-start.25 = (bf16[2,96,256]{2,1,0:T(8,128)(2,1)S(1)}, bf16[2,96,256]{2,1,0:T(8,128)(2,1)S(1)}, u32[]{:S(2)}, u32[]{:S(2)}) collective-permute-start(bf16[2,96,256]{2,1,0:T(8,128)(2,1)S(1)} %get-tuple-element.56), channel_id=1, source_target_pairs={{0,11},{1,12},{2,13},{3,14},{4,15},{5,0},{6,1},{7,2},{8,3},{9,4},{... | collective-permute-start | bytes 294920 | tf_op jit(solution)/shard_map/ppermute | solution.py:334
  278.7 11.8 %collective-permute-start.45 = (bf16[2,96,256]{2,1,0:T(8,128)(2,1)S(1)}, bf16[2,96,256]{2,1,0:T(8,128)(2,1)S(1)}, u32[]{:S(2)}, u32[]{:S(2)}) collective-permute-start(bf16[2,96,256]{2,1,0:T(8,128)(2,1)S(1)} %get-tuple-element.34), channel_id=1, source_target_pairs={{0,1},{1,2},{2,3},{3,4},{4,5},{5,6},{6,7},{7,8},{8,9},{9,10},{10,1... | collective-permute-start | bytes 294920 | tf_op jit(solution)/shard_map/ppermute | solution.py:334
  279.7 75.1 %collective-permute-start.59 = (bf16[2,96,256]{2,1,0:T(8,128)(2,1)S(1)}, bf16[2,96,256]{2,1,0:T(8,128)(2,1)S(1)}, u32[]{:S(2)}, u32[]{:S(2)}) collective-permute-start(bf16[2,96,256]{2,1,0:T(8,128)(2,1)S(1)} %get-tuple-element.20), channel_id=1, source_target_pairs={{0,15},{1,0},{2,1},{3,2},{4,3},{5,4},{6,5},{7,6},{8,7},{9,8},{10,9... | collective-permute-start | bytes 294920 | tf_op jit(solution)/shard_map/ppermute | solution.py:334
  279.7 75.0 %collective-permute-start.58 = (bf16[2,96,256]{2,1,0:T(8,128)(2,1)S(1)}, bf16[2,96,256]{2,1,0:T(8,128)(2,1)S(1)}, u32[]{:S(2)}, u32[]{:S(2)}) collective-permute-start(bf16[2,96,256]{2,1,0:T(8,128)(2,1)S(1)} %get-tuple-element.21), channel_id=1, source_target_pairs={{0,14},{1,15},{2,0},{3,1},{4,2},{5,3},{6,4},{7,5},{8,6},{9,7},{10,... | collective-permute-start | bytes 294920 | tf_op jit(solution)/shard_map/ppermute | solution.py:334
  279.8 74.9 %collective-permute-start.57 = (bf16[2,96,256]{2,1,0:T(8,128)(2,1)S(1)}, bf16[2,96,256]{2,1,0:T(8,128)(2,1)S(1)}, u32[]{:S(2)}, u32[]{:S(2)}) collective-permute-start(bf16[2,96,256]{2,1,0:T(8,128)(2,1)S(1)} %get-tuple-element.22), channel_id=1, source_target_pairs={{0,13},{1,14},{2,15},{3,0},{4,1},{5,2},{6,3},{7,4},{8,5},{9,6},{10... | collective-permute-start | bytes 294920 | tf_op jit(solution)/shard_map/ppermute | solution.py:334
  283.1 71.6 %collective-permute-start.56 = (bf16[2,96,256]{2,1,0:T(8,128)(2,1)S(1)}, bf16[2,96,256]{2,1,0:T(8,128)(2,1)S(1)}, u32[]{:S(2)}, u32[]{:S(2)}) collective-permute-start(bf16[2,96,256]{2,1,0:T(8,128)(2,1)S(1)} %get-tuple-element.23), channel_id=1, source_target_pairs={{0,12},{1,13},{2,14},{3,15},{4,0},{5,1},{6,2},{7,3},{8,4},{9,5},{1... | collective-permute-start | bytes 294920 | tf_op jit(solution)/shard_map/ppermute | solution.py:334
  311.9 8.7 %collective-permute-start.50 = (bf16[2,96,256]{2,1,0:T(8,128)(2,1)S(1)}, bf16[2,96,256]{2,1,0:T(8,128)(2,1)S(1)}, u32[]{:S(2)}, u32[]{:S(2)}) collective-permute-start(bf16[2,96,256]{2,1,0:T(8,128)(2,1)S(1)} %get-tuple-element.29), channel_id=1, source_target_pairs={{0,6},{1,7},{2,8},{3,9},{4,10},{5,11},{6,12},{7,13},{8,14},{9,15},... | collective-permute-start | bytes 294920 | tf_op jit(solution)/shard_map/ppermute | solution.py:334
  (47 other events, 427.2 us)

commit v10 on v8

--- a/solution.py
+++ b/solution.py
@@ -105,7 +105,10 @@
         _flush(gd_ref, scale_ref, gd_out, direct)
 
 
-def combine_kernel(order_ref, lang_ref, start_ref, back_ref, out_ref, acc_ref):
+def combine_kernel(order_ref, lang_ref, start_ref, back_ref, out_ref, *rest):
+    acc_ref = rest[-1]
+    if len(rest) == 2:
+        rest[0][...] = jnp.zeros_like(rest[0])
     block = out_ref.shape[0]
     b = pl.program_id(0)
     base = b * block
@@ -136,6 +139,77 @@
         return carry
 
     lax.fori_loop(first_at, end_at, add_member, 0)
+
+
+def scatter_kernel(order_ref, lang_ref, back_ref, zeros_hbm, out_hbm, acc_ref, stage_ref, sems):
+    del zeros_hbm
+    members = lang_ref.shape[0]
+    last_member = members - 1
+
+    def run_end(i):
+        return (i == last_member) | (lang_ref[jnp.minimum(i + 1, last_member)] != lang_ref[i])
+
+    def copy(i):
+        return pltpu.make_async_copy(stage_ref.at[i], out_hbm.at[lang_ref[i]], sems.at[i])
+
+    def add_member(i, carry):
+        first = (i == 0) | (lang_ref[jnp.maximum(i - 1, 0)] != lang_ref[i])
+        val = back_ref[order_ref[i]].astype(jnp.float32)
+
+        @pl.when(first)
+        def _():
+            acc_ref[...] = val
+
+        @pl.when(jnp.logical_not(first))
+        def _():
+            acc_ref[...] += val
+
+        @pl.when(run_end(i))
+        def _():
+            stage_ref[i] = acc_ref[...].astype(stage_ref.dtype)
+            copy(i).start()
+
+        return carry
+
+    def finish(i, carry):
+        @pl.when(run_end(i))
+        def _():
+            copy(i).wait()
+
+        return carry
+
+    lax.fori_loop(0, members, add_member, 0)
+    lax.fori_loop(0, members, finish, 0)
+
+
+def scatter_combine(plan, back, zeros):
+    _, order, sorted_langs, _ = plan
+    members, row_count, bottleneck = back.shape
+    lang_count = zeros.shape[0]
+    grid_spec = pltpu.PrefetchScalarGridSpec(
+        num_scalar_prefetch=2,
+        grid=(1,),
+        in_specs=[
+            pl.BlockSpec((members, row_count, bottleneck), lambda i, o, l: (0, 0, 0)),
+            pl.BlockSpec(memory_space=pl.ANY),
+        ],
+        out_specs=pl.BlockSpec(memory_space=pl.ANY),
+        scratch_shapes=[
+            pltpu.VMEM((row_count, bottleneck), jnp.float32),
+            pltpu.VMEM((members, row_count, bottleneck), jnp.bfloat16),
+            pltpu.SemaphoreType.DMA((members,)),
+        ],
+    )
+    return pl.pallas_call(
+        scatter_kernel,
+        grid_spec=grid_spec,
+        out_shape=jax.ShapeDtypeStruct((lang_count, row_count, bottleneck), jnp.bfloat16),
+        input_output_aliases={3: 0},
+        compiler_params=pltpu.CompilerParams(vmem_limit_bytes=48 * 1024 * 1024),
+        cost_estimate=pl.CostEstimate(
+            flops=back.size, bytes_accessed=back.size * 4, transcendentals=0
+        ),
+    )(order, sorted_langs, back, zeros)
 
 
 def combine_plan(slot_lang, lang_count):
@@ -148,28 +222,33 @@
     return block, order, sorted_langs, starts
 
 
-def combine(plan, back, lang_count):
+def combine(plan, back, lang_count, with_zeros=False):
     block, order, sorted_langs, starts = plan
     members, row_count, bottleneck = back.shape
+    outputs = 2 if with_zeros else 1
+    out_spec = pl.BlockSpec((block, row_count, bottleneck), lambda b, o, l, st: (b, 0, 0))
+    out_shape = jax.ShapeDtypeStruct((lang_count, row_count, bottleneck), jnp.bfloat16)
     grid_spec = pltpu.PrefetchScalarGridSpec(
         num_scalar_prefetch=3,
         grid=(lang_count // block,),
         in_specs=[pl.BlockSpec((members, row_count, bottleneck), lambda b, o, l, st: (0, 0, 0))],
-        out_specs=pl.BlockSpec((block, row_count, bottleneck), lambda b, o, l, st: (b, 0, 0)),
+        out_specs=[out_spec] * outputs,
         scratch_shapes=[pltpu.VMEM((row_count, bottleneck), jnp.float32)],
     )
-    return pl.pallas_call(
+    result = pl.pallas_call(
         combine_kernel,
         grid_spec=grid_spec,
-        out_shape=jax.ShapeDtypeStruct((lang_count, row_count, bottleneck), jnp.bfloat16),
+        out_shape=[out_shape] * outputs,
         compiler_params=pltpu.CompilerParams(
             dimension_semantics=("arbitrary",), vmem_limit_bytes=48 * 1024 * 1024
         ),
         cost_estimate=pl.CostEstimate(
-            flops=back.size, bytes_accessed=back.size * 2 + lang_count * row_count * bottleneck * 2,
+            flops=back.size,
+            bytes_accessed=back.size * 2 + outputs * lang_count * row_count * bottleneck * 2,
             transcendentals=0,
         ),
     )(order, sorted_langs, starts, back)
+    return tuple(result) if with_zeros else result[0]
 
 
 def gather_kernel(lang_ref, weight_hbm, out_ref, sems, *, slots):
@@ -350,8 +429,8 @@
     send_down, back_up = lax.optimization_barrier((send_down, back_up))
     back_down = exchange(send_down).reshape(devices * slots, row_count, bottleneck)
     plan = combine_plan(slot_lang, lang_count)
-    up_grads = combine(plan, back_up, lang_count)
-    down_grads = combine(plan, back_down, lang_count)
+    up_grads, zeros = combine(plan, back_up, lang_count, with_zeros=True)
+    down_grads = scatter_combine(plan, back_down, zeros)
     return (d_frames, down_grads, up_grads)
 
 

time: 178 us -> 174 us (0.978)
  waiting for transfers between devices: 107 us -> 105 us
    all_to_all x1, waiting for transfers between devices: 28.9 us -> 26.8 us  [on_device(): exchange(send_down).reshape(devices * slots, row_count, bottleneck)]
  transfers between devices with their start and end apart: 4 -> 4, of which waited for: 4 -> 4; matrix products, arithmetic and copies ran while one was open for 4% -> 4% of each run, Pallas kernels for 17% -> 19%
where the time goes in v10:
time: 174 us
  waiting for transfers between devices  105 us (60%)
  Pallas kernels  39.1 us (22%)
  starting transfers between devices  21.3 us (12%)
  local copies, waits for them, and re-layouts  5.2 us (3%)
  other arithmetic  2.5 us (1%)
    all_to_all x1, waiting for transfers between devices, on_device(): got_down = exchange(gather_rows(slot_lang, down_weight))  32.6 us
    all_to_all x1, waiting for transfers between devices, on_device(): exchange(send_down).reshape(devices * slots, row_count, bottleneck)  26.8 us
    all_to_all x1, waiting for transfers between devices, on_device(): back_up = exchange(send_up).reshape(devices * slots, row_count, bottleneck)  23.6 us
    all_to_all x1, waiting for transfers between devices, on_device(): got_up = exchange(gather_rows(slot_lang, up_weight))  22 us
    pallas_call x1, Pallas kernels, backward_pass(): pl.pallas_call(functools.partial(backward_kernel, direct=direct), grid_sp...  12.6 us
    pallas_call x1, Pallas kernels, forward_pass(): pl.pallas_call(functools.partial(forward_kernel, direct=direct), grid_spe...  9.95 us
    pallas_call x2, Pallas kernels, gather_rows(): pl.pallas_call(functools.partial(gather_kernel, slots=slots), grid_spec=g...  7.07 us
    pallas_call x1, Pallas kernels, combine(): pl.pallas_call(combine_kernel, grid_spec=grid_spec, out_shape=[out_shape]...  6.88 us
  transfers between devices with their start and end apart: 4, of which 4 were waited for; matrix products, arithmetic and copies ran while one was open for 4% of the time, Pallas kernels for 19%

profile of v10, /device:TPU:15, one launch (start us, length us, event | category | flops | bytes accessed | tf_op | source)
XLA Modules:
  0.0 173.7 jit_solution(11531231212140860476)
XLA Ops:
  0.6 0.8 copy.22
  1.5 3.5 %shard_map.103 = bf16[16,2,96,256]{3,2,1,0:T(8,128)(2,1)} custom-call(s32[32]{0:T(128)S(1)} %reshape.152.lang_ref, bf16[160,96,256]{2,1,0:T(8,128)(2,1)} %weight_hbm.2), custom_call_target="tpu_custom_call" | custom-call | bytes 3145728 | tf_op jit(solution)/shard_map/pallas_call | solution.py:286
  5.0 6.6 %all-to-all-start = ((bf16[16,2,96,256]{3,2,1,0:T(8,128)(2,1)}), bf16[16,2,96,256]{3,2,1,0:T(8,128)(2,1)S(1)}, u32[]{:S(2)}, u32[]{:S(2)}) async-start(bf16[16,2,96,256]{3,2,1,0:T(8,128)(2,1)} %shard_map.103), calls=%async_computation | async-start | bytes 3145728 | tf_op jit(solution)/shard_map/all_to_all | solution.py:420
  11.6 3.5 %shard_map.104 = bf16[16,2,96,256]{3,2,1,0:T(8,128)(2,1)} custom-call(s32[32]{0:T(128)S(1)} %reshape.152.lang_ref, bf16[160,96,256]{2,1,0:T(8,128)(2,1)} %weight_hbm.3), custom_call_target="tpu_custom_call" | custom-call | bytes 3145728 | tf_op jit(solution)/shard_map/pallas_call | solution.py:286
  15.2 32.6 %all-to-all-done.wd_ref = bf16[16,2,96,256]{3,2,1,0:T(8,128)(2,1)S(1)} async-done(((bf16[16,2,96,256]{3,2,1,0:T(8,128)(2,1)}), bf16[16,2,96,256]{3,2,1,0:T(8,128)(2,1)S(1)}, u32[]{:S(2)}, u32[]{:S(2)}) %all-to-all-start) | async-done | bytes 1572896 | tf_op jit(solution)/shard_map/all_to_all | solution.py:420
  47.8 4.9 %all-to-all-start.1 = ((bf16[16,2,96,256]{3,2,1,0:T(8,128)(2,1)}), bf16[16,2,96,256]{3,2,1,0:T(8,128)(2,1)}, u32[]{:S(2)}, u32[]{:S(2)}) async-start(bf16[16,2,96,256]{3,2,1,0:T(8,128)(2,1)} %shard_map.104), calls=%async_computation.1 | async-start | bytes 3145728 | tf_op jit(solution)/shard_map/all_to_all | solution.py:421
  52.7 0.6 dynamic_slice.10.slot_ref
  53.3 0.6 dynamic_slice.11.len_ref
  53.9 0.9 gather_fusion
  55.1 0.6 gather_fusion.1
  55.9 0.6 reshape.151.gain_ref
  56.5 0.6 and_select_fusion.scale_ref
  57.0 10.0 %shard_map.105 = (f32[4,256,256]{2,1,0:T(8,128)}, bf16[16,2,96,256]{3,2,1,0:T(8,128)(2,1)}) custom-call(s32[4]{0:T(128)} %dynamic_slice.10.slot_ref, s32[4]{0:T(128)} %dynamic_slice.11.len_ref, bf16[4,256,1536]{2,1,0:T(8,128)(2,1)} %frames_ref.3, bf16[4,256,1536]{2,1,0:T(8,128)(2,1)} %cot_ref.3, f32[1,1536]{1,0:T(1,128)} %reshape.151.gain_ref, ...), custom_call_target="tpu_custom_call" | custom-call | flops 1610612736 | bytes 9437184 | tf_op jit(solution)/shard_map/pallas_call | solution.py:343
  67.0 22.0 %all-to-all-done.1.wu_ref = bf16[16,2,96,256]{3,2,1,0:T(8,128)(2,1)} async-done(((bf16[16,2,96,256]{3,2,1,0:T(8,128)(2,1)}), bf16[16,2,96,256]{3,2,1,0:T(8,128)(2,1)}, u32[]{:S(2)}, u32[]{:S(2)}) %all-to-all-start.1) | async-done | bytes 1572896 | tf_op jit(solution)/shard_map/all_to_all | solution.py:421
  89.0 4.9 %all-to-all-start.2 = ((bf16[16,2,96,256]{3,2,1,0:T(8,128)(2,1)}), bf16[16,2,96,256]{3,2,1,0:T(8,128)(2,1)S(1)}, u32[]{:S(2)}, u32[]{:S(2)}) async-start(bf16[16,2,96,256]{3,2,1,0:T(8,128)(2,1)} %get-tuple-element.16), calls=%async_computation.2 | async-start | bytes 3145728 | tf_op jit(solution)/shard_map/all_to_all | solution.py:425
  93.9 12.6 %shard_map.106 = (bf16[4,256,1536]{2,1,0:T(8,128)(2,1)}, bf16[16,2,96,256]{3,2,1,0:T(8,128)(2,1)}) custom-call(s32[4]{0:T(128)} %dynamic_slice.10.slot_ref, s32[4]{0:T(128)} %dynamic_slice.11.len_ref, bf16[4,256,1536]{2,1,0:T(8,128)(2,1)} %frames_ref.3, bf16[4,256,1536]{2,1,0:T(8,128)(2,1)} %cot_ref.3, f32[1,1536]{1,0:T(1,128)} %reshape.151.gain_ref, ...), custom_call_target="tpu_custom_call" | custom-call | flops 2415919104 | bytes 15728640 | tf_op jit(solution)/shard_map/pallas_call | solution.py:384
  106.5 23.6 %all-to-all-done.2 = bf16[16,2,96,256]{3,2,1,0:T(8,128)(2,1)S(1)} async-done(((bf16[16,2,96,256]{3,2,1,0:T(8,128)(2,1)}), bf16[16,2,96,256]{3,2,1,0:T(8,128)(2,1)S(1)}, u32[]{:S(2)}, u32[]{:S(2)}) %all-to-all-start.2) | async-done | bytes 1572896 | tf_op jit(solution)/shard_map/all_to_all | solution.py:425
  130.1 4.9 %all-to-all-start.3 = ((bf16[16,2,96,256]{3,2,1,0:T(8,128)(2,1)}), bf16[16,2,96,256]{3,2,1,0:T(8,128)(2,1)S(1)}, u32[]{:S(2)}, u32[]{:S(2)}) async-start(bf16[16,2,96,256]{3,2,1,0:T(8,128)(2,1)} %get-tuple-element.17), calls=%async_computation.3 | async-start | bytes 3145728 | tf_op jit(solution)/shard_map/all_to_all | solution.py:430
  135.0 1.6 sort.17
  136.6 0.7 gather_fusion.2
  137.3 0.2 convert_reduce_fusion.start_ref
  137.5 6.9 %shard_map.107 = (bf16[160,96,256]{2,1,0:T(8,128)(2,1)}, bf16[160,96,256]{2,1,0:T(8,128)(2,1)}) custom-call(s32[32]{0:T(128)S(1)} %get-tuple-element.14.order_ref, s32[32]{0:T(128)S(1)} %gather_fusion.2, s32[6]{0:T(128)S(1)} %convert_reduce_fusion.start_ref, bf16[32,96,256]{2,1,0:T(8,128)(2,1)S(1)} %bitcast.14), custom_call_target="tpu_custom_call" | custom-call | flops 786432 | bytes 17301504 | tf_op jit(solution)/shard_map/pallas_call | solution.py:238
  144.4 26.8 %all-to-all-done.3 = bf16[16,2,96,256]{3,2,1,0:T(8,128)(2,1)S(1)} async-done(((bf16[16,2,96,256]{3,2,1,0:T(8,128)(2,1)}), bf16[16,2,96,256]{3,2,1,0:T(8,128)(2,1)S(1)}, u32[]{:S(2)}, u32[]{:S(2)}) %all-to-all-start.3) | async-done | bytes 1572896 | tf_op jit(solution)/shard_map/all_to_all | solution.py:430
  171.2 2.6 %shard_map.108 = bf16[160,96,256]{2,1,0:T(8,128)(2,1)} custom-call(s32[32]{0:T(128)S(1)} %get-tuple-element.14.order_ref, s32[32]{0:T(128)S(1)} %gather_fusion.2, bf16[32,96,256]{2,1,0:T(8,128)(2,1)S(1)} %bitcast.15, bf16[160,96,256]{2,1,0:T(8,128)(2,1)} %get-tuple-element.19.zeros_hbm), custom_call_target="tpu_custom_call", output_to_operand_aliasing={{}: (3, {})} | custom-call | flops 786432 | bytes 3145728 | tf_op jit(solution)/shard_map/pallas_call | solution.py:203
  (22 shorter events, 0.5 us)
Async XLA Ops:
  5.0 42.8 %all-to-all-start = ((bf16[16,2,96,256]{3,2,1,0:T(8,128)(2,1)}), bf16[16,2,96,256]{3,2,1,0:T(8,128)(2,1)S(1)}, u32[]{:S(2)}, u32[]{:S(2)}) async-start(bf16[16,2,96,256]{3,2,1,0:T(8,128)(2,1)} %shard_map.103), calls=%async_computation | async-start | bytes 3145728 | tf_op jit(solution)/shard_map/all_to_all | solution.py:420
  15.1 37.6 %copy-start.4 = (s32[64]{0:T(128)S(1)}, s32[64]{0:T(128)}, u32[]{:S(2)}) copy-start(s32[64]{0:T(128)} %param.14) | copy-start | bytes 772
  15.1 38.1 %copy-start.3 = (s32[64]{0:T(128)S(1)}, s32[64]{0:T(128)}, u32[]{:S(2)}) copy-start(s32[64]{0:T(128)} %param.15) | copy-start | bytes 772
  15.1 38.8 %copy-start = (s32[16,2]{0,1:T(2,128)S(1)}, s32[16,2]{0,1:T(2,128)}, u32[]{:S(2)}) copy-start(s32[16,2]{0,1:T(2,128)} %param.13) | copy-start | bytes 388
  15.2 40.7 %copy-start.2 = (f32[1536]{0:T(1024)S(1)}, f32[1536]{0:T(1024)}, u32[]{:S(2)}) copy-start(f32[1536]{0:T(1024)} %param.10) | copy-start | bytes 18436
  47.8 9.3 %copy-start.1 = (bf16[16,2,96,256]{3,2,1,0:T(8,128)(2,1)}, bf16[16,2,96,256]{3,2,1,0:T(8,128)(2,1)S(1)}, u32[]{:S(2)}) copy-start(bf16[16,2,96,256]{3,2,1,0:T(8,128)(2,1)S(1)} %all-to-all-done.wd_ref) | copy-start | bytes 4718596
  47.8 41.2 %all-to-all-start.1 = ((bf16[16,2,96,256]{3,2,1,0:T(8,128)(2,1)}), bf16[16,2,96,256]{3,2,1,0:T(8,128)(2,1)}, u32[]{:S(2)}, u32[]{:S(2)}) async-start(bf16[16,2,96,256]{3,2,1,0:T(8,128)(2,1)} %shard_map.104), calls=%async_computation.1 | async-start | bytes 3145728 | tf_op jit(solution)/shard_map/all_to_all | solution.py:421
  89.0 41.1 %all-to-all-start.2 = ((bf16[16,2,96,256]{3,2,1,0:T(8,128)(2,1)}), bf16[16,2,96,256]{3,2,1,0:T(8,128)(2,1)S(1)}, u32[]{:S(2)}, u32[]{:S(2)}) async-start(bf16[16,2,96,256]{3,2,1,0:T(8,128)(2,1)} %get-tuple-element.16), calls=%async_computation.2 | async-start | bytes 3145728 | tf_op jit(solution)/shard_map/all_to_all | solution.py:425
  130.1 41.1 %all-to-all-start.3 = ((bf16[16,2,96,256]{3,2,1,0:T(8,128)(2,1)}), bf16[16,2,96,256]{3,2,1,0:T(8,128)(2,1)S(1)}, u32[]{:S(2)}, u32[]{:S(2)}) async-start(bf16[16,2,96,256]{3,2,1,0:T(8,128)(2,1)} %get-tuple-element.17), calls=%async_computation.3 | async-start | bytes 3145728 | tf_op jit(solution)/shard_map/all_to_all | solution.py:430

commit v11 on v10

--- a/solution.py
+++ b/solution.py
@@ -251,23 +251,32 @@
     return tuple(result) if with_zeros else result[0]
 
 
-def gather_kernel(lang_ref, weight_hbm, out_ref, sems, *, slots):
+def gather_kernel(lang_ref, weight_hbm, out_hbm, stage_ref, sems_in, sems_out, *, slots):
     members = lang_ref.shape[0]
 
-    def copy(m):
+    def copy_in(m):
+        return pltpu.make_async_copy(weight_hbm.at[lang_ref[m]], stage_ref.at[m], sems_in.at[m])
+
+    def copy_out(m):
         return pltpu.make_async_copy(
-            weight_hbm.at[lang_ref[m]], out_ref.at[m // slots, m % slots], sems.at[m]
+            stage_ref.at[m], out_hbm.at[m // slots, m % slots], sems_out.at[m]
         )
 
     def start(m, carry):
-        copy(m).start()
+        copy_in(m).start()
+        return carry
+
+    def forward(m, carry):
+        copy_in(m).wait()
+        copy_out(m).start()
         return carry
 
     def finish(m, carry):
-        copy(m).wait()
+        copy_out(m).wait()
         return carry
 
     lax.fori_loop(0, members, start, 0)
+    lax.fori_loop(0, members, forward, 0)
     lax.fori_loop(0, members, finish, 0)
 
 
@@ -279,14 +288,18 @@
         num_scalar_prefetch=1,
         grid=(1,),
         in_specs=[pl.BlockSpec(memory_space=pl.ANY)],
-        out_specs=pl.BlockSpec((devices, slots, row_count, bottleneck), lambda i, ml: (0, 0, 0, 0)),
-        scratch_shapes=[pltpu.SemaphoreType.DMA((members,))],
+        out_specs=pl.BlockSpec(memory_space=pl.ANY),
+        scratch_shapes=[
+            pltpu.VMEM((members, row_count, bottleneck), weight.dtype),
+            pltpu.SemaphoreType.DMA((members,)),
+            pltpu.SemaphoreType.DMA((members,)),
+        ],
     )
     size = members * row_count * bottleneck * 2
     return pl.pallas_call(
         functools.partial(gather_kernel, slots=slots),
         grid_spec=grid_spec,
-        out_shape=jax.ShapeDtypeStruct((devices, slots, row_count, bottleneck), jnp.bfloat16),
+        out_shape=jax.ShapeDtypeStruct((devices, slots, row_count, bottleneck), weight.dtype),
         compiler_params=pltpu.CompilerParams(vmem_limit_bytes=48 * 1024 * 1024),
         cost_estimate=pl.CostEstimate(flops=0, bytes_accessed=2 * size, transcendentals=0),
     )(slot_lang.reshape(-1), weight)

time: 174 us -> 175 us (level)
  no operation moved by 1% of the time
where the time goes in v11:
time: 175 us; the launch traced here: 174 us
  waiting for transfers between devices  105 us (60%)
  Pallas kernels  38.9 us (22%)
  starting transfers between devices  21.3 us (12%)
  local copies, waits for them, and re-layouts  5.2 us (3%)
  other arithmetic  2.5 us (1%)
    all_to_all x1, waiting for transfers between devices, on_device(): got_down = exchange(gather_rows(slot_lang, down_weight))  32.5 us
    all_to_all x1, waiting for transfers between devices, on_device(): exchange(send_down).reshape(devices * slots, row_count, bottleneck)  27.1 us
    all_to_all x1, waiting for transfers between devices, on_device(): back_up = exchange(send_up).reshape(devices * slots, row_count, bottleneck)  23.6 us
    all_to_all x1, waiting for transfers between devices, on_device(): got_up = exchange(gather_rows(slot_lang, up_weight))  22 us
    pallas_call x1, Pallas kernels, backward_pass(): pl.pallas_call(functools.partial(backward_kernel, direct=direct), grid_sp...  12.6 us
    pallas_call x1, Pallas kernels, forward_pass(): pl.pallas_call(functools.partial(forward_kernel, direct=direct), grid_spe...  9.95 us
    pallas_call x2, Pallas kernels, gather_rows(): pl.pallas_call(functools.partial(gather_kernel, slots=slots), grid_spec=g...  7.1 us
    pallas_call x1, Pallas kernels, combine(): pl.pallas_call(combine_kernel, grid_spec=grid_spec, out_shape=[out_shape]...  6.61 us
  transfers between devices with their start and end apart: 4, of which 4 were waited for; matrix products, arithmetic and copies ran while one was open for 4% of the time, Pallas kernels for 19%

profile of v11, /device:TPU:15, one launch (start us, length us, event | category | flops | bytes accessed | tf_op | source)
XLA Modules:
  0.0 173.7 jit_solution(5917846595973832254)
XLA Ops:
  0.6 0.8 copy.22
  1.5 3.5 %shard_map.103 = bf16[16,2,96,256]{3,2,1,0:T(8,128)(2,1)} custom-call(s32[32]{0:T(128)S(1)} %reshape.152.lang_ref, bf16[160,96,256]{2,1,0:T(8,128)(2,1)} %weight_hbm.2), custom_call_target="tpu_custom_call" | custom-call | bytes 3145728 | tf_op jit(solution)/shard_map/pallas_call | solution.py:299
  5.0 6.6 %all-to-all-start = ((bf16[16,2,96,256]{3,2,1,0:T(8,128)(2,1)}), bf16[16,2,96,256]{3,2,1,0:T(8,128)(2,1)S(1)}, u32[]{:S(2)}, u32[]{:S(2)}) async-start(bf16[16,2,96,256]{3,2,1,0:T(8,128)(2,1)} %shard_map.103), calls=%async_computation | async-start | bytes 3145728 | tf_op jit(solution)/shard_map/all_to_all | solution.py:433
  11.6 3.6 %shard_map.104 = bf16[16,2,96,256]{3,2,1,0:T(8,128)(2,1)} custom-call(s32[32]{0:T(128)S(1)} %reshape.152.lang_ref, bf16[160,96,256]{2,1,0:T(8,128)(2,1)} %weight_hbm.3), custom_call_target="tpu_custom_call" | custom-call | bytes 3145728 | tf_op jit(solution)/shard_map/pallas_call | solution.py:299
  15.2 32.5 %all-to-all-done.wd_ref = bf16[16,2,96,256]{3,2,1,0:T(8,128)(2,1)S(1)} async-done(((bf16[16,2,96,256]{3,2,1,0:T(8,128)(2,1)}), bf16[16,2,96,256]{3,2,1,0:T(8,128)(2,1)S(1)}, u32[]{:S(2)}, u32[]{:S(2)}) %all-to-all-start) | async-done | bytes 1572896 | tf_op jit(solution)/shard_map/all_to_all | solution.py:433
  47.7 4.9 %all-to-all-start.1 = ((bf16[16,2,96,256]{3,2,1,0:T(8,128)(2,1)}), bf16[16,2,96,256]{3,2,1,0:T(8,128)(2,1)}, u32[]{:S(2)}, u32[]{:S(2)}) async-start(bf16[16,2,96,256]{3,2,1,0:T(8,128)(2,1)} %shard_map.104), calls=%async_computation.1 | async-start | bytes 3145728 | tf_op jit(solution)/shard_map/all_to_all | solution.py:434
  52.7 0.6 dynamic_slice.10.slot_ref
  53.2 0.6 dynamic_slice.11.len_ref
  53.9 0.9 gather_fusion
  55.1 0.6 gather_fusion.1
  55.8 0.6 reshape.151.gain_ref
  56.5 0.6 and_select_fusion.scale_ref
  57.0 10.0 %shard_map.105 = (f32[4,256,256]{2,1,0:T(8,128)}, bf16[16,2,96,256]{3,2,1,0:T(8,128)(2,1)}) custom-call(s32[4]{0:T(128)} %dynamic_slice.10.slot_ref, s32[4]{0:T(128)} %dynamic_slice.11.len_ref, bf16[4,256,1536]{2,1,0:T(8,128)(2,1)} %frames_ref.3, bf16[4,256,1536]{2,1,0:T(8,128)(2,1)} %cot_ref.3, f32[1,1536]{1,0:T(1,128)} %reshape.151.gain_ref, ...), custom_call_target="tpu_custom_call" | custom-call | flops 1610612736 | bytes 9437184 | tf_op jit(solution)/shard_map/pallas_call | solution.py:356
  67.0 22.0 %all-to-all-done.1.wu_ref = bf16[16,2,96,256]{3,2,1,0:T(8,128)(2,1)} async-done(((bf16[16,2,96,256]{3,2,1,0:T(8,128)(2,1)}), bf16[16,2,96,256]{3,2,1,0:T(8,128)(2,1)}, u32[]{:S(2)}, u32[]{:S(2)}) %all-to-all-start.1) | async-done | bytes 1572896 | tf_op jit(solution)/shard_map/all_to_all | solution.py:434
  88.9 4.9 %all-to-all-start.2 = ((bf16[16,2,96,256]{3,2,1,0:T(8,128)(2,1)}), bf16[16,2,96,256]{3,2,1,0:T(8,128)(2,1)S(1)}, u32[]{:S(2)}, u32[]{:S(2)}) async-start(bf16[16,2,96,256]{3,2,1,0:T(8,128)(2,1)} %get-tuple-element.16), calls=%async_computation.2 | async-start | bytes 3145728 | tf_op jit(solution)/shard_map/all_to_all | solution.py:438
  93.8 12.6 %shard_map.106 = (bf16[4,256,1536]{2,1,0:T(8,128)(2,1)}, bf16[16,2,96,256]{3,2,1,0:T(8,128)(2,1)}) custom-call(s32[4]{0:T(128)} %dynamic_slice.10.slot_ref, s32[4]{0:T(128)} %dynamic_slice.11.len_ref, bf16[4,256,1536]{2,1,0:T(8,128)(2,1)} %frames_ref.3, bf16[4,256,1536]{2,1,0:T(8,128)(2,1)} %cot_ref.3, f32[1,1536]{1,0:T(1,128)} %reshape.151.gain_ref, ...), custom_call_target="tpu_custom_call" | custom-call | flops 2415919104 | bytes 15728640 | tf_op jit(solution)/shard_map/pallas_call | solution.py:397
  106.5 23.6 %all-to-all-done.2 = bf16[16,2,96,256]{3,2,1,0:T(8,128)(2,1)S(1)} async-done(((bf16[16,2,96,256]{3,2,1,0:T(8,128)(2,1)}), bf16[16,2,96,256]{3,2,1,0:T(8,128)(2,1)S(1)}, u32[]{:S(2)}, u32[]{:S(2)}) %all-to-all-start.2) | async-done | bytes 1572896 | tf_op jit(solution)/shard_map/all_to_all | solution.py:438
  130.0 4.9 %all-to-all-start.3 = ((bf16[16,2,96,256]{3,2,1,0:T(8,128)(2,1)}), bf16[16,2,96,256]{3,2,1,0:T(8,128)(2,1)S(1)}, u32[]{:S(2)}, u32[]{:S(2)}) async-start(bf16[16,2,96,256]{3,2,1,0:T(8,128)(2,1)} %get-tuple-element.17), calls=%async_computation.3 | async-start | bytes 3145728 | tf_op jit(solution)/shard_map/all_to_all | solution.py:443
  134.9 1.6 sort.17
  136.6 0.7 gather_fusion.2
  137.3 0.2 convert_reduce_fusion.start_ref
  137.5 6.6 %shard_map.107 = (bf16[160,96,256]{2,1,0:T(8,128)(2,1)}, bf16[160,96,256]{2,1,0:T(8,128)(2,1)}) custom-call(s32[32]{0:T(128)S(1)} %get-tuple-element.14.order_ref, s32[32]{0:T(128)S(1)} %gather_fusion.2, s32[6]{0:T(128)S(1)} %convert_reduce_fusion.start_ref, bf16[32,96,256]{2,1,0:T(8,128)(2,1)S(1)} %bitcast.14), custom_call_target="tpu_custom_call" | custom-call | flops 786432 | bytes 17301504 | tf_op jit(solution)/shard_map/pallas_call | solution.py:238
  144.1 27.1 %all-to-all-done.3 = bf16[16,2,96,256]{3,2,1,0:T(8,128)(2,1)S(1)} async-done(((bf16[16,2,96,256]{3,2,1,0:T(8,128)(2,1)}), bf16[16,2,96,256]{3,2,1,0:T(8,128)(2,1)S(1)}, u32[]{:S(2)}, u32[]{:S(2)}) %all-to-all-start.3) | async-done | bytes 1572896 | tf_op jit(solution)/shard_map/all_to_all | solution.py:443
  171.1 2.6 %shard_map.108 = bf16[160,96,256]{2,1,0:T(8,128)(2,1)} custom-call(s32[32]{0:T(128)S(1)} %get-tuple-element.14.order_ref, s32[32]{0:T(128)S(1)} %gather_fusion.2, bf16[32,96,256]{2,1,0:T(8,128)(2,1)S(1)} %bitcast.15, bf16[160,96,256]{2,1,0:T(8,128)(2,1)} %get-tuple-element.19.zeros_hbm), custom_call_target="tpu_custom_call", output_to_operand_aliasing={{}: (3, {})} | custom-call | flops 786432 | bytes 3145728 | tf_op jit(solution)/shard_map/pallas_call | solution.py:203
  (22 shorter events, 0.5 us)
Async XLA Ops:
  5.0 42.8 %all-to-all-start = ((bf16[16,2,96,256]{3,2,1,0:T(8,128)(2,1)}), bf16[16,2,96,256]{3,2,1,0:T(8,128)(2,1)S(1)}, u32[]{:S(2)}, u32[]{:S(2)}) async-start(bf16[16,2,96,256]{3,2,1,0:T(8,128)(2,1)} %shard_map.103), calls=%async_computation | async-start | bytes 3145728 | tf_op jit(solution)/shard_map/all_to_all | solution.py:433
  15.2 37.5 %copy-start.4 = (s32[64]{0:T(128)S(1)}, s32[64]{0:T(128)}, u32[]{:S(2)}) copy-start(s32[64]{0:T(128)} %param.14) | copy-start | bytes 772
  15.2 38.1 %copy-start.3 = (s32[64]{0:T(128)S(1)}, s32[64]{0:T(128)}, u32[]{:S(2)}) copy-start(s32[64]{0:T(128)} %param.15) | copy-start | bytes 772
  15.2 38.7 %copy-start = (s32[16,2]{0,1:T(2,128)S(1)}, s32[16,2]{0,1:T(2,128)}, u32[]{:S(2)}) copy-start(s32[16,2]{0,1:T(2,128)} %param.13) | copy-start | bytes 388
  15.2 40.7 %copy-start.2 = (f32[1536]{0:T(1024)S(1)}, f32[1536]{0:T(1024)}, u32[]{:S(2)}) copy-start(f32[1536]{0:T(1024)} %param.10) | copy-start | bytes 18436
  47.7 9.3 %copy-start.1 = (bf16[16,2,96,256]{3,2,1,0:T(8,128)(2,1)}, bf16[16,2,96,256]{3,2,1,0:T(8,128)(2,1)S(1)}, u32[]{:S(2)}) copy-start(bf16[16,2,96,256]{3,2,1,0:T(8,128)(2,1)S(1)} %all-to-all-done.wd_ref) | copy-start | bytes 4718596
  47.7 41.2 %all-to-all-start.1 = ((bf16[16,2,96,256]{3,2,1,0:T(8,128)(2,1)}), bf16[16,2,96,256]{3,2,1,0:T(8,128)(2,1)}, u32[]{:S(2)}, u32[]{:S(2)}) async-start(bf16[16,2,96,256]{3,2,1,0:T(8,128)(2,1)} %shard_map.104), calls=%async_computation.1 | async-start | bytes 3145728 | tf_op jit(solution)/shard_map/all_to_all | solution.py:434
  88.9 41.1 %all-to-all-start.2 = ((bf16[16,2,96,256]{3,2,1,0:T(8,128)(2,1)}), bf16[16,2,96,256]{3,2,1,0:T(8,128)(2,1)S(1)}, u32[]{:S(2)}, u32[]{:S(2)}) async-start(bf16[16,2,96,256]{3,2,1,0:T(8,128)(2,1)} %get-tuple-element.16), calls=%async_computation.2 | async-start | bytes 3145728 | tf_op jit(solution)/shard_map/all_to_all | solution.py:438
  130.0 41.1 %all-to-all-start.3 = ((bf16[16,2,96,256]{3,2,1,0:T(8,128)(2,1)}), bf16[16,2,96,256]{3,2,1,0:T(8,128)(2,1)S(1)}, u32[]{:S(2)}, u32[]{:S(2)}) async-start(bf16[16,2,96,256]{3,2,1,0:T(8,128)(2,1)} %get-tuple-element.17), calls=%async_computation.3 | async-start | bytes 3145728 | tf_op jit(solution)/shard_map/all_to_all | solution.py:443

commit v12 on v10

--- a/solution.py
+++ b/solution.py
@@ -251,12 +251,12 @@
     return tuple(result) if with_zeros else result[0]
 
 
-def gather_kernel(lang_ref, weight_hbm, out_ref, sems, *, slots):
+def gather_kernel(lang_ref, weight_hbm, out_hbm, sems, *, slots):
     members = lang_ref.shape[0]
 
     def copy(m):
         return pltpu.make_async_copy(
-            weight_hbm.at[lang_ref[m]], out_ref.at[m // slots, m % slots], sems.at[m]
+            weight_hbm.at[lang_ref[m]], out_hbm.at[m // slots, m % slots], sems.at[m]
         )
 
     def start(m, carry):
@@ -279,15 +279,14 @@
         num_scalar_prefetch=1,
         grid=(1,),
         in_specs=[pl.BlockSpec(memory_space=pl.ANY)],
-        out_specs=pl.BlockSpec((devices, slots, row_count, bottleneck), lambda i, ml: (0, 0, 0, 0)),
+        out_specs=pl.BlockSpec(memory_space=pl.ANY),
         scratch_shapes=[pltpu.SemaphoreType.DMA((members,))],
     )
     size = members * row_count * bottleneck * 2
     return pl.pallas_call(
         functools.partial(gather_kernel, slots=slots),
         grid_spec=grid_spec,
-        out_shape=jax.ShapeDtypeStruct((devices, slots, row_count, bottleneck), jnp.bfloat16),
-        compiler_params=pltpu.CompilerParams(vmem_limit_bytes=48 * 1024 * 1024),
+        out_shape=jax.ShapeDtypeStruct((devices, slots, row_count, bottleneck), weight.dtype),
         cost_estimate=pl.CostEstimate(flops=0, bytes_accessed=2 * size, transcendentals=0),
     )(slot_lang.reshape(-1), weight)
 

time: 174 us -> 236 us (1.36)
  Pallas kernels: 39.1 us -> 131 us
  waiting for transfers between devices: 105 us -> 72.3 us
    pallas_call x2, Pallas kernels: 7.07 us -> 99.4 us  [gather_rows(): pl.pallas_call(functools.partial(gather_kernel, slots=slots), grid_spec=g...]
    all_to_all x1, waiting for transfers between devices: 32.6 us -> 0.01 us  [on_device(): got_down = exchange(gather_rows(slot_lang, down_weight))]
  transfers between devices with their start and end apart: 4 -> 4, of which waited for: 4 -> 3; matrix products, arithmetic and copies ran while one was open for 4% -> 3% of each run, Pallas kernels for 19% -> 34%
where the time goes in v12:
time: 236 us; the launch traced here: 235 us
  Pallas kernels  131 us (56%)
  waiting for transfers between devices  72.3 us (31%)
  starting transfers between devices  22.4 us (9%)
  local copies, waits for them, and re-layouts  5.77 us (2%)
  other arithmetic  2.51 us (1%)
    pallas_call x2, Pallas kernels, gather_rows(): pl.pallas_call(functools.partial(gather_kernel, slots=slots), grid_spec=g...  99.4 us
    all_to_all x1, waiting for transfers between devices, on_device(): exchange(send_down).reshape(devices * slots, row_count, bottleneck)  27 us
    all_to_all x1, waiting for transfers between devices, on_device(): back_up = exchange(send_up).reshape(devices * slots, row_count, bottleneck)  23.5 us
    all_to_all x1, waiting for transfers between devices, on_device(): got_up = exchange(gather_rows(slot_lang, up_weight))  21.7 us
    pallas_call x1, Pallas kernels, backward_pass(): pl.pallas_call(functools.partial(backward_kernel, direct=direct), grid_sp...  12.7 us
    pallas_call x1, Pallas kernels, forward_pass(): pl.pallas_call(functools.partial(forward_kernel, direct=direct), grid_spe...  10.1 us
    pallas_call x1, Pallas kernels, combine(): pl.pallas_call(combine_kernel, grid_spec=grid_spec, out_shape=[out_shape]...  6.64 us
    all_to_all x1, starting transfers between devices, on_device(): got_down = exchange(gather_rows(slot_lang, down_weight))  6.57 us
  transfers between devices with their start and end apart: 4, of which 3 were waited for; matrix products, arithmetic and copies ran while one was open for 3% of the time, Pallas kernels for 34%

profile of v12, /device:TPU:15, one launch (start us, length us, event | category | flops | bytes accessed | tf_op | source)
XLA Modules:
  0.0 235.1 jit_solution(15776085532024138248)
XLA Ops:
  0.6 0.8 copy.22
  1.4 0.7 reshape.152.lang_ref
  2.1 49.7 %shard_map.103 = bf16[16,2,96,256]{3,2,1,0:T(8,128)(2,1)} custom-call(s32[32]{0:T(128)} %reshape.152.lang_ref, bf16[160,96,256]{2,1,0:T(8,128)(2,1)} %weight_hbm.2), custom_call_target="tpu_custom_call" | custom-call | bytes 3145728 | tf_op jit(solution)/shard_map/pallas_call | solution.py:286
  51.8 6.6 %all-to-all-start = ((bf16[16,2,96,256]{3,2,1,0:T(8,128)(2,1)}), bf16[16,2,96,256]{3,2,1,0:T(8,128)(2,1)S(1)}, u32[]{:S(2)}, u32[]{:S(2)}) async-start(bf16[16,2,96,256]{3,2,1,0:T(8,128)(2,1)} %shard_map.103), calls=%async_computation | async-start | bytes 3145728 | tf_op jit(solution)/shard_map/all_to_all | solution.py:419
  58.3 49.7 %shard_map.104 = bf16[16,2,96,256]{3,2,1,0:T(8,128)(2,1)} custom-call(s32[32]{0:T(128)} %reshape.152.lang_ref, bf16[160,96,256]{2,1,0:T(8,128)(2,1)} %weight_hbm.3), custom_call_target="tpu_custom_call" | custom-call | bytes 3145728 | tf_op jit(solution)/shard_map/pallas_call | solution.py:286
  108.1 6.0 %all-to-all-start.1 = ((bf16[16,2,96,256]{3,2,1,0:T(8,128)(2,1)}), bf16[16,2,96,256]{3,2,1,0:T(8,128)(2,1)S(1)}, u32[]{:S(2)}, u32[]{:S(2)}) async-start(bf16[16,2,96,256]{3,2,1,0:T(8,128)(2,1)} %shard_map.104), calls=%async_computation.1 | async-start | bytes 3145728 | tf_op jit(solution)/shard_map/all_to_all | solution.py:420
  114.1 0.6 dynamic_slice.10.slot_ref
  114.8 0.6 dynamic_slice.11.len_ref
  115.4 0.9 gather_fusion
  116.6 0.6 gather_fusion.1
  117.3 0.6 reshape.151.gain_ref
  117.9 0.6 and_select_fusion.scale_ref
  118.5 10.1 %shard_map.105 = (f32[4,256,256]{2,1,0:T(8,128)}, bf16[16,2,96,256]{3,2,1,0:T(8,128)(2,1)}) custom-call(s32[4]{0:T(128)} %dynamic_slice.10.slot_ref, s32[4]{0:T(128)} %dynamic_slice.11.len_ref, bf16[4,256,1536]{2,1,0:T(8,128)(2,1)} %frames_ref.3, bf16[4,256,1536]{2,1,0:T(8,128)(2,1)} %cot_ref.3, f32[1,1536]{1,0:T(1,128)} %reshape.151.gain_ref, ...), custom_call_target="tpu_custom_call" | custom-call | flops 1610612736 | bytes 9437184 | tf_op jit(solution)/shard_map/pallas_call | solution.py:342
  128.6 21.7 %all-to-all-done.1.wu_ref = bf16[16,2,96,256]{3,2,1,0:T(8,128)(2,1)S(1)} async-done(((bf16[16,2,96,256]{3,2,1,0:T(8,128)(2,1)}), bf16[16,2,96,256]{3,2,1,0:T(8,128)(2,1)S(1)}, u32[]{:S(2)}, u32[]{:S(2)}) %all-to-all-start.1) | async-done | bytes 1572896 | tf_op jit(solution)/shard_map/all_to_all | solution.py:420
  150.3 4.9 %all-to-all-start.2 = ((bf16[16,2,96,256]{3,2,1,0:T(8,128)(2,1)}), bf16[16,2,96,256]{3,2,1,0:T(8,128)(2,1)S(1)}, u32[]{:S(2)}, u32[]{:S(2)}) async-start(bf16[16,2,96,256]{3,2,1,0:T(8,128)(2,1)} %get-tuple-element.16), calls=%async_computation.2 | async-start | bytes 3145728 | tf_op jit(solution)/shard_map/all_to_all | solution.py:424
  155.2 12.7 %shard_map.106 = (bf16[4,256,1536]{2,1,0:T(8,128)(2,1)}, bf16[16,2,96,256]{3,2,1,0:T(8,128)(2,1)}) custom-call(s32[4]{0:T(128)} %dynamic_slice.10.slot_ref, s32[4]{0:T(128)} %dynamic_slice.11.len_ref, bf16[4,256,1536]{2,1,0:T(8,128)(2,1)} %frames_ref.3, bf16[4,256,1536]{2,1,0:T(8,128)(2,1)} %cot_ref.3, f32[1,1536]{1,0:T(1,128)} %reshape.151.gain_ref, ...), custom_call_target="tpu_custom_call" | custom-call | flops 2415919104 | bytes 15728640 | tf_op jit(solution)/shard_map/pallas_call | solution.py:383
  167.9 23.5 %all-to-all-done.2 = bf16[16,2,96,256]{3,2,1,0:T(8,128)(2,1)S(1)} async-done(((bf16[16,2,96,256]{3,2,1,0:T(8,128)(2,1)}), bf16[16,2,96,256]{3,2,1,0:T(8,128)(2,1)S(1)}, u32[]{:S(2)}, u32[]{:S(2)}) %all-to-all-start.2) | async-done | bytes 1572896 | tf_op jit(solution)/shard_map/all_to_all | solution.py:424
  191.4 4.9 %all-to-all-start.3 = ((bf16[16,2,96,256]{3,2,1,0:T(8,128)(2,1)}), bf16[16,2,96,256]{3,2,1,0:T(8,128)(2,1)S(1)}, u32[]{:S(2)}, u32[]{:S(2)}) async-start(bf16[16,2,96,256]{3,2,1,0:T(8,128)(2,1)} %get-tuple-element.17), calls=%async_computation.3 | async-start | bytes 3145728 | tf_op jit(solution)/shard_map/all_to_all | solution.py:429
  196.3 1.6 sort.17
  198.0 0.7 gather_fusion.2
  198.7 0.2 convert_reduce_fusion.start_ref
  198.9 6.6 %shard_map.107 = (bf16[160,96,256]{2,1,0:T(8,128)(2,1)}, bf16[160,96,256]{2,1,0:T(8,128)(2,1)}) custom-call(s32[32]{0:T(128)S(1)} %get-tuple-element.14.order_ref, s32[32]{0:T(128)S(1)} %gather_fusion.2, s32[6]{0:T(128)S(1)} %convert_reduce_fusion.start_ref, bf16[32,96,256]{2,1,0:T(8,128)(2,1)S(1)} %bitcast.14), custom_call_target="tpu_custom_call" | custom-call | flops 786432 | bytes 17301504 | tf_op jit(solution)/shard_map/pallas_call | solution.py:238
  205.5 27.0 %all-to-all-done.3 = bf16[16,2,96,256]{3,2,1,0:T(8,128)(2,1)S(1)} async-done(((bf16[16,2,96,256]{3,2,1,0:T(8,128)(2,1)}), bf16[16,2,96,256]{3,2,1,0:T(8,128)(2,1)S(1)}, u32[]{:S(2)}, u32[]{:S(2)}) %all-to-all-start.3) | async-done | bytes 1572896 | tf_op jit(solution)/shard_map/all_to_all | solution.py:429
  232.5 2.6 %shard_map.108 = bf16[160,96,256]{2,1,0:T(8,128)(2,1)} custom-call(s32[32]{0:T(128)S(1)} %get-tuple-element.14.order_ref, s32[32]{0:T(128)S(1)} %gather_fusion.2, bf16[32,96,256]{2,1,0:T(8,128)(2,1)S(1)} %bitcast.15, bf16[160,96,256]{2,1,0:T(8,128)(2,1)} %get-tuple-element.19.zeros_hbm), custom_call_target="tpu_custom_call", output_to_operand_aliasing={{}: (3, {})} | custom-call | flops 786432 | bytes 3145728 | tf_op jit(solution)/shard_map/pallas_call | solution.py:203
  (26 shorter events, 0.5 us)
Async XLA Ops:
  51.8 56.3 %all-to-all-start = ((bf16[16,2,96,256]{3,2,1,0:T(8,128)(2,1)}), bf16[16,2,96,256]{3,2,1,0:T(8,128)(2,1)S(1)}, u32[]{:S(2)}, u32[]{:S(2)}) async-start(bf16[16,2,96,256]{3,2,1,0:T(8,128)(2,1)} %shard_map.103), calls=%async_computation | async-start | bytes 3145728 | tf_op jit(solution)/shard_map/all_to_all | solution.py:419
  108.0 6.1 %copy-start.6 = (s32[64]{0:T(128)S(1)}, s32[64]{0:T(128)}, u32[]{:S(2)}) copy-start(s32[64]{0:T(128)} %param.14) | copy-start | bytes 772
  108.1 6.7 %copy-start.5 = (s32[64]{0:T(128)S(1)}, s32[64]{0:T(128)}, u32[]{:S(2)}) copy-start(s32[64]{0:T(128)} %param.15) | copy-start | bytes 772
  108.1 7.3 %copy-start.1 = (s32[16,2]{0,1:T(2,128)S(1)}, s32[16,2]{0,1:T(2,128)}, u32[]{:S(2)}) copy-start(s32[16,2]{0,1:T(2,128)} %param.13) | copy-start | bytes 388
  108.1 9.2 %copy-start.4 = (f32[1536]{0:T(1024)S(1)}, f32[1536]{0:T(1024)}, u32[]{:S(2)}) copy-start(f32[1536]{0:T(1024)} %param.10) | copy-start | bytes 18436
  108.1 10.4 %copy-start.2 = (bf16[16,2,96,256]{3,2,1,0:T(8,128)(2,1)}, bf16[16,2,96,256]{3,2,1,0:T(8,128)(2,1)S(1)}, u32[]{:S(2)}) copy-start(bf16[16,2,96,256]{3,2,1,0:T(8,128)(2,1)S(1)} %all-to-all-done.wd_ref) | copy-start | bytes 4718596
  108.1 42.2 %all-to-all-start.1 = ((bf16[16,2,96,256]{3,2,1,0:T(8,128)(2,1)}), bf16[16,2,96,256]{3,2,1,0:T(8,128)(2,1)S(1)}, u32[]{:S(2)}, u32[]{:S(2)}) async-start(bf16[16,2,96,256]{3,2,1,0:T(8,128)(2,1)} %shard_map.104), calls=%async_computation.1 | async-start | bytes 3145728 | tf_op jit(solution)/shard_map/all_to_all | solution.py:420
  150.3 4.9 %copy-start.3 = (bf16[16,2,96,256]{3,2,1,0:T(8,128)(2,1)}, bf16[16,2,96,256]{3,2,1,0:T(8,128)(2,1)S(1)}, u32[]{:S(2)}) copy-start(bf16[16,2,96,256]{3,2,1,0:T(8,128)(2,1)S(1)} %all-to-all-done.1.wu_ref) | copy-start | bytes 4718596
  150.3 41.1 %all-to-all-start.2 = ((bf16[16,2,96,256]{3,2,1,0:T(8,128)(2,1)}), bf16[16,2,96,256]{3,2,1,0:T(8,128)(2,1)S(1)}, u32[]{:S(2)}, u32[]{:S(2)}) async-start(bf16[16,2,96,256]{3,2,1,0:T(8,128)(2,1)} %get-tuple-element.16), calls=%async_computation.2 | async-start | bytes 3145728 | tf_op jit(solution)/shard_map/all_to_all | solution.py:424
  167.9 28.4 %copy-start = (s32[32]{0:T(128)S(1)}, s32[32]{0:T(128)}, u32[]{:S(2)}) copy-start(s32[32]{0:T(128)} %reshape.152.lang_ref) | copy-start | bytes 388
  191.4 41.1 %all-to-all-start.3 = ((bf16[16,2,96,256]{3,2,1,0:T(8,128)(2,1)}), bf16[16,2,96,256]{3,2,1,0:T(8,128)(2,1)S(1)}, u32[]{:S(2)}, u32[]{:S(2)}) async-start(bf16[16,2,96,256]{3,2,1,0:T(8,128)(2,1)} %get-tuple-element.17), calls=%async_computation.3 | async-start | bytes 3145728 | tf_op jit(solution)/shard_map/all_to_all | solution.py:429

commit v13 on v12

--- a/solution.py
+++ b/solution.py
@@ -251,42 +251,48 @@
     return tuple(result) if with_zeros else result[0]
 
 
-def gather_kernel(lang_ref, weight_hbm, out_hbm, sems, *, slots):
-    members = lang_ref.shape[0]
-
-    def copy(m):
+def gather_kernel(lang_ref, weight_hbm, out_ref, sems, *, slots):
+    per_part = out_ref.shape[0] * slots
+    base = pl.program_id(0) * per_part
+
+    def copy(k):
         return pltpu.make_async_copy(
-            weight_hbm.at[lang_ref[m]], out_hbm.at[m // slots, m % slots], sems.at[m]
+            weight_hbm.at[lang_ref[base + k]], out_ref.at[k // slots, k % slots], sems.at[k]
         )
 
-    def start(m, carry):
-        copy(m).start()
+    def start(k, carry):
+        copy(k).start()
         return carry
 
-    def finish(m, carry):
-        copy(m).wait()
+    def finish(k, carry):
+        copy(k).wait()
         return carry
 
-    lax.fori_loop(0, members, start, 0)
-    lax.fori_loop(0, members, finish, 0)
+    lax.fori_loop(0, per_part, start, 0)
+    lax.fori_loop(0, per_part, finish, 0)
 
 
 def gather_rows(slot_lang, weight):
     devices, slots = slot_lang.shape
     _, row_count, bottleneck = weight.shape
-    members = devices * slots
+    parts = 4 if devices % 4 == 0 else 1
     grid_spec = pltpu.PrefetchScalarGridSpec(
         num_scalar_prefetch=1,
-        grid=(1,),
+        grid=(parts,),
         in_specs=[pl.BlockSpec(memory_space=pl.ANY)],
-        out_specs=pl.BlockSpec(memory_space=pl.ANY),
-        scratch_shapes=[pltpu.SemaphoreType.DMA((members,))],
-    )
-    size = members * row_count * bottleneck * 2
+        out_specs=pl.BlockSpec(
+            (devices // parts, slots, row_count, bottleneck), lambda p, ml: (p, 0, 0, 0)
+        ),
+        scratch_shapes=[pltpu.SemaphoreType.DMA((devices // parts * slots,))],
+    )
+    size = devices * slots * row_count * bottleneck * 2
     return pl.pallas_call(
         functools.partial(gather_kernel, slots=slots),
         grid_spec=grid_spec,
         out_shape=jax.ShapeDtypeStruct((devices, slots, row_count, bottleneck), weight.dtype),
+        compiler_params=pltpu.CompilerParams(
+            dimension_semantics=("arbitrary",), vmem_limit_bytes=48 * 1024 * 1024
+        ),
         cost_estimate=pl.CostEstimate(flops=0, bytes_accessed=2 * size, transcendentals=0),
     )(slot_lang.reshape(-1), weight)
 

time: 236 us -> 177 us (0.75)
  Pallas kernels: 131 us -> 43.1 us
  waiting for transfers between devices: 72.3 us -> 103 us
    pallas_call x2, Pallas kernels: 99.4 us -> 11.3 us  [gather_rows(): pl.pallas_call(functools.partial(gather_kernel, slots=slots), grid_spec=g...]
    all_to_all x1, waiting for transfers between devices: 0.01 us -> 30.5 us  [on_device(): got_down = exchange(gather_rows(slot_lang, down_weight))]
  transfers between devices with their start and end apart: 4 -> 4, of which waited for: 3 -> 4; matrix products, arithmetic and copies ran while one was open for 3% -> 4% of each run, Pallas kernels for 34% -> 20%
where the time goes in v13:
time: 177 us; the launch traced here: 176 us
  waiting for transfers between devices  103 us (58%)
  Pallas kernels  43.1 us (24%)
  starting transfers between devices  21.3 us (12%)
  local copies, waits for them, and re-layouts  5.2 us (3%)
  other arithmetic  2.5 us (1%)
    all_to_all x1, waiting for transfers between devices, on_device(): got_down = exchange(gather_rows(slot_lang, down_weight))  30.5 us
    all_to_all x1, waiting for transfers between devices, on_device(): exchange(send_down).reshape(devices * slots, row_count, bottleneck)  27 us
    all_to_all x1, waiting for transfers between devices, on_device(): back_up = exchange(send_up).reshape(devices * slots, row_count, bottleneck)  23.6 us
    all_to_all x1, waiting for transfers between devices, on_device(): got_up = exchange(gather_rows(slot_lang, up_weight))  22 us
    pallas_call x1, Pallas kernels, backward_pass(): pl.pallas_call(functools.partial(backward_kernel, direct=direct), grid_sp...  12.6 us
    pallas_call x2, Pallas kernels, gather_rows(): pl.pallas_call(functools.partial(gather_kernel, slots=slots), grid_spec=g...  11.3 us
    pallas_call x1, Pallas kernels, forward_pass(): pl.pallas_call(functools.partial(forward_kernel, direct=direct), grid_spe...  9.95 us
    pallas_call x1, Pallas kernels, combine(): pl.pallas_call(combine_kernel, grid_spec=grid_spec, out_shape=[out_shape]...  6.64 us
  transfers between devices with their start and end apart: 4, of which 4 were waited for; matrix products, arithmetic and copies ran while one was open for 4% of the time, Pallas kernels for 20%

profile of v13, /device:TPU:15, one launch (start us, length us, event | category | flops | bytes accessed | tf_op | source)
XLA Modules:
  0.0 175.9 jit_solution(14289953487657125092)
XLA Ops:
  0.6 0.8 copy.22
  1.5 5.7 %shard_map.103 = bf16[16,2,96,256]{3,2,1,0:T(8,128)(2,1)} custom-call(s32[32]{0:T(128)S(1)} %reshape.152.lang_ref, bf16[160,96,256]{2,1,0:T(8,128)(2,1)} %weight_hbm.2), custom_call_target="tpu_custom_call" | custom-call | bytes 3145728 | tf_op jit(solution)/shard_map/pallas_call | solution.py:289
  7.1 6.6 %all-to-all-start = ((bf16[16,2,96,256]{3,2,1,0:T(8,128)(2,1)}), bf16[16,2,96,256]{3,2,1,0:T(8,128)(2,1)S(1)}, u32[]{:S(2)}, u32[]{:S(2)}) async-start(bf16[16,2,96,256]{3,2,1,0:T(8,128)(2,1)} %shard_map.103), calls=%async_computation | async-start | bytes 3145728 | tf_op jit(solution)/shard_map/all_to_all | solution.py:425
  13.7 5.7 %shard_map.104 = bf16[16,2,96,256]{3,2,1,0:T(8,128)(2,1)} custom-call(s32[32]{0:T(128)S(1)} %reshape.152.lang_ref, bf16[160,96,256]{2,1,0:T(8,128)(2,1)} %weight_hbm.3), custom_call_target="tpu_custom_call" | custom-call | bytes 3145728 | tf_op jit(solution)/shard_map/pallas_call | solution.py:289
  19.4 30.5 %all-to-all-done.wd_ref = bf16[16,2,96,256]{3,2,1,0:T(8,128)(2,1)S(1)} async-done(((bf16[16,2,96,256]{3,2,1,0:T(8,128)(2,1)}), bf16[16,2,96,256]{3,2,1,0:T(8,128)(2,1)S(1)}, u32[]{:S(2)}, u32[]{:S(2)}) %all-to-all-start) | async-done | bytes 1572896 | tf_op jit(solution)/shard_map/all_to_all | solution.py:425
  49.9 4.9 %all-to-all-start.1 = ((bf16[16,2,96,256]{3,2,1,0:T(8,128)(2,1)}), bf16[16,2,96,256]{3,2,1,0:T(8,128)(2,1)}, u32[]{:S(2)}, u32[]{:S(2)}) async-start(bf16[16,2,96,256]{3,2,1,0:T(8,128)(2,1)} %shard_map.104), calls=%async_computation.1 | async-start | bytes 3145728 | tf_op jit(solution)/shard_map/all_to_all | solution.py:426
  54.8 0.6 dynamic_slice.10.slot_ref
  55.4 0.6 dynamic_slice.11.len_ref
  56.1 0.9 gather_fusion
  57.3 0.6 gather_fusion.1
  58.0 0.6 reshape.151.gain_ref
  58.6 0.6 and_select_fusion.scale_ref
  59.2 10.0 %shard_map.105 = (f32[4,256,256]{2,1,0:T(8,128)}, bf16[16,2,96,256]{3,2,1,0:T(8,128)(2,1)}) custom-call(s32[4]{0:T(128)} %dynamic_slice.10.slot_ref, s32[4]{0:T(128)} %dynamic_slice.11.len_ref, bf16[4,256,1536]{2,1,0:T(8,128)(2,1)} %frames_ref.3, bf16[4,256,1536]{2,1,0:T(8,128)(2,1)} %cot_ref.3, f32[1,1536]{1,0:T(1,128)} %reshape.151.gain_ref, ...), custom_call_target="tpu_custom_call" | custom-call | flops 1610612736 | bytes 9437184 | tf_op jit(solution)/shard_map/pallas_call | solution.py:348
  69.1 22.0 %all-to-all-done.1.wu_ref = bf16[16,2,96,256]{3,2,1,0:T(8,128)(2,1)} async-done(((bf16[16,2,96,256]{3,2,1,0:T(8,128)(2,1)}), bf16[16,2,96,256]{3,2,1,0:T(8,128)(2,1)}, u32[]{:S(2)}, u32[]{:S(2)}) %all-to-all-start.1) | async-done | bytes 1572896 | tf_op jit(solution)/shard_map/all_to_all | solution.py:426
  91.1 4.9 %all-to-all-start.2 = ((bf16[16,2,96,256]{3,2,1,0:T(8,128)(2,1)}), bf16[16,2,96,256]{3,2,1,0:T(8,128)(2,1)S(1)}, u32[]{:S(2)}, u32[]{:S(2)}) async-start(bf16[16,2,96,256]{3,2,1,0:T(8,128)(2,1)} %get-tuple-element.16), calls=%async_computation.2 | async-start | bytes 3145728 | tf_op jit(solution)/shard_map/all_to_all | solution.py:430
  96.0 12.6 %shard_map.106 = (bf16[4,256,1536]{2,1,0:T(8,128)(2,1)}, bf16[16,2,96,256]{3,2,1,0:T(8,128)(2,1)}) custom-call(s32[4]{0:T(128)} %dynamic_slice.10.slot_ref, s32[4]{0:T(128)} %dynamic_slice.11.len_ref, bf16[4,256,1536]{2,1,0:T(8,128)(2,1)} %frames_ref.3, bf16[4,256,1536]{2,1,0:T(8,128)(2,1)} %cot_ref.3, f32[1,1536]{1,0:T(1,128)} %reshape.151.gain_ref, ...), custom_call_target="tpu_custom_call" | custom-call | flops 2415919104 | bytes 15728640 | tf_op jit(solution)/shard_map/pallas_call | solution.py:389
  108.6 23.6 %all-to-all-done.2 = bf16[16,2,96,256]{3,2,1,0:T(8,128)(2,1)S(1)} async-done(((bf16[16,2,96,256]{3,2,1,0:T(8,128)(2,1)}), bf16[16,2,96,256]{3,2,1,0:T(8,128)(2,1)S(1)}, u32[]{:S(2)}, u32[]{:S(2)}) %all-to-all-start.2) | async-done | bytes 1572896 | tf_op jit(solution)/shard_map/all_to_all | solution.py:430
  132.2 4.9 %all-to-all-start.3 = ((bf16[16,2,96,256]{3,2,1,0:T(8,128)(2,1)}), bf16[16,2,96,256]{3,2,1,0:T(8,128)(2,1)S(1)}, u32[]{:S(2)}, u32[]{:S(2)}) async-start(bf16[16,2,96,256]{3,2,1,0:T(8,128)(2,1)} %get-tuple-element.17), calls=%async_computation.3 | async-start | bytes 3145728 | tf_op jit(solution)/shard_map/all_to_all | solution.py:435
  137.1 1.6 sort.17
  138.7 0.7 gather_fusion.2
  139.4 0.2 convert_reduce_fusion.start_ref
  139.6 6.6 %shard_map.107 = (bf16[160,96,256]{2,1,0:T(8,128)(2,1)}, bf16[160,96,256]{2,1,0:T(8,128)(2,1)}) custom-call(s32[32]{0:T(128)S(1)} %get-tuple-element.14.order_ref, s32[32]{0:T(128)S(1)} %gather_fusion.2, s32[6]{0:T(128)S(1)} %convert_reduce_fusion.start_ref, bf16[32,96,256]{2,1,0:T(8,128)(2,1)S(1)} %bitcast.14), custom_call_target="tpu_custom_call" | custom-call | flops 786432 | bytes 17301504 | tf_op jit(solution)/shard_map/pallas_call | solution.py:238
  146.2 27.0 %all-to-all-done.3 = bf16[16,2,96,256]{3,2,1,0:T(8,128)(2,1)S(1)} async-done(((bf16[16,2,96,256]{3,2,1,0:T(8,128)(2,1)}), bf16[16,2,96,256]{3,2,1,0:T(8,128)(2,1)S(1)}, u32[]{:S(2)}, u32[]{:S(2)}) %all-to-all-start.3) | async-done | bytes 1572896 | tf_op jit(solution)/shard_map/all_to_all | solution.py:435
  173.3 2.6 %shard_map.108 = bf16[160,96,256]{2,1,0:T(8,128)(2,1)} custom-call(s32[32]{0:T(128)S(1)} %get-tuple-element.14.order_ref, s32[32]{0:T(128)S(1)} %gather_fusion.2, bf16[32,96,256]{2,1,0:T(8,128)(2,1)S(1)} %bitcast.15, bf16[160,96,256]{2,1,0:T(8,128)(2,1)} %get-tuple-element.19.zeros_hbm), custom_call_target="tpu_custom_call", output_to_operand_aliasing={{}: (3, {})} | custom-call | flops 786432 | bytes 3145728 | tf_op jit(solution)/shard_map/pallas_call | solution.py:203
  (22 shorter events, 0.5 us)
Async XLA Ops:
  7.1 42.8 %all-to-all-start = ((bf16[16,2,96,256]{3,2,1,0:T(8,128)(2,1)}), bf16[16,2,96,256]{3,2,1,0:T(8,128)(2,1)S(1)}, u32[]{:S(2)}, u32[]{:S(2)}) async-start(bf16[16,2,96,256]{3,2,1,0:T(8,128)(2,1)} %shard_map.103), calls=%async_computation | async-start | bytes 3145728 | tf_op jit(solution)/shard_map/all_to_all | solution.py:425
  19.4 35.4 %copy-start.4 = (s32[64]{0:T(128)S(1)}, s32[64]{0:T(128)}, u32[]{:S(2)}) copy-start(s32[64]{0:T(128)} %param.14) | copy-start | bytes 772
  19.4 36.0 %copy-start.3 = (s32[64]{0:T(128)S(1)}, s32[64]{0:T(128)}, u32[]{:S(2)}) copy-start(s32[64]{0:T(128)} %param.15) | copy-start | bytes 772
  19.4 36.7 %copy-start = (s32[16,2]{0,1:T(2,128)S(1)}, s32[16,2]{0,1:T(2,128)}, u32[]{:S(2)}) copy-start(s32[16,2]{0,1:T(2,128)} %param.13) | copy-start | bytes 388
  19.4 38.6 %copy-start.2 = (f32[1536]{0:T(1024)S(1)}, f32[1536]{0:T(1024)}, u32[]{:S(2)}) copy-start(f32[1536]{0:T(1024)} %param.10) | copy-start | bytes 18436
  49.9 9.3 %copy-start.1 = (bf16[16,2,96,256]{3,2,1,0:T(8,128)(2,1)}, bf16[16,2,96,256]{3,2,1,0:T(8,128)(2,1)S(1)}, u32[]{:S(2)}) copy-start(bf16[16,2,96,256]{3,2,1,0:T(8,128)(2,1)S(1)} %all-to-all-done.wd_ref) | copy-start | bytes 4718596
  49.9 41.2 %all-to-all-start.1 = ((bf16[16,2,96,256]{3,2,1,0:T(8,128)(2,1)}), bf16[16,2,96,256]{3,2,1,0:T(8,128)(2,1)}, u32[]{:S(2)}, u32[]{:S(2)}) async-start(bf16[16,2,96,256]{3,2,1,0:T(8,128)(2,1)} %shard_map.104), calls=%async_computation.1 | async-start | bytes 3145728 | tf_op jit(solution)/shard_map/all_to_all | solution.py:426
  91.1 41.1 %all-to-all-start.2 = ((bf16[16,2,96,256]{3,2,1,0:T(8,128)(2,1)}), bf16[16,2,96,256]{3,2,1,0:T(8,128)(2,1)S(1)}, u32[]{:S(2)}, u32[]{:S(2)}) async-start(bf16[16,2,96,256]{3,2,1,0:T(8,128)(2,1)} %get-tuple-element.16), calls=%async_computation.2 | async-start | bytes 3145728 | tf_op jit(solution)/shard_map/all_to_all | solution.py:430
  132.2 41.1 %all-to-all-start.3 = ((bf16[16,2,96,256]{3,2,1,0:T(8,128)(2,1)}), bf16[16,2,96,256]{3,2,1,0:T(8,128)(2,1)S(1)}, u32[]{:S(2)}, u32[]{:S(2)}) async-start(bf16[16,2,96,256]{3,2,1,0:T(8,128)(2,1)} %get-tuple-element.17), calls=%async_computation.3 | async-start | bytes 3145728 | tf_op jit(solution)/shard_map/all_to_all | solution.py:435

commit v14 on v10

--- a/solution.py
+++ b/solution.py
@@ -141,7 +141,8 @@
     lax.fori_loop(first_at, end_at, add_member, 0)
 
 
-def scatter_kernel(order_ref, lang_ref, back_ref, zeros_hbm, out_hbm, acc_ref, stage_ref, sems):
+def scatter_kernel(order_ref, lang_ref, back_hbm, zeros_hbm, out_hbm, acc_ref, in_ref, stage_ref,
+                   sems_in, sems_out):
     del zeros_hbm
     members = lang_ref.shape[0]
     last_member = members - 1
@@ -149,12 +150,20 @@
     def run_end(i):
         return (i == last_member) | (lang_ref[jnp.minimum(i + 1, last_member)] != lang_ref[i])
 
-    def copy(i):
-        return pltpu.make_async_copy(stage_ref.at[i], out_hbm.at[lang_ref[i]], sems.at[i])
+    def copy_in(i):
+        return pltpu.make_async_copy(back_hbm.at[order_ref[i]], in_ref.at[i], sems_in.at[i])
+
+    def copy_out(i):
+        return pltpu.make_async_copy(stage_ref.at[i], out_hbm.at[lang_ref[i]], sems_out.at[i])
+
+    def fetch(i, carry):
+        copy_in(i).start()
+        return carry
 
     def add_member(i, carry):
+        copy_in(i).wait()
         first = (i == 0) | (lang_ref[jnp.maximum(i - 1, 0)] != lang_ref[i])
-        val = back_ref[order_ref[i]].astype(jnp.float32)
+        val = in_ref[i].astype(jnp.float32)
 
         @pl.when(first)
         def _():
@@ -167,17 +176,18 @@
         @pl.when(run_end(i))
         def _():
             stage_ref[i] = acc_ref[...].astype(stage_ref.dtype)
-            copy(i).start()
+            copy_out(i).start()
 
         return carry
 
     def finish(i, carry):
         @pl.when(run_end(i))
         def _():
-            copy(i).wait()
-
-        return carry
-
+            copy_out(i).wait()
+
+        return carry
+
+    lax.fori_loop(0, members, fetch, 0)
     lax.fori_loop(0, members, add_member, 0)
     lax.fori_loop(0, members, finish, 0)
 
@@ -189,14 +199,13 @@
     grid_spec = pltpu.PrefetchScalarGridSpec(
         num_scalar_prefetch=2,
         grid=(1,),
-        in_specs=[
-            pl.BlockSpec((members, row_count, bottleneck), lambda i, o, l: (0, 0, 0)),
-            pl.BlockSpec(memory_space=pl.ANY),
-        ],
+        in_specs=[pl.BlockSpec(memory_space=pl.ANY), pl.BlockSpec(memory_space=pl.ANY)],
         out_specs=pl.BlockSpec(memory_space=pl.ANY),
         scratch_shapes=[
             pltpu.VMEM((row_count, bottleneck), jnp.float32),
             pltpu.VMEM((members, row_count, bottleneck), jnp.bfloat16),
+            pltpu.VMEM((members, row_count, bottleneck), jnp.bfloat16),
+            pltpu.SemaphoreType.DMA((members,)),
             pltpu.SemaphoreType.DMA((members,)),
         ],
     )

time: 174 us -> 177 us (1.017)
  Pallas kernels: 39.1 us -> 41.6 us
    pallas_call x1, Pallas kernels: 2.59 us -> 5.24 us  [scatter_combine(): pl.pallas_call(scatter_kernel, grid_spec=grid_spec, out_shape=jax.ShapeDt...]
where the time goes in v14:
time: 177 us; the launch traced here: 176 us
  waiting for transfers between devices  105 us (59%)
  Pallas kernels  41.6 us (24%)
  starting transfers between devices  21.3 us (12%)
  local copies, waits for them, and re-layouts  5.2 us (3%)
  other arithmetic  2.5 us (1%)
    all_to_all x1, waiting for transfers between devices, on_device(): got_down = exchange(gather_rows(slot_lang, down_weight))  32.6 us
    all_to_all x1, waiting for transfers between devices, on_device(): exchange(send_down).reshape(devices * slots, row_count, bottleneck)  27.1 us
    all_to_all x1, waiting for transfers between devices, on_device(): back_up = exchange(send_up).reshape(devices * slots, row_count, bottleneck)  23.5 us
    all_to_all x1, waiting for transfers between devices, on_device(): got_up = exchange(gather_rows(slot_lang, up_weight))  21.8 us
    pallas_call x1, Pallas kernels, backward_pass(): pl.pallas_call(functools.partial(backward_kernel, direct=direct), grid_sp...  12.7 us
    pallas_call x1, Pallas kernels, forward_pass(): pl.pallas_call(functools.partial(forward_kernel, direct=direct), grid_spe...  10.2 us
    pallas_call x2, Pallas kernels, gather_rows(): pl.pallas_call(functools.partial(gather_kernel, slots=slots), grid_spec=g...  6.89 us
    pallas_call x1, Pallas kernels, combine(): pl.pallas_call(combine_kernel, grid_spec=grid_spec, out_shape=[out_shape]...  6.58 us
  transfers between devices with their start and end apart: 4, of which 4 were waited for; matrix products, arithmetic and copies ran while one was open for 4% of the time, Pallas kernels for 19%

profile of v14, /device:TPU:15, one launch (start us, length us, event | category | flops | bytes accessed | tf_op | source)
XLA Modules:
  0.0 176.3 jit_solution(6224219555461718094)
XLA Ops:
  0.6 0.8 copy.22
  1.5 3.4 %shard_map.103 = bf16[16,2,96,256]{3,2,1,0:T(8,128)(2,1)} custom-call(s32[32]{0:T(128)S(1)} %reshape.152.lang_ref, bf16[160,96,256]{2,1,0:T(8,128)(2,1)} %weight_hbm.2), custom_call_target="tpu_custom_call" | custom-call | bytes 3145728 | tf_op jit(solution)/shard_map/pallas_call | solution.py:295
  4.9 6.6 %all-to-all-start = ((bf16[16,2,96,256]{3,2,1,0:T(8,128)(2,1)}), bf16[16,2,96,256]{3,2,1,0:T(8,128)(2,1)S(1)}, u32[]{:S(2)}, u32[]{:S(2)}) async-start(bf16[16,2,96,256]{3,2,1,0:T(8,128)(2,1)} %shard_map.103), calls=%async_computation | async-start | bytes 3145728 | tf_op jit(solution)/shard_map/all_to_all | solution.py:429
  11.5 3.5 %shard_map.104 = bf16[16,2,96,256]{3,2,1,0:T(8,128)(2,1)} custom-call(s32[32]{0:T(128)S(1)} %reshape.152.lang_ref, bf16[160,96,256]{2,1,0:T(8,128)(2,1)} %weight_hbm.3), custom_call_target="tpu_custom_call" | custom-call | bytes 3145728 | tf_op jit(solution)/shard_map/pallas_call | solution.py:295
  15.0 32.6 %all-to-all-done.wd_ref = bf16[16,2,96,256]{3,2,1,0:T(8,128)(2,1)S(1)} async-done(((bf16[16,2,96,256]{3,2,1,0:T(8,128)(2,1)}), bf16[16,2,96,256]{3,2,1,0:T(8,128)(2,1)S(1)}, u32[]{:S(2)}, u32[]{:S(2)}) %all-to-all-start) | async-done | bytes 1572896 | tf_op jit(solution)/shard_map/all_to_all | solution.py:429
  47.6 4.9 %all-to-all-start.1 = ((bf16[16,2,96,256]{3,2,1,0:T(8,128)(2,1)}), bf16[16,2,96,256]{3,2,1,0:T(8,128)(2,1)}, u32[]{:S(2)}, u32[]{:S(2)}) async-start(bf16[16,2,96,256]{3,2,1,0:T(8,128)(2,1)} %shard_map.104), calls=%async_computation.1 | async-start | bytes 3145728 | tf_op jit(solution)/shard_map/all_to_all | solution.py:430
  52.6 0.6 dynamic_slice.10.slot_ref
  53.1 0.6 dynamic_slice.11.len_ref
  53.8 0.9 gather_fusion
  55.0 0.6 gather_fusion.1
  55.8 0.6 reshape.151.gain_ref
  56.4 0.6 and_select_fusion.scale_ref
  56.9 10.2 %shard_map.105 = (f32[4,256,256]{2,1,0:T(8,128)}, bf16[16,2,96,256]{3,2,1,0:T(8,128)(2,1)}) custom-call(s32[4]{0:T(128)} %dynamic_slice.10.slot_ref, s32[4]{0:T(128)} %dynamic_slice.11.len_ref, bf16[4,256,1536]{2,1,0:T(8,128)(2,1)} %frames_ref.3, bf16[4,256,1536]{2,1,0:T(8,128)(2,1)} %cot_ref.3, f32[1,1536]{1,0:T(1,128)} %reshape.151.gain_ref, ...), custom_call_target="tpu_custom_call" | custom-call | flops 1610612736 | bytes 9437184 | tf_op jit(solution)/shard_map/pallas_call | solution.py:352
  67.1 21.8 %all-to-all-done.1.wu_ref = bf16[16,2,96,256]{3,2,1,0:T(8,128)(2,1)} async-done(((bf16[16,2,96,256]{3,2,1,0:T(8,128)(2,1)}), bf16[16,2,96,256]{3,2,1,0:T(8,128)(2,1)}, u32[]{:S(2)}, u32[]{:S(2)}) %all-to-all-start.1) | async-done | bytes 1572896 | tf_op jit(solution)/shard_map/all_to_all | solution.py:430
  88.8 4.9 %all-to-all-start.2 = ((bf16[16,2,96,256]{3,2,1,0:T(8,128)(2,1)}), bf16[16,2,96,256]{3,2,1,0:T(8,128)(2,1)S(1)}, u32[]{:S(2)}, u32[]{:S(2)}) async-start(bf16[16,2,96,256]{3,2,1,0:T(8,128)(2,1)} %get-tuple-element.16), calls=%async_computation.2 | async-start | bytes 3145728 | tf_op jit(solution)/shard_map/all_to_all | solution.py:434
  93.8 12.7 %shard_map.106 = (bf16[4,256,1536]{2,1,0:T(8,128)(2,1)}, bf16[16,2,96,256]{3,2,1,0:T(8,128)(2,1)}) custom-call(s32[4]{0:T(128)} %dynamic_slice.10.slot_ref, s32[4]{0:T(128)} %dynamic_slice.11.len_ref, bf16[4,256,1536]{2,1,0:T(8,128)(2,1)} %frames_ref.3, bf16[4,256,1536]{2,1,0:T(8,128)(2,1)} %cot_ref.3, f32[1,1536]{1,0:T(1,128)} %reshape.151.gain_ref, ...), custom_call_target="tpu_custom_call" | custom-call | flops 2415919104 | bytes 15728640 | tf_op jit(solution)/shard_map/pallas_call | solution.py:393
  106.5 23.5 %all-to-all-done.2 = bf16[16,2,96,256]{3,2,1,0:T(8,128)(2,1)S(1)} async-done(((bf16[16,2,96,256]{3,2,1,0:T(8,128)(2,1)}), bf16[16,2,96,256]{3,2,1,0:T(8,128)(2,1)S(1)}, u32[]{:S(2)}, u32[]{:S(2)}) %all-to-all-start.2) | async-done | bytes 1572896 | tf_op jit(solution)/shard_map/all_to_all | solution.py:434
  129.9 4.9 %all-to-all-start.3 = ((bf16[16,2,96,256]{3,2,1,0:T(8,128)(2,1)}), bf16[16,2,96,256]{3,2,1,0:T(8,128)(2,1)S(1)}, u32[]{:S(2)}, u32[]{:S(2)}) async-start(bf16[16,2,96,256]{3,2,1,0:T(8,128)(2,1)} %get-tuple-element.17), calls=%async_computation.3 | async-start | bytes 3145728 | tf_op jit(solution)/shard_map/all_to_all | solution.py:439
  134.8 1.6 sort.17
  136.5 0.7 gather_fusion.2
  137.2 0.2 convert_reduce_fusion.start_ref
  137.4 6.6 %shard_map.107 = (bf16[160,96,256]{2,1,0:T(8,128)(2,1)}, bf16[160,96,256]{2,1,0:T(8,128)(2,1)}) custom-call(s32[32]{0:T(128)S(1)} %get-tuple-element.14.order_ref, s32[32]{0:T(128)S(1)} %gather_fusion.2, s32[6]{0:T(128)S(1)} %convert_reduce_fusion.start_ref, bf16[32,96,256]{2,1,0:T(8,128)(2,1)S(1)} %bitcast.14), custom_call_target="tpu_custom_call" | custom-call | flops 786432 | bytes 17301504 | tf_op jit(solution)/shard_map/pallas_call | solution.py:247
  143.9 27.1 %all-to-all-done.3 = bf16[16,2,96,256]{3,2,1,0:T(8,128)(2,1)S(1)} async-done(((bf16[16,2,96,256]{3,2,1,0:T(8,128)(2,1)}), bf16[16,2,96,256]{3,2,1,0:T(8,128)(2,1)S(1)}, u32[]{:S(2)}, u32[]{:S(2)}) %all-to-all-start.3) | async-done | bytes 1572896 | tf_op jit(solution)/shard_map/all_to_all | solution.py:439
  171.0 5.2 %shard_map.108 = bf16[160,96,256]{2,1,0:T(8,128)(2,1)} custom-call(s32[32]{0:T(128)S(1)} %get-tuple-element.14.order_ref, s32[32]{0:T(128)S(1)} %gather_fusion.2, bf16[32,96,256]{2,1,0:T(8,128)(2,1)S(1)} %bitcast.15, bf16[160,96,256]{2,1,0:T(8,128)(2,1)} %get-tuple-element.19.zeros_hbm), custom_call_target="tpu_custom_call", output_to_operand_aliasing={{}: (3, {})} | custom-call | flops 786432 | bytes 3145728 | tf_op jit(solution)/shard_map/pallas_call | solution.py:212
  (22 shorter events, 0.5 us)
Async XLA Ops:
  4.9 42.8 %all-to-all-start = ((bf16[16,2,96,256]{3,2,1,0:T(8,128)(2,1)}), bf16[16,2,96,256]{3,2,1,0:T(8,128)(2,1)S(1)}, u32[]{:S(2)}, u32[]{:S(2)}) async-start(bf16[16,2,96,256]{3,2,1,0:T(8,128)(2,1)} %shard_map.103), calls=%async_computation | async-start | bytes 3145728 | tf_op jit(solution)/shard_map/all_to_all | solution.py:429
  14.9 37.6 %copy-start.4 = (s32[64]{0:T(128)S(1)}, s32[64]{0:T(128)}, u32[]{:S(2)}) copy-start(s32[64]{0:T(128)} %param.14) | copy-start | bytes 772
  15.0 38.2 %copy-start.3 = (s32[64]{0:T(128)S(1)}, s32[64]{0:T(128)}, u32[]{:S(2)}) copy-start(s32[64]{0:T(128)} %param.15) | copy-start | bytes 772
  15.0 38.8 %copy-start = (s32[16,2]{0,1:T(2,128)S(1)}, s32[16,2]{0,1:T(2,128)}, u32[]{:S(2)}) copy-start(s32[16,2]{0,1:T(2,128)} %param.13) | copy-start | bytes 388
  15.0 40.8 %copy-start.2 = (f32[1536]{0:T(1024)S(1)}, f32[1536]{0:T(1024)}, u32[]{:S(2)}) copy-start(f32[1536]{0:T(1024)} %param.10) | copy-start | bytes 18436
  47.6 9.3 %copy-start.1 = (bf16[16,2,96,256]{3,2,1,0:T(8,128)(2,1)}, bf16[16,2,96,256]{3,2,1,0:T(8,128)(2,1)S(1)}, u32[]{:S(2)}) copy-start(bf16[16,2,96,256]{3,2,1,0:T(8,128)(2,1)S(1)} %all-to-all-done.wd_ref) | copy-start | bytes 4718596
  47.6 41.2 %all-to-all-start.1 = ((bf16[16,2,96,256]{3,2,1,0:T(8,128)(2,1)}), bf16[16,2,96,256]{3,2,1,0:T(8,128)(2,1)}, u32[]{:S(2)}, u32[]{:S(2)}) async-start(bf16[16,2,96,256]{3,2,1,0:T(8,128)(2,1)} %shard_map.104), calls=%async_computation.1 | async-start | bytes 3145728 | tf_op jit(solution)/shard_map/all_to_all | solution.py:430
  88.8 41.1 %all-to-all-start.2 = ((bf16[16,2,96,256]{3,2,1,0:T(8,128)(2,1)}), bf16[16,2,96,256]{3,2,1,0:T(8,128)(2,1)S(1)}, u32[]{:S(2)}, u32[]{:S(2)}) async-start(bf16[16,2,96,256]{3,2,1,0:T(8,128)(2,1)} %get-tuple-element.16), calls=%async_computation.2 | async-start | bytes 3145728 | tf_op jit(solution)/shard_map/all_to_all | solution.py:434
  129.9 41.1 %all-to-all-start.3 = ((bf16[16,2,96,256]{3,2,1,0:T(8,128)(2,1)}), bf16[16,2,96,256]{3,2,1,0:T(8,128)(2,1)S(1)}, u32[]{:S(2)}, u32[]{:S(2)}) async-start(bf16[16,2,96,256]{3,2,1,0:T(8,128)(2,1)} %get-tuple-element.17), calls=%async_computation.3 | async-start | bytes 3145728 | tf_op jit(solution)/shard_map/all_to_all | solution.py:439

commit v15 on v10

--- a/solution.py
+++ b/solution.py
@@ -416,7 +416,11 @@
     scaling = lax.rsqrt(jnp.maximum(counts, 1).astype(jnp.float32))
     member_langs = slot_lang.reshape(-1)
     own_scale = jnp.take(scaling, lax.dynamic_index_in_dim(slot_lang, self_index, 0, False))
-    exchange = functools.partial(lax.all_to_all, axis_name="dp", split_axis=0, concat_axis=0, tiled=True)
+    def exchange(x):
+        flat = x.reshape(x.shape[0], x.shape[1] * x.shape[2], x.shape[3])
+        moved = lax.all_to_all(flat, "dp", split_axis=0, concat_axis=0, tiled=True)
+        return moved.reshape(x.shape)
+
     got_down = exchange(gather_rows(slot_lang, down_weight))
     got_up = exchange(gather_rows(slot_lang, up_weight))
     pre_act, send_up = forward_pass(

time: 174 us -> 174 us (level)
  no operation moved by 1% of the time
where the time goes in v15:
time: 174 us
  waiting for transfers between devices  105 us (60%)
  Pallas kernels  38.9 us (22%)
  starting transfers between devices  21.3 us (12%)
  local copies, waits for them, and re-layouts  5.2 us (3%)
  other arithmetic  2.5 us (1%)
    all_to_all x4, waiting for transfers between devices, exchange(): moved = lax.all_to_all(flat, 'dp', split_axis=0, concat_axis=0, tiled=True)  105 us
    all_to_all x4, starting transfers between devices, exchange(): moved = lax.all_to_all(flat, 'dp', split_axis=0, concat_axis=0, tiled=True)  21.3 us
    pallas_call x1, Pallas kernels, backward_pass(): pl.pallas_call(functools.partial(backward_kernel, direct=direct), grid_sp...  12.6 us
    pallas_call x1, Pallas kernels, forward_pass(): pl.pallas_call(functools.partial(forward_kernel, direct=direct), grid_spe...  9.95 us
    pallas_call x2, Pallas kernels, gather_rows(): pl.pallas_call(functools.partial(gather_kernel, slots=slots), grid_spec=g...  6.98 us
    pallas_call x1, Pallas kernels, combine(): pl.pallas_call(combine_kernel, grid_spec=grid_spec, out_shape=[out_shape]...  6.72 us
  transfers between devices with their start and end apart: 4, of which 4 were waited for; matrix products, arithmetic and copies ran while one was open for 4% of the time, Pallas kernels for 19%

profile of v15, /device:TPU:15, one launch (start us, length us, event | category | flops | bytes accessed | tf_op | source)
XLA Modules:
  0.0 173.7 jit_solution(16771319258959412806)
XLA Ops:
  0.6 0.8 copy.22
  1.5 3.4 %shard_map.103 = bf16[16,2,96,256]{3,2,1,0:T(8,128)(2,1)} custom-call(s32[32]{0:T(128)S(1)} %reshape.164.lang_ref, bf16[160,96,256]{2,1,0:T(8,128)(2,1)} %weight_hbm.2), custom_call_target="tpu_custom_call" | custom-call | bytes 3145728 | tf_op jit(solution)/shard_map/pallas_call | solution.py:286
  4.9 6.6 %all-to-all-start = ((bf16[16,192,256]{2,1,0:T(8,128)(2,1)}), bf16[16,192,256]{2,1,0:T(8,128)(2,1)S(1)}, u32[]{:S(2)}, u32[]{:S(2)}) async-start(bf16[16,192,256]{2,1,0:T(8,128)(2,1)} %bitcast), calls=%async_computation | async-start | bytes 3145728 | tf_op jit(solution)/shard_map/all_to_all | solution.py:421
  11.5 3.5 %shard_map.104 = bf16[16,2,96,256]{3,2,1,0:T(8,128)(2,1)} custom-call(s32[32]{0:T(128)S(1)} %reshape.164.lang_ref, bf16[160,96,256]{2,1,0:T(8,128)(2,1)} %weight_hbm.3), custom_call_target="tpu_custom_call" | custom-call | bytes 3145728 | tf_op jit(solution)/shard_map/pallas_call | solution.py:286
  15.1 32.6 %all-to-all-done = bf16[16,192,256]{2,1,0:T(8,128)(2,1)S(1)} async-done(((bf16[16,192,256]{2,1,0:T(8,128)(2,1)}), bf16[16,192,256]{2,1,0:T(8,128)(2,1)S(1)}, u32[]{:S(2)}, u32[]{:S(2)}) %all-to-all-start) | async-done | bytes 1572896 | tf_op jit(solution)/shard_map/all_to_all | solution.py:421
  47.7 4.9 %all-to-all-start.1 = ((bf16[16,192,256]{2,1,0:T(8,128)(2,1)}), bf16[16,192,256]{2,1,0:T(8,128)(2,1)}, u32[]{:S(2)}, u32[]{:S(2)}) async-start(bf16[16,192,256]{2,1,0:T(8,128)(2,1)} %bitcast.2), calls=%async_computation.1 | async-start | bytes 3145728 | tf_op jit(solution)/shard_map/all_to_all | solution.py:421
  52.6 0.6 dynamic_slice.10.slot_ref
  53.2 0.6 dynamic_slice.11.len_ref
  53.8 0.9 gather_fusion
  55.0 0.6 gather_fusion.1
  55.8 0.6 reshape.163.gain_ref
  56.4 0.6 and_select_fusion.scale_ref
  57.0 10.0 %shard_map.105 = (f32[4,256,256]{2,1,0:T(8,128)}, bf16[16,2,96,256]{3,2,1,0:T(8,128)(2,1)}) custom-call(s32[4]{0:T(128)} %dynamic_slice.10.slot_ref, s32[4]{0:T(128)} %dynamic_slice.11.len_ref, bf16[4,256,1536]{2,1,0:T(8,128)(2,1)} %frames_ref.3, bf16[4,256,1536]{2,1,0:T(8,128)(2,1)} %cot_ref.3, f32[1,1536]{1,0:T(1,128)} %reshape.163.gain_ref, ...), custom_call_target="tpu_custom_call" | custom-call | flops 1610612736 | bytes 9437184 | tf_op jit(solution)/shard_map/pallas_call | solution.py:343
  66.9 22.0 %all-to-all-done.1 = bf16[16,192,256]{2,1,0:T(8,128)(2,1)} async-done(((bf16[16,192,256]{2,1,0:T(8,128)(2,1)}), bf16[16,192,256]{2,1,0:T(8,128)(2,1)}, u32[]{:S(2)}, u32[]{:S(2)}) %all-to-all-start.1) | async-done | bytes 1572896 | tf_op jit(solution)/shard_map/all_to_all | solution.py:421
  88.9 4.9 %all-to-all-start.2 = ((bf16[16,192,256]{2,1,0:T(8,128)(2,1)}), bf16[16,192,256]{2,1,0:T(8,128)(2,1)S(1)}, u32[]{:S(2)}, u32[]{:S(2)}) async-start(bf16[16,192,256]{2,1,0:T(8,128)(2,1)} %bitcast.25), calls=%async_computation.2 | async-start | bytes 3145728 | tf_op jit(solution)/shard_map/all_to_all | solution.py:421
  93.8 12.6 %shard_map.106 = (bf16[4,256,1536]{2,1,0:T(8,128)(2,1)}, bf16[16,2,96,256]{3,2,1,0:T(8,128)(2,1)}) custom-call(s32[4]{0:T(128)} %dynamic_slice.10.slot_ref, s32[4]{0:T(128)} %dynamic_slice.11.len_ref, bf16[4,256,1536]{2,1,0:T(8,128)(2,1)} %frames_ref.3, bf16[4,256,1536]{2,1,0:T(8,128)(2,1)} %cot_ref.3, f32[1,1536]{1,0:T(1,128)} %reshape.163.gain_ref, ...), custom_call_target="tpu_custom_call" | custom-call | flops 2415919104 | bytes 15728640 | tf_op jit(solution)/shard_map/pallas_call | solution.py:384
  106.4 23.6 %all-to-all-done.2 = bf16[16,192,256]{2,1,0:T(8,128)(2,1)S(1)} async-done(((bf16[16,192,256]{2,1,0:T(8,128)(2,1)}), bf16[16,192,256]{2,1,0:T(8,128)(2,1)S(1)}, u32[]{:S(2)}, u32[]{:S(2)}) %all-to-all-start.2) | async-done | bytes 1572896 | tf_op jit(solution)/shard_map/all_to_all | solution.py:421
  130.0 4.9 %all-to-all-start.3 = ((bf16[16,192,256]{2,1,0:T(8,128)(2,1)}), bf16[16,192,256]{2,1,0:T(8,128)(2,1)S(1)}, u32[]{:S(2)}, u32[]{:S(2)}) async-start(bf16[16,192,256]{2,1,0:T(8,128)(2,1)} %bitcast.24), calls=%async_computation.3 | async-start | bytes 3145728 | tf_op jit(solution)/shard_map/all_to_all | solution.py:421
  134.9 1.6 sort.17
  136.5 0.7 gather_fusion.2
  137.2 0.2 convert_reduce_fusion.start_ref
  137.4 6.7 %shard_map.107 = (bf16[160,96,256]{2,1,0:T(8,128)(2,1)}, bf16[160,96,256]{2,1,0:T(8,128)(2,1)}) custom-call(s32[32]{0:T(128)S(1)} %get-tuple-element.14.order_ref, s32[32]{0:T(128)S(1)} %gather_fusion.2, s32[6]{0:T(128)S(1)} %convert_reduce_fusion.start_ref, bf16[32,96,256]{2,1,0:T(8,128)(2,1)S(1)} %bitcast.20), custom_call_target="tpu_custom_call" | custom-call | flops 786432 | bytes 17301504 | tf_op jit(solution)/shard_map/pallas_call | solution.py:238
  144.1 27.0 %all-to-all-done.3 = bf16[16,192,256]{2,1,0:T(8,128)(2,1)S(1)} async-done(((bf16[16,192,256]{2,1,0:T(8,128)(2,1)}), bf16[16,192,256]{2,1,0:T(8,128)(2,1)S(1)}, u32[]{:S(2)}, u32[]{:S(2)}) %all-to-all-start.3) | async-done | bytes 1572896 | tf_op jit(solution)/shard_map/all_to_all | solution.py:421
  171.1 2.6 %shard_map.108 = bf16[160,96,256]{2,1,0:T(8,128)(2,1)} custom-call(s32[32]{0:T(128)S(1)} %get-tuple-element.14.order_ref, s32[32]{0:T(128)S(1)} %gather_fusion.2, bf16[32,96,256]{2,1,0:T(8,128)(2,1)S(1)} %bitcast.21, bf16[160,96,256]{2,1,0:T(8,128)(2,1)} %get-tuple-element.19.zeros_hbm), custom_call_target="tpu_custom_call", output_to_operand_aliasing={{}: (3, {})} | custom-call | flops 786432 | bytes 3145728 | tf_op jit(solution)/shard_map/pallas_call | solution.py:203
  (22 shorter events, 0.5 us)
Async XLA Ops:
  4.9 42.8 %all-to-all-start = ((bf16[16,192,256]{2,1,0:T(8,128)(2,1)}), bf16[16,192,256]{2,1,0:T(8,128)(2,1)S(1)}, u32[]{:S(2)}, u32[]{:S(2)}) async-start(bf16[16,192,256]{2,1,0:T(8,128)(2,1)} %bitcast), calls=%async_computation | async-start | bytes 3145728 | tf_op jit(solution)/shard_map/all_to_all | solution.py:421
  15.0 37.5 %copy-start.4 = (s32[64]{0:T(128)S(1)}, s32[64]{0:T(128)}, u32[]{:S(2)}) copy-start(s32[64]{0:T(128)} %param.14) | copy-start | bytes 772
  15.1 38.1 %copy-start.3 = (s32[64]{0:T(128)S(1)}, s32[64]{0:T(128)}, u32[]{:S(2)}) copy-start(s32[64]{0:T(128)} %param.15) | copy-start | bytes 772
  15.1 38.8 %copy-start = (s32[16,2]{0,1:T(2,128)S(1)}, s32[16,2]{0,1:T(2,128)}, u32[]{:S(2)}) copy-start(s32[16,2]{0,1:T(2,128)} %param.13) | copy-start | bytes 388
  15.1 40.7 %copy-start.2 = (f32[1536]{0:T(1024)S(1)}, f32[1536]{0:T(1024)}, u32[]{:S(2)}) copy-start(f32[1536]{0:T(1024)} %param.10) | copy-start | bytes 18436
  47.7 9.3 %copy-start.1 = (bf16[16,192,256]{2,1,0:T(8,128)(2,1)}, bf16[16,192,256]{2,1,0:T(8,128)(2,1)S(1)}, u32[]{:S(2)}) copy-start(bf16[16,192,256]{2,1,0:T(8,128)(2,1)S(1)} %all-to-all-done) | copy-start | bytes 4718596
  47.7 41.2 %all-to-all-start.1 = ((bf16[16,192,256]{2,1,0:T(8,128)(2,1)}), bf16[16,192,256]{2,1,0:T(8,128)(2,1)}, u32[]{:S(2)}, u32[]{:S(2)}) async-start(bf16[16,192,256]{2,1,0:T(8,128)(2,1)} %bitcast.2), calls=%async_computation.1 | async-start | bytes 3145728 | tf_op jit(solution)/shard_map/all_to_all | solution.py:421
  88.9 41.1 %all-to-all-start.2 = ((bf16[16,192,256]{2,1,0:T(8,128)(2,1)}), bf16[16,192,256]{2,1,0:T(8,128)(2,1)S(1)}, u32[]{:S(2)}, u32[]{:S(2)}) async-start(bf16[16,192,256]{2,1,0:T(8,128)(2,1)} %bitcast.25), calls=%async_computation.2 | async-start | bytes 3145728 | tf_op jit(solution)/shard_map/all_to_all | solution.py:421
  130.0 41.1 %all-to-all-start.3 = ((bf16[16,192,256]{2,1,0:T(8,128)(2,1)}), bf16[16,192,256]{2,1,0:T(8,128)(2,1)S(1)}, u32[]{:S(2)}, u32[]{:S(2)}) async-start(bf16[16,192,256]{2,1,0:T(8,128)(2,1)} %bitcast.24), calls=%async_computation.3 | async-start | bytes 3145728 | tf_op jit(solution)/shard_map/all_to_all | solution.py:421

commit v16 on v10

--- a/solution.py
+++ b/solution.py
@@ -417,8 +417,13 @@
     member_langs = slot_lang.reshape(-1)
     own_scale = jnp.take(scaling, lax.dynamic_index_in_dim(slot_lang, self_index, 0, False))
     exchange = functools.partial(lax.all_to_all, axis_name="dp", split_axis=0, concat_axis=0, tiled=True)
-    got_down = exchange(gather_rows(slot_lang, down_weight))
-    got_up = exchange(gather_rows(slot_lang, up_weight))
+    got = exchange(
+        jnp.concatenate(
+            [gather_rows(slot_lang, down_weight), gather_rows(slot_lang, up_weight)], axis=1
+        )
+    )
+    got_down = got[:, :slots]
+    got_up = got[:, slots:]
     pre_act, send_up = forward_pass(
         frames, cotangent, gain, got_down, own_slot, own_lengths, own_scale
     )

time: 174 us -> 182 us (1.046)
  waiting for transfers between devices: 105 us -> 116 us
  starting transfers between devices: 21.3 us -> 16.7 us
  Pallas kernels: 39.1 us -> 36.5 us
  other arithmetic: 2.5 us -> 4.42 us
  local copies, waits for them, and re-layouts: 5.2 us -> 7.09 us
    all_to_all x2 -> x1, waiting for transfers between devices: 54.6 us -> 65.5 us  [on_device(): exchange(jnp.concatenate([gather_rows(slot_lang, down_weight), gather_row...]
    all_to_all x2 -> x1, starting transfers between devices: 11.5 us -> 6.7 us  [on_device(): exchange(jnp.concatenate([gather_rows(slot_lang, down_weight), gather_row...]
    pallas_call x2, Pallas kernels: 7.07 us -> 4.71 us  [gather_rows(): pl.pallas_call(functools.partial(gather_kernel, slots=slots), grid_spec=g...]
    concatenate x0 -> x1, other arithmetic: none -> 1.94 us  [on_device(): jnp.concatenate([gather_rows(slot_lang, down_weight), gather_rows(slot_la...]
    slice x0 -> x1, local copies, waits for them, and re-layouts: none -> 1.89 us  [on_device(): got_up = got[:, slots:]]
  transfers between devices with their start and end apart: 4 -> 3, of which waited for: 4 -> 3; matrix products, arithmetic and copies ran while one was open for 4% -> 4% of each run, Pallas kernels for 19% -> 11%
where the time goes in v16:
time: 182 us
  waiting for transfers between devices  116 us (64%)
  Pallas kernels  36.5 us (20%)
  starting transfers between devices  16.7 us (9%)
  local copies, waits for them, and re-layouts  7.09 us (4%)
  other arithmetic  4.42 us (2%)
    all_to_all x1, waiting for transfers between devices, on_device(): exchange(jnp.concatenate([gather_rows(slot_lang, down_weight), gather_row...  65.5 us
    all_to_all x1, waiting for transfers between devices, on_device(): exchange(send_down).reshape(devices * slots, row_count, bottleneck)  27 us
    all_to_all x1, waiting for transfers between devices, on_device(): back_up = exchange(send_up).reshape(devices * slots, row_count, bottleneck)  23.6 us
    pallas_call x1, Pallas kernels, backward_pass(): pl.pallas_call(functools.partial(backward_kernel, direct=direct), grid_sp...  12.6 us
    pallas_call x1, Pallas kernels, forward_pass(): pl.pallas_call(functools.partial(forward_kernel, direct=direct), grid_spe...  9.95 us
    all_to_all x1, starting transfers between devices, on_device(): exchange(jnp.concatenate([gather_rows(slot_lang, down_weight), gather_row...  6.7 us
    pallas_call x1, Pallas kernels, combine(): pl.pallas_call(combine_kernel, grid_spec=grid_spec, out_shape=[out_shape]...  6.66 us
    all_to_all x1, starting transfers between devices, on_device(): back_up = exchange(send_up).reshape(devices * slots, row_count, bottleneck)  5.07 us
  transfers between devices with their start and end apart: 3, of which 3 were waited for; matrix products, arithmetic and copies ran while one was open for 4% of the time, Pallas kernels for 11%

profile of v16, /device:TPU:15, one launch (start us, length us, event | category | flops | bytes accessed | tf_op | source)
XLA Modules:
  0.0 181.5 jit_solution(13818719078006393728)
XLA Ops:
  0.6 0.8 copy.22
  1.5 2.3 %shard_map.104 = bf16[16,2,96,256]{3,2,1,0:T(8,128)(2,1)S(1)} custom-call(s32[32]{0:T(128)S(1)} %reshape.152.lang_ref, bf16[160,96,256]{2,1,0:T(8,128)(2,1)} %weight_hbm.3), custom_call_target="tpu_custom_call" | custom-call | bytes 3145728 | tf_op jit(solution)/shard_map/pallas_call | solution.py:286
  3.8 2.4 %shard_map.103 = bf16[16,2,96,256]{3,2,1,0:T(8,128)(2,1)S(1)} custom-call(s32[32]{0:T(128)S(1)} %reshape.152.lang_ref, bf16[160,96,256]{2,1,0:T(8,128)(2,1)} %weight_hbm.2), custom_call_target="tpu_custom_call" | custom-call | bytes 3145728 | tf_op jit(solution)/shard_map/pallas_call | solution.py:286
  6.2 1.9 %pad_maximum_fusion = bf16[16,4,96,256]{3,2,1,0:T(8,128)(2,1)} fusion(bf16[16,2,96,256]{3,2,1,0:T(8,128)(2,1)S(1)} %shard_map.104, bf16[16,2,96,256]{3,2,1,0:T(8,128)(2,1)S(1)} %shard_map.103), kind=kLoop, calls=%fused_computation.3 | loop fusion | flops 1572864 | bytes 6291456 | tf_op jit(solution)/shard_map/concatenate | solution.py:421
  8.2 6.7 %all-to-all-start = ((bf16[16,4,96,256]{3,2,1,0:T(8,128)(2,1)}), bf16[16,4,96,256]{3,2,1,0:T(8,128)(2,1)S(1)}, u32[]{:S(2)}, u32[]{:S(2)}) async-start(bf16[16,4,96,256]{3,2,1,0:T(8,128)(2,1)} %pad_maximum_fusion), calls=%async_computation | async-start | bytes 6291456 | tf_op jit(solution)/shard_map/all_to_all | solution.py:420
  14.9 0.7 dynamic_slice.10.slot_ref
  15.5 0.6 dynamic_slice.11.len_ref
  16.1 0.9 gather_fusion
  17.3 0.6 gather_fusion.1
  18.1 0.6 reshape.151.gain_ref
  18.7 0.5 and_select_fusion.scale_ref
  19.2 65.5 %all-to-all-done = bf16[16,4,96,256]{3,2,1,0:T(8,128)(2,1)S(1)} async-done(((bf16[16,4,96,256]{3,2,1,0:T(8,128)(2,1)}), bf16[16,4,96,256]{3,2,1,0:T(8,128)(2,1)S(1)}, u32[]{:S(2)}, u32[]{:S(2)}) %all-to-all-start) | async-done | bytes 3145760 | tf_op jit(solution)/shard_map/all_to_all | solution.py:420
  84.7 1.9 %fusion.9 = (bf16[16,2,96,256]{3,2,1,0:T(8,128)(2,1)}, bf16[16,2,96,256]{3,2,1,0:T(8,128)(2,1)}) fusion(bf16[16,4,96,256]{3,2,1,0:T(8,128)(2,1)S(1)} %all-to-all-done), kind=kLoop, calls=%fused_computation.31 | loop fusion | bytes 6291456 | tf_op jit(solution)/shard_map/slice | solution.py:426
  86.6 10.0 %shard_map.105 = (f32[4,256,256]{2,1,0:T(8,128)}, bf16[16,2,96,256]{3,2,1,0:T(8,128)(2,1)}) custom-call(s32[4]{0:T(128)} %dynamic_slice.10.slot_ref, s32[4]{0:T(128)} %dynamic_slice.11.len_ref, bf16[4,256,1536]{2,1,0:T(8,128)(2,1)} %frames_ref.3, bf16[4,256,1536]{2,1,0:T(8,128)(2,1)} %cot_ref.3, f32[1,1536]{1,0:T(1,128)} %reshape.151.gain_ref, ...), custom_call_target="tpu_custom_call" | custom-call | flops 1610612736 | bytes 9437184 | tf_op jit(solution)/shard_map/pallas_call | solution.py:343
  96.6 5.1 %all-to-all-start.1 = ((bf16[16,2,96,256]{3,2,1,0:T(8,128)(2,1)}), bf16[16,2,96,256]{3,2,1,0:T(8,128)(2,1)S(1)}, u32[]{:S(2)}, u32[]{:S(2)}) async-start(bf16[16,2,96,256]{3,2,1,0:T(8,128)(2,1)} %get-tuple-element.16), calls=%async_computation.1 | async-start | bytes 3145728 | tf_op jit(solution)/shard_map/all_to_all | solution.py:430
  101.7 12.6 %shard_map.106 = (bf16[4,256,1536]{2,1,0:T(8,128)(2,1)}, bf16[16,2,96,256]{3,2,1,0:T(8,128)(2,1)}) custom-call(s32[4]{0:T(128)} %dynamic_slice.10.slot_ref, s32[4]{0:T(128)} %dynamic_slice.11.len_ref, bf16[4,256,1536]{2,1,0:T(8,128)(2,1)} %frames_ref.3, bf16[4,256,1536]{2,1,0:T(8,128)(2,1)} %cot_ref.3, f32[1,1536]{1,0:T(1,128)} %reshape.151.gain_ref, ...), custom_call_target="tpu_custom_call" | custom-call | flops 2415919104 | bytes 15728640 | tf_op jit(solution)/shard_map/pallas_call | solution.py:384
  114.3 23.6 %all-to-all-done.1 = bf16[16,2,96,256]{3,2,1,0:T(8,128)(2,1)S(1)} async-done(((bf16[16,2,96,256]{3,2,1,0:T(8,128)(2,1)}), bf16[16,2,96,256]{3,2,1,0:T(8,128)(2,1)S(1)}, u32[]{:S(2)}, u32[]{:S(2)}) %all-to-all-start.1) | async-done | bytes 1572896 | tf_op jit(solution)/shard_map/all_to_all | solution.py:430
  137.8 4.9 %all-to-all-start.2 = ((bf16[16,2,96,256]{3,2,1,0:T(8,128)(2,1)}), bf16[16,2,96,256]{3,2,1,0:T(8,128)(2,1)S(1)}, u32[]{:S(2)}, u32[]{:S(2)}) async-start(bf16[16,2,96,256]{3,2,1,0:T(8,128)(2,1)} %get-tuple-element.17), calls=%async_computation.2 | async-start | bytes 3145728 | tf_op jit(solution)/shard_map/all_to_all | solution.py:435
  142.8 1.6 sort.17
  144.4 0.7 gather_fusion.2
  145.1 0.2 convert_reduce_fusion.start_ref
  145.3 6.7 %shard_map.107 = (bf16[160,96,256]{2,1,0:T(8,128)(2,1)}, bf16[160,96,256]{2,1,0:T(8,128)(2,1)}) custom-call(s32[32]{0:T(128)S(1)} %get-tuple-element.14.order_ref, s32[32]{0:T(128)S(1)} %gather_fusion.2, s32[6]{0:T(128)S(1)} %convert_reduce_fusion.start_ref, bf16[32,96,256]{2,1,0:T(8,128)(2,1)S(1)} %bitcast.14), custom_call_target="tpu_custom_call" | custom-call | flops 786432 | bytes 17301504 | tf_op jit(solution)/shard_map/pallas_call | solution.py:238
  151.9 27.0 %all-to-all-done.2 = bf16[16,2,96,256]{3,2,1,0:T(8,128)(2,1)S(1)} async-done(((bf16[16,2,96,256]{3,2,1,0:T(8,128)(2,1)}), bf16[16,2,96,256]{3,2,1,0:T(8,128)(2,1)S(1)}, u32[]{:S(2)}, u32[]{:S(2)}) %all-to-all-start.2) | async-done | bytes 1572896 | tf_op jit(solution)/shard_map/all_to_all | solution.py:435
  178.9 2.6 %shard_map.108 = bf16[160,96,256]{2,1,0:T(8,128)(2,1)} custom-call(s32[32]{0:T(128)S(1)} %get-tuple-element.14.order_ref, s32[32]{0:T(128)S(1)} %gather_fusion.2, bf16[32,96,256]{2,1,0:T(8,128)(2,1)S(1)} %bitcast.15, bf16[160,96,256]{2,1,0:T(8,128)(2,1)} %get-tuple-element.19.zeros_hbm), custom_call_target="tpu_custom_call", output_to_operand_aliasing={{}: (3, {})} | custom-call | flops 786432 | bytes 3145728 | tf_op jit(solution)/shard_map/pallas_call | solution.py:203
  (20 shorter events, 0.5 us)
Async XLA Ops:
  8.1 6.7 %copy-start.3 = (s32[64]{0:T(128)S(1)}, s32[64]{0:T(128)}, u32[]{:S(2)}) copy-start(s32[64]{0:T(128)} %param.14) | copy-start | bytes 772
  8.1 7.4 %copy-start.2 = (s32[64]{0:T(128)S(1)}, s32[64]{0:T(128)}, u32[]{:S(2)}) copy-start(s32[64]{0:T(128)} %param.15) | copy-start | bytes 772
  8.1 8.0 %copy-start = (s32[16,2]{0,1:T(2,128)S(1)}, s32[16,2]{0,1:T(2,128)}, u32[]{:S(2)}) copy-start(s32[16,2]{0,1:T(2,128)} %param.13) | copy-start | bytes 388
  8.1 9.9 %copy-start.1 = (f32[1536]{0:T(1024)S(1)}, f32[1536]{0:T(1024)}, u32[]{:S(2)}) copy-start(f32[1536]{0:T(1024)} %param.10) | copy-start | bytes 18436
  8.2 76.6 %all-to-all-start = ((bf16[16,4,96,256]{3,2,1,0:T(8,128)(2,1)}), bf16[16,4,96,256]{3,2,1,0:T(8,128)(2,1)S(1)}, u32[]{:S(2)}, u32[]{:S(2)}) async-start(bf16[16,4,96,256]{3,2,1,0:T(8,128)(2,1)} %pad_maximum_fusion), calls=%async_computation | async-start | bytes 6291456 | tf_op jit(solution)/shard_map/all_to_all | solution.py:420
  96.6 41.3 %all-to-all-start.1 = ((bf16[16,2,96,256]{3,2,1,0:T(8,128)(2,1)}), bf16[16,2,96,256]{3,2,1,0:T(8,128)(2,1)S(1)}, u32[]{:S(2)}, u32[]{:S(2)}) async-start(bf16[16,2,96,256]{3,2,1,0:T(8,128)(2,1)} %get-tuple-element.16), calls=%async_computation.1 | async-start | bytes 3145728 | tf_op jit(solution)/shard_map/all_to_all | solution.py:430
  137.8 41.1 %all-to-all-start.2 = ((bf16[16,2,96,256]{3,2,1,0:T(8,128)(2,1)}), bf16[16,2,96,256]{3,2,1,0:T(8,128)(2,1)S(1)}, u32[]{:S(2)}, u32[]{:S(2)}) async-start(bf16[16,2,96,256]{3,2,1,0:T(8,128)(2,1)} %get-tuple-element.17), calls=%async_computation.2 | async-start | bytes 3145728 | tf_op jit(solution)/shard_map/all_to_all | solution.py:435
